TPU v7x, 512 devices: a whole 4x8x8 slice. The times are simulated.
512 devices in a mesh: member: 16 (over x_lo, y), dp: 32 (over z, x_hi, core).
Axes of the slice: x: 4 (x_hi: 2, x_lo: 2; x = x_hi * 2 + x_lo), y: 8, z: 8, core: 2. Of those that a mesh axis runs over, the one named last changes fastest.
Arguments:
- inputs: bfloat16 [8192, 64], P('dp'), may hold values from -6 to 6
- observed: float32 [64, 8192], P('member', 'dp'), may hold values from -6 to 6
- noise: bfloat16 [2, 32, 64, 8192], P(None, None, 'member', 'dp'), may hold values from -4 to 4
- w_in: float32 [32, 64, 4096], P('member', None, 'dp'), may hold values from -0.75 to 0.75
- b_in: float32 [32, 4096], P('member', 'dp'), may hold values from -3 to 3
- w_out: float32 [32, 64, 4096], P('member', None, 'dp'), may hold values from -0.09375 to 0.09375
- b_out: float32 [32, 64], P('member'), may hold values from -3 to 3
Outputs:
- new_w_in: float32 [32, 64, 4096], P('member', None, 'dp')
- new_b_in: float32 [32, 4096], P('member', 'dp')
- new_w_out: float32 [32, 64, 4096], P('member', None, 'dp')
- new_b_out: float32 [32, 64], P('member')
All inputs are finite; a program needn't handle non-finite values.
Results may differ from a plain program's by a relative error of at most 0.00056.
Values may be sent and summed in bfloat16 or wider, within the bound.
No kernel may reach another device: no remote copies, remote signals or barrier semaphores. Data moves between devices by JAX's collectives and lax.ppermute only.
A program may use at most 64 MiB of HBM per device.

v0:
```python
import jax
import jax.numpy as jnp
from jax import lax
from jax.sharding import PartitionSpec as P

UPDATES = 2


ridge_level = 0.5


def solve_gain(gram, cross):
    eye = jnp.eye(gram.shape[0], dtype=gram.dtype)
    factor = jnp.linalg.cholesky(gram + ridge_level * eye)
    middle = lax.linalg.triangular_solve(factor, cross, left_side=True, lower=True)
    return lax.linalg.triangular_solve(factor, middle, left_side=True, lower=True, transpose_a=True)


def predict(inputs, w_in, b_in, w_out, b_out):
    shards = (
        w_in.astype(jnp.bfloat16),
        w_out.astype(jnp.bfloat16),
        b_in.astype(jnp.bfloat16)[:, None, :],
    )

    def single(item):
        weight_in, weight_out, bias_in = item
        pre = jnp.dot(inputs, weight_in, preferred_element_type=jnp.float32) + bias_in.astype(
            jnp.float32
        )
        hidden = jnp.tanh(pre).astype(jnp.bfloat16)
        return lax.dot_general(
            weight_out, hidden, (((1,), (1,)), ((), ())), preferred_element_type=jnp.float32
        )

    total = lax.map(
        single,
        (
            lax.all_gather(shards[0], "dp", axis=2, tiled=True),
            lax.all_gather(shards[1], "dp", axis=2, tiled=True),
            lax.all_gather(shards[2], "dp", axis=2, tiled=True),
        ),
    )
    return total + b_out[:, :, None]


def mix_own(own, whole, columns):
    flat = whole.reshape(whole.shape[0], -1)
    moved = lax.dot_general(
        columns, flat, (((0,), (0,)), ((), ())), precision=lax.Precision.HIGHEST
    )
    return own + moved.reshape(own.shape)


def on_device(inputs, observed, noise, w_in, b_in, w_out, b_out):
    per_device = w_in.shape[0]
    count = observed.shape[0] * lax.axis_size("member") * observed.shape[1] * lax.axis_size("dp")
    for update in range(UPDATES):
        predicted = predict(inputs, w_in, b_in, w_out, b_out)
        collected = lax.all_to_all(
            predicted.astype(jnp.bfloat16), "member", split_axis=1, concat_axis=0, tiled=True
        ).astype(predicted.dtype)
        mean_pred = jnp.mean(collected, axis=0)
        anomaly = (collected - mean_pred[None]).reshape(collected.shape[0], -1)
        misfit = (observed[None] + noise[update].astype(jnp.float32) - collected).reshape(
            collected.shape[0], -1
        )
        gram_part = lax.dot_general(
            anomaly, anomaly, (((1,), (1,)), ((), ())), precision=lax.Precision.HIGHEST
        )
        cross_part = lax.dot_general(
            anomaly, misfit, (((1,), (1,)), ((), ())), precision=lax.Precision.HIGHEST
        )
        gram, cross = lax.psum((gram_part, cross_part), ("member", "dp"))
        gain = solve_gain(gram / count, cross / count)
        whole_in, whole_bias, whole_out, whole_bout = (
            lax.all_gather(w_in, "member", axis=0, tiled=True),
            lax.all_gather(b_in, "member", axis=0, tiled=True),
            lax.all_gather(w_out, "member", axis=0, tiled=True),
            lax.all_gather(b_out, "member", axis=0, tiled=True),
        )
        first = lax.axis_index("member") * per_device
        columns = lax.dynamic_slice_in_dim(gain, first, per_device, 1)
        w_in = mix_own(w_in, whole_in, columns)
        b_in = mix_own(b_in, whole_bias, columns)
        w_out = mix_own(w_out, whole_out, columns)
        b_out = mix_own(b_out, whole_bout, columns)
    return (w_in, b_in, w_out, b_out)


def solution(mesh):
    placed = (
        P("dp", None),
        P("member", "dp"),
        P(None, None, "member", "dp"),
        P("member", None, "dp"),
        P("member", "dp"),
        P("member", None, "dp"),
        P("member", None),
    )
    return jax.shard_map(
        on_device,
        mesh=mesh,
        in_specs=placed,
        out_specs=(
            P("member", None, "dp"),
            P("member", "dp"),
            P("member", None, "dp"),
            P("member", None),
        ),
        check_vma=False,
    )
```

profile of v0, /device:TPU:1, one launch (start us, length us, event | category | flops | bytes accessed | tf_op | source)
XLA Modules:
  0.0 656.1 jit_solution(13720734547421046891)
XLA Ops:
  7.2 1.5 convert_element_type.118
  8.7 1.5 convert_element_type.119
  10.3 0.7 all-gather.21.cloned.1.call-update
  11.0 0.7 convert_element_type.120
  11.7 48.9 %all-gather = bf16[2,4096]{1,0:T(2,128)(2,1)S(1)} all-gather(bf16[2,128]{1,0:T(2,128)(2,1)S(1)} %convert_element_type.120), channel_id=2, replica_groups=mesh['member'=16,'dp'=32] {'dp'}, dimensions={1}, use_global_device_ids=true | all-gather | bytes 16896 | tf_op jit(solution)/shard_map/all_gather | solution.py:41
  60.6 35.2 %all-gather.15.cloned.1.call-done = bf16[2,64,4096]{2,1,0:T(8,128)(2,1)} async-done(((bf16[2,64,128]{2,1,0:T(8,128)(2,1)}), bf16[2,64,4096]{2,1,0:T(8,128)(2,1)}) %all-gather.15.cloned.1.call-update) | async-done | bytes 1048592 | tf_op jit(solution)/shard_map/all_gather | solution.py:40
  95.8 79.4 %all-gather.17.cloned.1.call-done = bf16[2,64,4096]{2,1,0:T(8,128)(2,1)} async-done(((bf16[2,64,128]{2,1,0:T(8,128)(2,1)}), bf16[2,64,4096]{2,1,0:T(8,128)(2,1)}) %all-gather.17.cloned.1.call-update) | async-done | bytes 1048592 | tf_op jit(solution)/shard_map/all_gather | solution.py:39
  175.2 5.3 while.20
  175.3 2.6 fusion.92
  177.9 2.6 fusion.92
  180.6 0.7 copy.79
  181.3 6.6 %all-to-all-start = ((bf16[2,64,256]{2,0,1:T(2,128)(2,1)}), bf16[2,64,256]{2,0,1:T(2,128)(2,1)S(1)}, u32[]{:S(2)}, u32[]{:S(2)}) async-start(bf16[2,64,256]{2,0,1:T(2,128)(2,1)} %copy.79), calls=%async_computation | async-start | bytes 131072 | tf_op jit(solution)/shard_map/all_to_all | solution.py:60
  188.0 0.5 all-gather.19.cloned.1.call-update
  188.5 6.8 %all-to-all-done = bf16[2,64,256]{2,0,1:T(2,128)(2,1)S(1)} async-done(((bf16[2,64,256]{2,0,1:T(2,128)(2,1)}), bf16[2,64,256]{2,0,1:T(2,128)(2,1)S(1)}, u32[]{:S(2)}, u32[]{:S(2)}) %all-to-all-start) | async-done | bytes 65568 | tf_op jit(solution)/shard_map/all_to_all | solution.py:60
  196.3 98.6 %all-reduce.1 = (f32[32,32]{0,1:T(8,128)S(1)}, f32[32,32]{0,1:T(8,128)S(1)}) all-reduce(f32[32,32]{0,1:T(8,128)S(1)} %convolution_bitcast_fusion.3, f32[32,32]{0,1:T(8,128)S(1)} %convolution_bitcast_fusion.2), channel_id=1, replica_groups=mesh['member'=16,'dp'=32] {'member','dp'}, use_global_device_ids=true, to_apply=%region_3.4 | all-reduce | flops 2048 | bytes 16384 | tf_op jit(solution)/shard_map/psum | solution.py:74
  294.9 2.9 cholesky.44
  297.9 0.6 compare_reduce_fusion.1
  298.5 0.7 fusion.42
  299.2 2.4 custom-call.11
  302.1 3.0 fusion.64
  305.2 2.2 all-gather.19.cloned.1.call-done
  307.4 3.0 fusion.65
  310.4 24.5 %all-gather.3 = f32[16,2,64]{2,1,0:T(2,128)S(1)} all-gather(f32[1,2,64]{2,1,0:T(2,128)S(1)} %bitcast.235), channel_id=1, replica_groups=mesh['member'=16,'dp'=32] {'member'}, dimensions={0}, use_global_device_ids=true | all-gather | bytes 8704 | tf_op jit(solution)/shard_map/all_gather | solution.py:80
  334.9 22.7 %all-gather.2 = f32[16,2,128]{2,1,0:T(2,128)S(1)} all-gather(f32[1,2,128]{2,1,0:T(2,128)S(1)} %bitcast.237), channel_id=1, replica_groups=mesh['member'=16,'dp'=32] {'member'}, dimensions={0}, use_global_device_ids=true | all-gather | bytes 17408 | tf_op jit(solution)/shard_map/all_gather | solution.py:78
  357.6 0.6 copy.102
  358.5 67.2 %all-gather.1 = bf16[2,4096]{1,0:T(2,128)(2,1)S(1)} all-gather(bf16[2,128]{1,0:T(2,128)(2,1)S(1)} %get-tuple-element.163), channel_id=3, replica_groups=mesh['member'=16,'dp'=32] {'dp'}, dimensions={1}, use_global_device_ids=true | all-gather | bytes 16896 | tf_op jit(solution)/shard_map/all_gather | solution.py:41
  425.8 1.8 copy.90
  427.7 32.0 %all-gather.25.cloned.1.call-done = bf16[2,64,4096]{2,0,1:T(2,128)(2,1)} async-done(((bf16[2,64,128]{2,0,1:T(2,128)(2,1)}), bf16[2,64,4096]{2,0,1:T(2,128)(2,1)}) %all-gather.25.cloned.1.call-update) | async-done | bytes 1048592 | tf_op jit(solution)/shard_map/all_gather | solution.py:39
  459.6 1.8 copy.91
  461.5 2.9 while.21
  461.5 1.4 fusion.96
  462.9 1.4 fusion.96
  464.4 0.7 copy.93
  465.1 7.3 %all-to-all-start.1 = ((bf16[2,64,256]{2,0,1:T(2,128)(2,1)}), bf16[2,64,256]{2,0,1:T(2,128)(2,1)S(1)}, u32[]{:S(2)}, u32[]{:S(2)}) async-start(bf16[2,64,256]{2,0,1:T(2,128)(2,1)} %copy.93), calls=%async_computation.1 | async-start | bytes 131072 | tf_op jit(solution)/shard_map/all_to_all | solution.py:60
  472.5 0.6 copy.100
  473.2 27.3 %all-gather.5 = f32[16,2,64]{2,1,0:T(2,128)S(1)} all-gather(f32[1,2,64]{2,1,0:T(2,128)S(1)} %bitcast.234), channel_id=1, replica_groups=mesh['member'=16,'dp'=32] {'member'}, dimensions={0}, use_global_device_ids=true | all-gather | bytes 8704 | tf_op jit(solution)/shard_map/all_gather | solution.py:80
  500.4 23.3 %all-gather.4 = f32[16,2,128]{2,1,0:T(2,128)S(1)} all-gather(f32[1,2,128]{2,1,0:T(2,128)S(1)} %bitcast.236), channel_id=1, replica_groups=mesh['member'=16,'dp'=32] {'member'}, dimensions={0}, use_global_device_ids=true | all-gather | bytes 17408 | tf_op jit(solution)/shard_map/all_gather | solution.py:78
  524.7 109.9 %all-reduce = (f32[32,32]{0,1:T(8,128)S(1)}, f32[32,32]{0,1:T(8,128)S(1)}) all-reduce(f32[32,32]{0,1:T(8,128)S(1)} %convolution_bitcast_fusion.1, f32[32,32]{0,1:T(8,128)S(1)} %convolution_bitcast_fusion), channel_id=1, replica_groups=mesh['member'=16,'dp'=32] {'member','dp'}, use_global_device_ids=true, to_apply=%region_10.14 | all-reduce | flops 2048 | bytes 16384 | tf_op jit(solution)/shard_map/psum | solution.py:74
  634.7 2.9 cholesky.55
  637.6 0.6 compare_reduce_fusion
  638.3 0.7 fusion.43
  638.9 2.4 custom-call.13
  641.9 2.4 convolution_add_fusion.2
  644.2 0.6 copy.105
  644.9 0.7 convolution_add_fusion.6
  645.6 0.7 convolution_add_fusion.7
  646.3 2.4 convolution_add_fusion.3
  648.7 0.6 copy.104
  (75 shorter events, 4.0 us)
Async XLA Ops:
  7.2 88.7 %all-gather.15.cloned.1.call-start = ((), (), s32[]{:S(2)}) async-start(), calls=%async_computation.2 | async-start | bytes 1081344 | tf_op jit(solution)/shard_map/all_gather | solution.py:40
  8.7 166.5 %all-gather.17.cloned.1.call-start = ((), (), s32[]{:S(2)}) async-start(), calls=%async_computation.3 | async-start | bytes 1081344 | tf_op jit(solution)/shard_map/all_gather | solution.py:39
  10.2 291.9 %all-gather.21.cloned.1.call-start = ((), (), s32[]{:S(2)}) async-start(), calls=%async_computation.5 | async-start | bytes 1114112 | tf_op jit(solution)/shard_map/all_gather | solution.py:79
  175.2 5.3 copy-start.4
  180.5 15.4 %copy-start.2 = (bf16[2,32,4,256]{3,2,1,0:T(4,128)(2,1)S(1)}, bf16[2,32,4,256]{3,2,1,0:T(4,128)(2,1)}, u32[]{:S(2)}) copy-start(bf16[2,32,4,256]{3,2,1,0:T(4,128)(2,1)} %param.18) | copy-start | bytes 393220
  180.5 15.4 %copy-start.3 = (f32[4,256]{1,0:T(4,128)S(1)}, f32[4,256]{1,0:T(4,128)}, u32[]{:S(2)}) copy-start(f32[4,256]{1,0:T(4,128)} %param.17) | copy-start | bytes 12292
  181.3 14.0 %all-to-all-start = ((bf16[2,64,256]{2,0,1:T(2,128)(2,1)}), bf16[2,64,256]{2,0,1:T(2,128)(2,1)S(1)}, u32[]{:S(2)}, u32[]{:S(2)}) async-start(bf16[2,64,256]{2,0,1:T(2,128)(2,1)} %copy.79), calls=%async_computation | async-start | bytes 131072 | tf_op jit(solution)/shard_map/all_to_all | solution.py:60
  187.9 119.4 %all-gather.19.cloned.1.call-start = ((), (), s32[]{:S(2)}) async-start(), calls=%async_computation.4 | async-start | bytes 1114112 | tf_op jit(solution)/shard_map/all_gather | solution.py:77
  188.5 237.3 %all-gather.23.cloned.1.call-start = ((), (), s32[]{:S(2)}) async-start(), calls=%async_computation.6 | async-start | bytes 1081344 | tf_op jit(solution)/shard_map/all_gather | solution.py:40
  195.4 106.7 %copy-start = (f32[2,64,128]{2,1,0:T(8,128)S(1)}, f32[2,64,128]{2,1,0:T(8,128)}, u32[]{:S(2)}) copy-start(f32[2,64,128]{2,1,0:T(8,128)} %param.21) | copy-start | bytes 196612
  196.0 111.4 %copy-start.1 = (f32[2,64,128]{2,1,0:T(8,128)S(1)}, f32[2,64,128]{2,1,0:T(8,128)}, u32[]{:S(2)}) copy-start(f32[2,64,128]{2,1,0:T(8,128)} %param.19) | copy-start | bytes 196612
  302.1 32.8 %copy-start.5 = (f32[2,128]{1,0:T(2,128)S(1)}, f32[2,128]{1,0:T(2,128)}, u32[]{:S(2)}) copy-start(f32[2,128]{1,0:T(2,128)} %param.20) | copy-start | bytes 3076
  305.1 154.5 %all-gather.25.cloned.1.call-start = ((), (), s32[]{:S(2)}) async-start(), calls=%async_computation.7 | async-start | bytes 1081344 | tf_op jit(solution)/shard_map/all_gather | solution.py:39
  310.4 331.5 %all-gather.29.cloned.1.call-start = ((), (), s32[]{:S(2)}) async-start(), calls=%async_computation.9 | async-start | bytes 1114112 | tf_op jit(solution)/shard_map/all_gather | solution.py:79
  427.6 33.8 %copy-start.6 = (bf16[256,64]{0,1:T(8,128)(2,1)S(1)}, bf16[256,64]{0,1:T(8,128)(2,1)}, u32[]{:S(2)}) copy-start(bf16[256,64]{0,1:T(8,128)(2,1)} %get-tuple-element.315) | copy-start | bytes 98308
  465.1 58.6 %all-to-all-start.1 = ((bf16[2,64,256]{2,0,1:T(2,128)(2,1)}), bf16[2,64,256]{2,0,1:T(2,128)(2,1)S(1)}, u32[]{:S(2)}, u32[]{:S(2)}) async-start(bf16[2,64,256]{2,0,1:T(2,128)(2,1)} %copy.93), calls=%async_computation.1 | async-start | bytes 131072 | tf_op jit(solution)/shard_map/all_to_all | solution.py:60
  472.4 173.9 %all-gather.27.cloned.1.call-start = ((), (), s32[]{:S(2)}) async-start(), calls=%async_computation.8 | async-start | bytes 1114112 | tf_op jit(solution)/shard_map/all_gather | solution.py:77
Sparse Core Ops, SparseCore 0:
  11.7 84.0 all-gather.14
  99.5 75.6 all-gather.16
  177.3 58.8 all-gather.20
  238.1 69.2 all-gather.18
  310.9 76.3 all-gather.22
  390.8 68.7 all-gather.24
  461.7 62.1 all-gather.28
  526.5 68.6 all-gather.26
where the time goes:
time: 657 us; the launch traced here: 656 us
  blocking collectives  422 us (64%)
  waiting for transfers between devices  157 us (24%)
  matrix products  22.2 us (3%)
  other arithmetic  17.7 us (3%)
  between operations  14.5 us (2%)
  starting transfers between devices  14.2 us (2%)
  local copies, waits for them, and re-layouts  8.08 us (1%)
    psum x2, blocking collectives, on_device(): gram, cross = lax.psum((gram_part, cross_part), ('member', 'dp'))  208 us
    all_gather x2, blocking collectives, predict(): lax.all_gather(shards[2], 'dp', axis=2, tiled=True)  116 us
    all_gather x2, waiting for transfers between devices, predict(): lax.all_gather(shards[0], 'dp', axis=2, tiled=True)  111 us
    all_gather x2, blocking collectives, on_device(): lax.all_gather(b_out, 'member', axis=0, tiled=True)  51.8 us
    all_gather x2, blocking collectives, on_device(): lax.all_gather(b_in, 'member', axis=0, tiled=True)  46 us
    all_gather x2, waiting for transfers between devices, predict(): lax.all_gather(shards[1], 'dp', axis=2, tiled=True)  35.2 us
    all_to_all x2, starting transfers between devices, on_device(): lax.all_to_all(predicted.astype(jnp.bfloat16), 'member', split_axis=1, co...  13.8 us
  transfers between devices with their start and end apart: 10, of which 5 were waited for; matrix products, arithmetic and copies ran while one was open for 7% of the time, Pallas kernels for 0%

commit v1 on v0

v1 whole, which is shorter than its diff:
```python
import jax
import jax.numpy as jnp
from jax import lax
from jax.sharding import PartitionSpec as P

UPDATES = 2


ridge_level = 0.5


def solve_gain(gram, cross):
    eye = jnp.eye(gram.shape[0], dtype=gram.dtype)
    factor = jnp.linalg.cholesky(gram + ridge_level * eye)
    middle = lax.linalg.triangular_solve(factor, cross, left_side=True, lower=True)
    return lax.linalg.triangular_solve(factor, middle, left_side=True, lower=True, transpose_a=True)


def pack(w_in, b_in, w_out, b_out):
    n = w_in.shape[0]
    return jnp.concatenate(
        [w_in.reshape(n, -1), w_out.reshape(n, -1), b_in.reshape(n, -1), b_out.reshape(n, -1)], axis=1
    )


def unpack(flat, f_in, hid, outs):
    n = flat.shape[0]
    a = f_in * hid
    b = a + outs * hid
    c = b + hid
    return (
        flat[:, :a].reshape(n, f_in, hid),
        flat[:, b:c].reshape(n, hid),
        flat[:, a:b].reshape(n, outs, hid),
        flat[:, c:].reshape(n, outs),
    )


def predict(inputs, own_flat, b_out, f_in, hid, outs):
    n = own_flat.shape[0]
    a = f_in * hid
    b = a + outs * hid
    rounded = own_flat[:, : b + hid].astype(jnp.bfloat16)
    gathered = lax.all_gather(rounded, "dp", axis=0, tiled=False)
    d = gathered.shape[0]
    w_in = gathered[:, :, :a].reshape(d, n, f_in, hid)
    w_out = gathered[:, :, a:b].reshape(d, n, outs, hid)
    b_in = gathered[:, :, b : b + hid]
    pre = jnp.einsum("sf,dnfh->nsdh", inputs, w_in, preferred_element_type=jnp.float32)
    pre = pre + jnp.transpose(b_in, (1, 0, 2)).astype(jnp.float32)[:, None, :, :]
    hidden = jnp.tanh(pre).astype(jnp.bfloat16)
    pred = jnp.einsum("dnoh,nsdh->nos", w_out, hidden, preferred_element_type=jnp.float32)
    return pred + b_out[:, :, None]


def on_device(inputs, observed, noise, w_in, b_in, w_out, b_out):
    per_device = w_in.shape[0]
    f_in, hid = w_in.shape[1], w_in.shape[2]
    outs = w_out.shape[1]
    count = observed.shape[0] * lax.axis_size("member") * observed.shape[1] * lax.axis_size("dp")
    first = lax.axis_index("member") * per_device
    own = pack(w_in, b_in, w_out, b_out)
    whole = lax.all_gather(own, "member", axis=0, tiled=True)
    for update in range(UPDATES):
        own_b_out = own[:, -outs:]
        predicted = predict(inputs, own, own_b_out, f_in, hid, outs)
        collected = lax.all_to_all(predicted, "member", split_axis=1, concat_axis=0, tiled=True)
        mean_pred = jnp.mean(collected, axis=0)
        anomaly = (collected - mean_pred[None]).reshape(collected.shape[0], -1)
        misfit = (observed[None] + noise[update].astype(jnp.float32) - collected).reshape(
            collected.shape[0], -1
        )
        gram_part = lax.dot_general(
            anomaly, anomaly, (((1,), (1,)), ((), ())), precision=lax.Precision.HIGHEST
        )
        cross_part = lax.dot_general(
            anomaly, misfit, (((1,), (1,)), ((), ())), precision=lax.Precision.HIGHEST
        )
        gram, cross = lax.psum((gram_part, cross_part), ("member", "dp"))
        gain = solve_gain(gram / count, cross / count)
        if update + 1 < UPDATES:
            moved = lax.dot_general(
                gain, whole, (((0,), (0,)), ((), ())), precision=lax.Precision.HIGHEST
            )
            whole = whole + moved
            own = lax.dynamic_slice_in_dim(whole, first, per_device, 0)
        else:
            columns = lax.dynamic_slice_in_dim(gain, first, per_device, 1)
            moved = lax.dot_general(
                columns, whole, (((0,), (0,)), ((), ())), precision=lax.Precision.HIGHEST
            )
            own = own + moved
    return unpack(own, f_in, hid, outs)


def solution(mesh):
    placed = (
        P("dp", None),
        P("member", "dp"),
        P(None, None, "member", "dp"),
        P("member", None, "dp"),
        P("member", "dp"),
        P("member", None, "dp"),
        P("member", None),
    )
    return jax.shard_map(
        on_device,
        mesh=mesh,
        in_specs=placed,
        out_specs=(
            P("member", None, "dp"),
            P("member", "dp"),
            P("member", None, "dp"),
            P("member", None),
        ),
        check_vma=False,
    )
```

time: 657 us -> 512 us (0.78)
  blocking collectives: 422 us -> 217 us
  waiting for transfers between devices: 157 us -> 219 us
  local copies, waits for them, and re-layouts: 8.08 us -> 21.8 us
  matrix products: 22.2 us -> 13.7 us
  starting transfers between devices: 14.2 us -> 6.69 us
    all_gather x6 -> x0, blocking collectives: 214 us -> none  [the longest x2 116 us: predict(): lax.all_gather(shards[2], 'dp', axis=2, tiled=True)]
    all_gather x8 -> x3, waiting for transfers between devices: 149 us -> 219 us  [the longest x2 171 us: predict(): gathered = lax.all_gather(rounded, 'dp', axis=0, tiled=False)]
    all_to_all x0 -> x1, blocking collectives: none -> 13.8 us  [on_device(): lax.all_to_all(predicted, 'member', split_axis=1, concat_axis=0, tiled=True)]
    dot_general x12 -> x5, matrix products: 20.3 us -> 11.9 us  [the longest x1 4.17 us: on_device(): lax.dot_general(gain, whole, (((0,), (0,)), ((), ())), precision=lax.Prec...]
    slice x0 -> x6, local copies, waits for them, and re-layouts: none -> 8.23 us  [the longest x1 4.04 us: predict(): w_in = gathered[:, :, :a].reshape(d, n, f_in, hid)]
    all_to_all x2 -> x1, starting transfers between devices: 13.8 us -> 6.57 us  [on_device(): lax.all_to_all(predicted, 'member', split_axis=1, concat_axis=0, tiled=True)]
    reshape x0 -> x5, local copies, waits for them, and re-layouts: none -> 6.86 us  [the longest x2 3.46 us: predict(): w_out = gathered[:, :, a:b].reshape(d, n, outs, hid)]
    all_to_all x2 -> x1, waiting for transfers between devices: 6.76 us -> 0.01 us  [on_device(): lax.all_to_all(predicted, 'member', split_axis=1, concat_axis=0, tiled=True)]
  transfers between devices with their start and end apart: 10 -> 4, of which waited for: 5 -> 3; matrix products, arithmetic and copies ran while one was open for 7% -> 3% of each run, Pallas kernels for 0% -> 0%
where the time goes in v1:
time: 512 us; the launch traced here: 511 us
  waiting for transfers between devices  219 us (43%)
  blocking collectives  217 us (42%)
  local copies, waits for them, and re-layouts  21.8 us (4%)
  other arithmetic  19.5 us (4%)
  between operations  14 us (3%)
  matrix products  13.7 us (3%)
  starting transfers between devices  6.69 us (1%)
    psum x2, blocking collectives, on_device(): gram, cross = lax.psum((gram_part, cross_part), ('member', 'dp'))  203 us
    all_gather x2, waiting for transfers between devices, predict(): gathered = lax.all_gather(rounded, 'dp', axis=0, tiled=False)  171 us
    all_gather x1, waiting for transfers between devices, on_device(): whole = lax.all_gather(own, 'member', axis=0, tiled=True)  47.6 us
    all_to_all x1, blocking collectives, on_device(): lax.all_to_all(predicted, 'member', split_axis=1, concat_axis=0, tiled=True)  13.8 us
  transfers between devices with their start and end apart: 4, of which 3 were waited for; matrix products, arithmetic and copies ran while one was open for 3% of the time, Pallas kernels for 0%

profile of v1, /device:TPU:1, one launch (start us, length us, event | category | flops | bytes accessed | tf_op | source)
XLA Modules:
  0.0 511.3 jit_solution(14198276268625181387)
XLA Ops:
  7.2 0.7 convert_bitcast_fusion.2
  7.9 0.8 convert.20
  8.8 0.8 convert.19
  9.6 0.7 pad_maximum_fusion
  10.4 1.0 copy_bitcast_fusion.2
  11.4 1.4 maximum_bitcast_fusion
  12.8 90.6 %all-gather.7.cloned.1.call-done = bf16[32,2,16512]{2,1,0:T(2,128)(2,1)} async-done(((bf16[1,2,16512]{2,1,0:T(2,128)(2,1)}), bf16[32,2,16512]{2,1,0:T(2,128)(2,1)}) %all-gather.7.cloned.1.call-update) | async-done | bytes 2113552 | tf_op jit(solution)/shard_map/all_gather | solution.py:44
  103.4 0.7 convert_bitcast_fusion.1
  104.1 2.9 fusion.60
  107.1 0.8 reshape.148
  107.9 0.8 reshape.147
  108.8 2.5 fusion.20
  111.3 0.7 copy.43
  112.1 6.6 %all-to-all-start = ((f32[2,64,256]{2,0,1:T(2,128)}), f32[2,64,256]{2,0,1:T(2,128)S(1)}, u32[]{:S(2)}, u32[]{:S(2)}) async-start(f32[2,64,256]{2,0,1:T(2,128)} %copy.43), calls=%async_computation | async-start | bytes 262144 | tf_op jit(solution)/shard_map/all_to_all | solution.py:67
  118.8 47.6 %all-gather.9.cloned.1.call-done = f32[16,2,16576]{2,1,0:T(2,128)} async-done(((f32[1,2,16576]{2,1,0:T(2,128)}), f32[16,2,16576]{2,1,0:T(2,128)}) %all-gather.9.cloned.1.call-update) | async-done | bytes 2121744 | tf_op jit(solution)/shard_map/all_gather | solution.py:63
  166.4 3.7 reshape.128
  170.2 0.3 convolution_bitcast_fusion.3
  170.4 0.3 convolution_bitcast_fusion.2
  170.7 107.1 %all-reduce.1 = (f32[32,32]{0,1:T(8,128)S(1)}, f32[32,32]{0,1:T(8,128)S(1)}) all-reduce(f32[32,32]{0,1:T(8,128)S(1)} %convolution_bitcast_fusion.3, f32[32,32]{0,1:T(8,128)S(1)} %convolution_bitcast_fusion.2), channel_id=1, replica_groups=mesh['member'=16,'dp'=32] {'member','dp'}, use_global_device_ids=true, to_apply=%region_1.0 | all-reduce | flops 2048 | bytes 16384 | tf_op jit(solution)/shard_map/psum | solution.py:79
  277.9 2.9 cholesky.44
  280.8 0.6 compare_reduce_fusion.1
  281.5 0.7 fusion.39
  282.1 2.4 custom-call.11
  284.6 0.2 fusion.46
  285.0 4.2 convolution_add_fusion
  289.1 0.7 fusion.35
  289.9 80.4 %all-gather.11.cloned.1.call-done = bf16[32,2,16512]{2,1,0:T(2,128)(2,1)} async-done(((bf16[1,2,16512]{2,1,0:T(2,128)(2,1)}), bf16[32,2,16512]{2,1,0:T(2,128)(2,1)}) %all-gather.11.cloned.1.call-update) | async-done | bytes 2113552 | tf_op jit(solution)/shard_map/all_gather | solution.py:44
  370.3 4.0 fusion.59
  374.4 2.6 reshape.116
  377.0 0.7 convert_bitcast_fusion
  377.8 1.6 reshape.149
  379.4 3.2 fusion.1
  382.6 0.8 fusion.17
  383.6 13.8 %all_to_all.30 = f32[2,64,256]{2,0,1:T(2,128)S(1)} all-to-all(f32[2,64,256]{2,0,1:T(2,128)S(1)} %copy.55), channel_id=1, replica_groups=mesh['member'=16,'dp'=32] {'member'}, dimensions={1} | all-to-all | bytes 262144 | tf_op jit(solution)/shard_map/all_to_all | solution.py:67
  397.5 0.2 convolution_bitcast_fusion.1
  397.8 0.3 convolution_bitcast_fusion
  398.0 96.0 %all-reduce = (f32[32,32]{0,1:T(8,128)S(1)}, f32[32,32]{0,1:T(8,128)S(1)}) all-reduce(f32[32,32]{0,1:T(8,128)S(1)} %convolution_bitcast_fusion.1, f32[32,32]{0,1:T(8,128)S(1)} %convolution_bitcast_fusion), channel_id=1, replica_groups=mesh['member'=16,'dp'=32] {'member','dp'}, use_global_device_ids=true, to_apply=%region_6.10 | all-reduce | flops 2048 | bytes 16384 | tf_op jit(solution)/shard_map/psum | solution.py:79
  494.1 2.9 cholesky.55
  497.1 0.6 compare_reduce_fusion
  497.7 0.7 fusion.40
  498.4 2.4 custom-call.13
  500.8 0.2 fusion.41
  501.0 0.2 fusion.43
  501.3 1.1 convolution_add_fusion.1
  502.4 0.6 slice.74
  503.0 0.6 slice.76
  503.5 0.6 copy.119
  504.2 0.6 copy.118
  (40 shorter events, 1.1 us)
Async XLA Ops:
  7.2 101.6 %copy-start = (bf16[256,64]{0,1:T(8,128)(2,1)S(1)}, bf16[256,64]{0,1:T(8,128)(2,1)}, u32[]{:S(2)}) copy-start(bf16[256,64]{0,1:T(8,128)(2,1)} %param.12) | copy-start | bytes 98308
  7.2 96.2 %all-gather.7.cloned.1.call-start = ((), (), s32[]{:S(2)}) async-start(), calls=%async_computation.2 | async-start | bytes 2179584 | tf_op jit(solution)/shard_map/all_gather | solution.py:44
  10.3 156.0 %all-gather.9.cloned.1.call-start = ((), (), s32[]{:S(2)}) async-start(), calls=%async_computation.3 | async-start | bytes 2263040 | tf_op jit(solution)/shard_map/all_gather | solution.py:63
  107.1 1.7 copy-start.4
  108.8 9.9 %copy-start.2 = (bf16[2,32,4,256]{3,2,1,0:T(4,128)(2,1)S(1)}, bf16[2,32,4,256]{3,2,1,0:T(4,128)(2,1)}, u32[]{:S(2)}) copy-start(bf16[2,32,4,256]{3,2,1,0:T(4,128)(2,1)} %param.14) | copy-start | bytes 393220
  112.1 58.0 %all-to-all-start = ((f32[2,64,256]{2,0,1:T(2,128)}), f32[2,64,256]{2,0,1:T(2,128)S(1)}, u32[]{:S(2)}, u32[]{:S(2)}) async-start(f32[2,64,256]{2,0,1:T(2,128)} %copy.43), calls=%async_computation | async-start | bytes 262144 | tf_op jit(solution)/shard_map/all_to_all | solution.py:67
  118.6 251.7 %all-gather.11.cloned.1.call-start = ((), (), s32[]{:S(2)}) async-start(), calls=%async_computation.4 | async-start | bytes 2179584 | tf_op jit(solution)/shard_map/all_gather | solution.py:44
  118.7 51.4 %copy-start.3 = (f32[4,256]{1,0:T(4,128)S(1)}, f32[4,256]{1,0:T(4,128)}, u32[]{:S(2)}) copy-start(f32[4,256]{1,0:T(4,128)} %param.13) | copy-start | bytes 12292
  379.4 3.2 copy-start.1
Sparse Core Ops, SparseCore 0:
  11.4 91.9 all-gather.6
  105.5 60.8 all-gather.8
  290.0 80.3 all-gather.10

commit v2 on v1

--- a/solution.py
+++ b/solution.py
@@ -36,35 +36,62 @@
     )
 
 
-def predict(inputs, own_flat, b_out, f_in, hid, outs):
-    n = own_flat.shape[0]
+def gather_sum(x, axis):
+    n = lax.axis_size(axis)
+    tiles = jnp.broadcast_to(x[None], (n,) + x.shape)
+    return jnp.sum(lax.all_to_all(tiles, axis, split_axis=0, concat_axis=0, tiled=True), axis=0)
+
+
+def swap_pair(x):
+    n = lax.axis_size("dp")
+    return lax.ppermute(x, "dp", [(i, i ^ 1) for i in range(n)])
+
+
+def predict(inputs_pair, own_flat, f_in, hid, outs, parity):
+    n_dp = lax.axis_size("dp")
     a = f_in * hid
     b = a + outs * hid
     rounded = own_flat[:, : b + hid].astype(jnp.bfloat16)
-    gathered = lax.all_gather(rounded, "dp", axis=0, tiled=False)
-    d = gathered.shape[0]
-    w_in = gathered[:, :, :a].reshape(d, n, f_in, hid)
-    w_out = gathered[:, :, a:b].reshape(d, n, outs, hid)
-    b_in = gathered[:, :, b : b + hid]
-    pre = jnp.einsum("sf,dnfh->nsdh", inputs, w_in, preferred_element_type=jnp.float32)
-    pre = pre + jnp.transpose(b_in, (1, 0, 2)).astype(jnp.float32)[:, None, :, :]
+    tiles = jnp.tile(rounded, (n_dp // rounded.shape[0], 1))
+    got = lax.all_to_all(tiles, "dp", split_axis=0, concat_axis=0, tiled=True)
+    d = got.shape[0]
+    w_in = got[:, :a].reshape(d, f_in, hid)
+    w_out = got[:, a:b].reshape(d, outs, hid)
+    b_in = got[:, b : b + hid]
+    b_out = jnp.where(parity == 0, own_flat[0, -outs:], own_flat[1, -outs:])
+    pre = jnp.einsum("sf,dfh->sdh", inputs_pair, w_in, preferred_element_type=jnp.float32)
+    pre = pre + b_in.astype(jnp.float32)[None]
     hidden = jnp.tanh(pre).astype(jnp.bfloat16)
-    pred = jnp.einsum("dnoh,nsdh->nos", w_out, hidden, preferred_element_type=jnp.float32)
-    return pred + b_out[:, :, None]
+    pred = jnp.einsum("doh,sdh->os", w_out, hidden, preferred_element_type=jnp.float32)
+    return pred + b_out[:, None]
+
+
+def collect(pred, n_samples, parity):
+    n_m = lax.axis_size("member")
+    outs = pred.shape[0]
+    blocks = pred.reshape(n_m, outs // n_m, pred.shape[1])
+    got = lax.all_to_all(blocks, "member", split_axis=0, concat_axis=0, tiled=True)
+    mine = got[:, :, :n_samples]
+    other = swap_pair(got[:, :, n_samples:])
+    even = jnp.where(parity == 0, mine, other)
+    odd = jnp.where(parity == 0, other, mine)
+    return jnp.stack([even, odd], axis=1).reshape(2 * n_m, outs // n_m, n_samples)
 
 
 def on_device(inputs, observed, noise, w_in, b_in, w_out, b_out):
     per_device = w_in.shape[0]
     f_in, hid = w_in.shape[1], w_in.shape[2]
     outs = w_out.shape[1]
+    n_samples = inputs.shape[0]
     count = observed.shape[0] * lax.axis_size("member") * observed.shape[1] * lax.axis_size("dp")
     first = lax.axis_index("member") * per_device
+    parity = lax.axis_index("dp") % 2
+    inputs_pair = jnp.concatenate([inputs, swap_pair(inputs)], axis=0)
     own = pack(w_in, b_in, w_out, b_out)
     whole = lax.all_gather(own, "member", axis=0, tiled=True)
     for update in range(UPDATES):
-        own_b_out = own[:, -outs:]
-        predicted = predict(inputs, own, own_b_out, f_in, hid, outs)
-        collected = lax.all_to_all(predicted, "member", split_axis=1, concat_axis=0, tiled=True)
+        predicted = predict(inputs_pair, own, f_in, hid, outs, parity)
+        collected = collect(predicted, n_samples, parity)
         mean_pred = jnp.mean(collected, axis=0)
         anomaly = (collected - mean_pred[None]).reshape(collected.shape[0], -1)
         misfit = (observed[None] + noise[update].astype(jnp.float32) - collected).reshape(
@@ -76,8 +103,8 @@
         cross_part = lax.dot_general(
             anomaly, misfit, (((1,), (1,)), ((), ())), precision=lax.Precision.HIGHEST
         )
-        gram, cross = lax.psum((gram_part, cross_part), ("member", "dp"))
-        gain = solve_gain(gram / count, cross / count)
+        sums = gather_sum(gather_sum(jnp.stack([gram_part, cross_part]), "member"), "dp")
+        gain = solve_gain(sums[0] / count, sums[1] / count)
         if update + 1 < UPDATES:
             moved = lax.dot_general(
                 gain, whole, (((0,), (0,)), ((), ())), precision=lax.Precision.HIGHEST

time: 512 us -> 290 us (0.57)
  blocking collectives: 217 us -> 51.8 us
  waiting for transfers between devices: 219 us -> 84.5 us
  starting transfers between devices: 6.69 us -> 59.7 us
  other arithmetic: 19.5 us -> 35 us
  local copies, waits for them, and re-layouts: 21.8 us -> 31.3 us
    psum x2 -> x0, blocking collectives: 203 us -> none  [on_device(): gram, cross = lax.psum((gram_part, cross_part), ('member', 'dp'))]
    all_gather x2 -> x0, waiting for transfers between devices: 171 us -> none  [predict(): gathered = lax.all_gather(rounded, 'dp', axis=0, tiled=False)]
    all_to_all x1 -> x4, waiting for transfers between devices: 0.01 us -> 74.1 us  [the longest x2 54.6 us: predict(): got = lax.all_to_all(tiles, 'dp', split_axis=0, concat_axis=0, tiled=True)]
    all_to_all x1 -> x4, starting transfers between devices: 6.57 us -> 48.2 us  [the longest x2 33.7 us: predict(): got = lax.all_to_all(tiles, 'dp', split_axis=0, concat_axis=0, tiled=True)]
    all_gather x1, waiting for transfers between devices: 47.6 us -> 8.93 us  [on_device(): whole = lax.all_gather(own, 'member', axis=0, tiled=True)]
    all_to_all x1 -> x4, blocking collectives: 13.8 us -> 51.8 us  [the longest x3 41 us: gather_sum(): lax.all_to_all(tiles, axis, split_axis=0, concat_axis=0, tiled=True)]
    all_to_all x0 -> x6, other arithmetic: none -> 19.5 us  [the longest x2 15.1 us: predict(): got = lax.all_to_all(tiles, 'dp', split_axis=0, concat_axis=0, tiled=True)]
    unnamed x15 -> x44, local copies, waits for them, and re-layouts: 5.69 us -> 19.3 us
  transfers between devices with their start and end apart: 4 -> 8, of which waited for: 3 -> 7; matrix products, arithmetic and copies ran while one was open for 3% -> 5% of each run, Pallas kernels for 0% -> 0%
where the time goes in v2:
time: 290 us; the launch traced here: 289 us
  waiting for transfers between devices  84.5 us (29%)
  starting transfers between devices  59.7 us (21%)
  blocking collectives  51.8 us (18%)
  other arithmetic  35 us (12%)
  local copies, waits for them, and re-layouts  31.3 us (11%)
  between operations  14.7 us (5%)
  matrix products  12 us (4%)
    all_to_all x2, waiting for transfers between devices, predict(): got = lax.all_to_all(tiles, 'dp', split_axis=0, concat_axis=0, tiled=True)  54.6 us
    all_to_all x3, blocking collectives, gather_sum(): lax.all_to_all(tiles, axis, split_axis=0, concat_axis=0, tiled=True)  41 us
    all_to_all x2, starting transfers between devices, predict(): got = lax.all_to_all(tiles, 'dp', split_axis=0, concat_axis=0, tiled=True)  33.7 us
    unnamed x44, local copies, waits for them, and re-layouts  19.3 us
    all_to_all x2, other arithmetic, predict(): got = lax.all_to_all(tiles, 'dp', split_axis=0, concat_axis=0, tiled=True)  15.1 us
    all_to_all x1, waiting for transfers between devices, gather_sum(): lax.all_to_all(tiles, axis, split_axis=0, concat_axis=0, tiled=True)  12.9 us
    ppermute x3, starting transfers between devices, swap_pair(): return lax.ppermute(x, 'dp', [(i, i ^ 1) for i in range(n)])  11.4 us
    all_to_all x1, blocking collectives, collect(): lax.all_to_all(blocks, 'member', split_axis=0, concat_axis=0, tiled=True)  10.8 us
  transfers between devices with their start and end apart: 8, of which 7 were waited for; matrix products, arithmetic and copies ran while one was open for 5% of the time, Pallas kernels for 0%

profile of v2, /device:TPU:1, one launch (start us, length us, event | category | flops | bytes accessed | tf_op | source)
XLA Modules:
  0.0 289.1 jit_solution(6216444850438449542)
XLA Ops:
  7.2 0.7 convert.16
  7.8 1.0 fusion.58
  9.4 2.0 all_to_all.46
  12.0 7.0 %reduce.14 = bf16[32,16512]{1,0:T(8,128)(2,1)S(1)} reduce(bf16[32,1,16512]{2,1,0:T(2,128)(2,1)S(1)} %all_to_all.46, bf16[]{:T(256)} %broadcast.178), dimensions={1}, to_apply=%all_to_all.46.reduce_sub_computation | reduce | bytes 2113538 | tf_op jit(solution)/shard_map/all_to_all | solution.py:56
  19.1 1.6 reshape.215
  20.7 14.4 %all-to-all-start = ((bf16[32,2,8256]{2,1,0:T(2,128)(2,1)}), bf16[32,2,8256]{2,1,0:T(2,128)(2,1)S(1)}, u32[]{:S(2)}, u32[]{:S(2)}) async-start(bf16[32,2,8256]{2,1,0:T(2,128)(2,1)} %reshape.215), calls=%async_computation | async-start | bytes 2129920 | tf_op jit(solution)/shard_map/all_to_all | solution.py:56
  35.1 2.1 collective-permute-start
  37.4 26.2 %all-to-all-done = bf16[32,2,8256]{2,1,0:T(2,128)(2,1)S(1)} async-done(((bf16[32,2,8256]{2,1,0:T(2,128)(2,1)}), bf16[32,2,8256]{2,1,0:T(2,128)(2,1)S(1)}, u32[]{:S(2)}, u32[]{:S(2)}) %all-to-all-start) | async-done | bytes 1056800 | tf_op jit(solution)/shard_map/all_to_all | solution.py:56
  63.6 1.3 reshape.216
  65.4 2.5 fusion.10
  67.8 0.7 reshape.186
  68.5 6.9 %all-to-all-start.1 = ((f32[16,4,512]{2,1,0:T(4,128)}), f32[16,4,512]{2,1,0:T(4,128)S(1)}, u32[]{:S(2)}, u32[]{:S(2)}) async-start(f32[16,4,512]{2,1,0:T(4,128)} %reshape.186), calls=%async_computation.1 | async-start | bytes 262144 | tf_op jit(solution)/shard_map/all_to_all | solution.py:73
  75.6 0.7 maximum_bitcast_fusion
  76.3 6.6 %all-to-all-done.1 = f32[16,4,512]{2,1,0:T(4,128)S(1)} async-done(((f32[16,4,512]{2,1,0:T(4,128)}), f32[16,4,512]{2,1,0:T(4,128)S(1)}, u32[]{:S(2)}, u32[]{:S(2)}) %all-to-all-start.1) | async-done | bytes 131104 | tf_op jit(solution)/shard_map/all_to_all | solution.py:73
  83.0 4.7 %collective-permute-start.1 = (f32[16,4,256]{2,0,1:T(8,128)S(1)}, f32[16,4,256]{2,0,1:T(8,128)S(1)}, u32[]{:S(2)}, u32[]{:S(2)}) collective-permute-start(f32[16,4,256]{2,0,1:T(8,128)S(1)} %copy.112), channel_id=1, source_target_pairs={{0,1},{1,0},{2,3},{3,2},{4,5},{5,4},{6,7},{7,6},{8,9},{9,8},{10,11... | collective-permute-start | bytes 196616 | tf_op jit(solution)/shard_map/ppermute | solution.py:47
  89.6 10.8 %all_to_all.56 = f32[16,1,2048]{2,1,0:T(1,128)S(1)} all-to-all(f32[16,1,2048]{2,1,0:T(1,128)S(1)} %reshape.217), channel_id=1, replica_groups=mesh['member'=16,'dp'=32] {'member'}, dimensions={0} | all-to-all | bytes 262144 | tf_op jit(solution)/shard_map/all_to_all | solution.py:42
  100.9 0.9 reduce.15
  102.2 1.2 reshape.219
  103.4 7.5 %all-to-all-start.3 = ((f32[32,1,2048]{2,1,0:T(1,128)}), f32[32,1,2048]{2,1,0:T(1,128)S(1)}, u32[]{:S(2)}, u32[]{:S(2)}) async-start(f32[32,1,2048]{2,1,0:T(1,128)} %reshape.219), calls=%async_computation.3 | async-start | bytes 524288 | tf_op jit(solution)/shard_map/all_to_all | solution.py:42
  110.9 12.9 %all-to-all-done.3 = f32[32,1,2048]{2,1,0:T(1,128)S(1)} async-done(((f32[32,1,2048]{2,1,0:T(1,128)}), f32[32,1,2048]{2,1,0:T(1,128)S(1)}, u32[]{:S(2)}, u32[]{:S(2)}) %all-to-all-start.3) | async-done | bytes 262176 | tf_op jit(solution)/shard_map/all_to_all | solution.py:42
  123.8 1.3 reduce.16
  125.7 2.9 %cholesky.44 = f32[32,32]{1,0:T(8,128)S(1)} custom-call(f32[32,32]{1,0:T(8,128)S(1)} %fusion.43), custom_call_target="Cholesky" | custom-call | tf_op jit(solution)/shard_map/jit(cholesky)/cholesky | solution.py:14
  128.7 0.6 compare_reduce_fusion.1
  129.3 0.7 fusion.30
  130.0 2.4 custom-call.11
  132.9 8.9 %all-gather.3.cloned.1.call-done = f32[16,2,16576]{2,1,0:T(2,128)} async-done(((f32[1,2,16576]{2,1,0:T(2,128)}), f32[16,2,16576]{2,1,0:T(2,128)}) %all-gather.3.cloned.1.call-update) | async-done | bytes 2121744 | tf_op jit(solution)/shard_map/all_gather | solution.py:91
  141.8 3.7 %reshape.199 = f32[32,16576]{1,0:T(8,128)} reshape(f32[16,2,16576]{2,1,0:T(2,128)} %all-gather.3.cloned.1.call-done) | data formatting | bytes 4243456
  145.5 4.1 %convolution_add_fusion = f32[32,16576]{1,0:T(8,128)S(1)} fusion(f32[32,16576]{1,0:T(8,128)} %reshape.199, f32[32,32]{1,0:T(8,128)S(1)} %fusion.41), kind=kOutput, calls=%fused_computation | convolution fusion | flops 204216320 | bytes 4247552 | tf_op jit(solution)/shard_map/dot_general | solution.py:109
  150.3 4.0 %all_to_all.47 = bf16[32,1,16512]{2,1,0:T(2,128)(2,1)} reshape(bf16[16,2,16512]{2,1,0:T(2,128)(2,1)S(1)} %tile.5) | data formatting | bytes 2113536 | tf_op jit(solution)/shard_map/all_to_all | solution.py:56
  154.3 8.1 %reduce.17 = bf16[32,16512]{1,0:T(8,128)(2,1)S(1)} reduce(bf16[32,1,16512]{2,1,0:T(2,128)(2,1)} %all_to_all.47, bf16[]{:T(256)} %broadcast.178), dimensions={1}, to_apply=%all_to_all.47.reduce_sub_computation | reduce | bytes 2113538 | tf_op jit(solution)/shard_map/all_to_all | solution.py:56
  162.4 1.8 reshape.221
  164.2 19.3 %all-to-all-start.4 = ((bf16[32,2,8256]{2,1,0:T(2,128)(2,1)}), bf16[32,2,8256]{2,1,0:T(2,128)(2,1)S(1)}, u32[]{:S(2)}, u32[]{:S(2)}) async-start(bf16[32,2,8256]{2,1,0:T(2,128)(2,1)} %reshape.221), calls=%async_computation.4 | async-start | bytes 2129920 | tf_op jit(solution)/shard_map/all_to_all | solution.py:56
  183.6 28.4 %all-to-all-done.4 = bf16[32,2,8256]{2,1,0:T(2,128)(2,1)S(1)} async-done(((bf16[32,2,8256]{2,1,0:T(2,128)(2,1)}), bf16[32,2,8256]{2,1,0:T(2,128)(2,1)S(1)}, u32[]{:S(2)}, u32[]{:S(2)}) %all-to-all-start.4) | async-done | bytes 1056800 | tf_op jit(solution)/shard_map/all_to_all | solution.py:56
  212.0 3.6 %reshape.222 = bf16[32,1,16512]{2,1,0:T(2,128)(2,1)} reshape(bf16[32,2,8256]{2,1,0:T(2,128)(2,1)S(1)} %all-to-all-done.4) | data formatting | bytes 2113536
  215.7 1.7 copy.175
  217.7 2.5 fusion.11
  220.2 10.8 %all_to_all.57 = f32[16,4,512]{2,1,0:T(4,128)S(1)} all-to-all(f32[16,4,512]{2,1,0:T(4,128)S(1)} %reshape.189), channel_id=1, replica_groups=mesh['member'=16,'dp'=32] {'member'}, dimensions={0} | all-to-all | bytes 262144 | tf_op jit(solution)/shard_map/all_to_all | solution.py:73
  231.0 4.5 %collective-permute-start.2 = (f32[16,4,256]{2,0,1:T(8,128)S(1)}, f32[16,4,256]{2,0,1:T(8,128)S(1)}, u32[]{:S(2)}, u32[]{:S(2)}) collective-permute-start(f32[16,4,256]{2,0,1:T(8,128)S(1)} %copy.116), channel_id=1, source_target_pairs={{0,1},{1,0},{2,3},{3,2},{4,5},{5,4},{6,7},{7,6},{8,9},{9,8},{10,11... | collective-permute-start | bytes 196616 | tf_op jit(solution)/shard_map/ppermute | solution.py:47
  235.6 0.9 collective-permute-done.2
  237.6 10.2 %all_to_all.58 = f32[16,1,2048]{2,1,0:T(1,128)S(1)} all-to-all(f32[16,1,2048]{2,1,0:T(1,128)S(1)} %reshape.223), channel_id=1, replica_groups=mesh['member'=16,'dp'=32] {'member'}, dimensions={0} | all-to-all | bytes 262144 | tf_op jit(solution)/shard_map/all_to_all | solution.py:42
  247.8 0.9 reduce.18
  249.6 20.0 %all_to_all.59 = f32[32,1,2048]{2,1,0:T(1,128)S(1)} all-to-all(f32[32,1,2048]{2,1,0:T(1,128)S(1)} %reshape.225), channel_id=1, replica_groups=mesh['member'=16,'dp'=32] {'dp'}, dimensions={0} | all-to-all | bytes 524288 | tf_op jit(solution)/shard_map/all_to_all | solution.py:42
  269.6 1.3 reduce.19
  271.5 2.9 %cholesky.55 = f32[32,32]{1,0:T(8,128)S(1)} custom-call(f32[32,32]{1,0:T(8,128)S(1)} %fusion.37), custom_call_target="Cholesky" | custom-call | tf_op jit(solution)/shard_map/jit(cholesky)/cholesky | solution.py:14
  274.5 0.6 compare_reduce_fusion
  275.1 0.7 fusion.31
  275.8 2.4 custom-call.13
  278.7 1.1 convolution_add_fusion.1
  (98 shorter events, 12.0 us)
Async XLA Ops:
  19.0 16.1 %copy-start.6 = (bf16[256,64]{0,1:T(8,128)(2,1)S(1)}, bf16[256,64]{0,1:T(8,128)(2,1)}, u32[]{:S(2)}) copy-start(bf16[256,64]{0,1:T(8,128)(2,1)} %param.12) | copy-start | bytes 98308
  19.0 18.3 %copy-start.4 = (f32[2,64]{1,0:T(2,128)S(1)}, f32[2,64]{1,0:T(2,128)}, u32[]{:S(2)}) copy-start(f32[2,64]{1,0:T(2,128)} %param.18) | copy-start | bytes 1540
  19.0 18.3 %copy-start = (f32[2,64,128]{2,1,0:T(8,128)S(1)}, f32[2,64,128]{2,1,0:T(8,128)}, u32[]{:S(2)}) copy-start(f32[2,64,128]{2,1,0:T(8,128)} %param.17) | copy-start | bytes 196612
  19.0 18.3 %copy-start.1 = (f32[2,64,128]{2,1,0:T(8,128)S(1)}, f32[2,64,128]{2,1,0:T(8,128)}, u32[]{:S(2)}) copy-start(f32[2,64,128]{2,1,0:T(8,128)} %param.15) | copy-start | bytes 196612
  20.7 42.9 %all-to-all-start = ((bf16[32,2,8256]{2,1,0:T(2,128)(2,1)}), bf16[32,2,8256]{2,1,0:T(2,128)(2,1)S(1)}, u32[]{:S(2)}, u32[]{:S(2)}) async-start(bf16[32,2,8256]{2,1,0:T(2,128)(2,1)} %reshape.215), calls=%async_computation | async-start | bytes 2129920 | tf_op jit(solution)/shard_map/all_to_all | solution.py:56
  35.1 30.2 %collective-permute-start = (bf16[256,64]{0,1:T(8,128)(2,1)S(1)}, bf16[256,64]{0,1:T(8,128)(2,1)S(1)}, u32[]{:S(2)}, u32[]{:S(2)}) collective-permute-start(bf16[256,64]{0,1:T(8,128)(2,1)S(1)} %copy-done.6), channel_id=1, source_target_pairs={{0,1},{1,0},{2,3},{3,2},{4,5},{5,4},{6,7},{7,6},{8,9},{9,8},{10,11... | collective-permute-start | bytes 98312 | tf_op jit(solution)/shard_map/ppermute | solution.py:47
  65.3 10.2 %copy-start.5 = (f32[2,128]{1,0:T(2,128)S(1)}, f32[2,128]{1,0:T(2,128)}, u32[]{:S(2)}) copy-start(f32[2,128]{1,0:T(2,128)} %param.16) | copy-start | bytes 3076
  65.4 22.4 %copy-start.2 = (bf16[2,32,4,256]{3,2,1,0:T(4,128)(2,1)S(1)}, bf16[2,32,4,256]{3,2,1,0:T(4,128)(2,1)}, u32[]{:S(2)}) copy-start(bf16[2,32,4,256]{3,2,1,0:T(4,128)(2,1)} %param.14) | copy-start | bytes 393220
  65.4 23.1 %copy-start.3 = (f32[4,256]{1,0:T(4,128)S(1)}, f32[4,256]{1,0:T(4,128)}, u32[]{:S(2)}) copy-start(f32[4,256]{1,0:T(4,128)} %param.13) | copy-start | bytes 12292
  68.5 14.4 %all-to-all-start.1 = ((f32[16,4,512]{2,1,0:T(4,128)}), f32[16,4,512]{2,1,0:T(4,128)S(1)}, u32[]{:S(2)}, u32[]{:S(2)}) async-start(f32[16,4,512]{2,1,0:T(4,128)} %reshape.186), calls=%async_computation.1 | async-start | bytes 262144 | tf_op jit(solution)/shard_map/all_to_all | solution.py:73
  75.5 66.3 %all-gather.3.cloned.1.call-start = ((), (), s32[]{:S(2)}) async-start(), calls=%async_computation.8 | async-start | bytes 2263040 | tf_op jit(solution)/shard_map/all_gather | solution.py:91
  83.0 5.4 %collective-permute-start.1 = (f32[16,4,256]{2,0,1:T(8,128)S(1)}, f32[16,4,256]{2,0,1:T(8,128)S(1)}, u32[]{:S(2)}, u32[]{:S(2)}) collective-permute-start(f32[16,4,256]{2,0,1:T(8,128)S(1)} %copy.112), channel_id=1, source_target_pairs={{0,1},{1,0},{2,3},{3,2},{4,5},{5,4},{6,7},{7,6},{8,9},{9,8},{10,11... | collective-permute-start | bytes 196616 | tf_op jit(solution)/shard_map/ppermute | solution.py:47
  103.4 20.5 %all-to-all-start.3 = ((f32[32,1,2048]{2,1,0:T(1,128)}), f32[32,1,2048]{2,1,0:T(1,128)S(1)}, u32[]{:S(2)}, u32[]{:S(2)}) async-start(f32[32,1,2048]{2,1,0:T(1,128)} %reshape.219), calls=%async_computation.3 | async-start | bytes 524288 | tf_op jit(solution)/shard_map/all_to_all | solution.py:42
  164.2 47.8 %all-to-all-start.4 = ((bf16[32,2,8256]{2,1,0:T(2,128)(2,1)}), bf16[32,2,8256]{2,1,0:T(2,128)(2,1)S(1)}, u32[]{:S(2)}, u32[]{:S(2)}) async-start(bf16[32,2,8256]{2,1,0:T(2,128)(2,1)} %reshape.221), calls=%async_computation.4 | async-start | bytes 2129920 | tf_op jit(solution)/shard_map/all_to_all | solution.py:56
  231.0 5.4 %collective-permute-start.2 = (f32[16,4,256]{2,0,1:T(8,128)S(1)}, f32[16,4,256]{2,0,1:T(8,128)S(1)}, u32[]{:S(2)}, u32[]{:S(2)}) collective-permute-start(f32[16,4,256]{2,0,1:T(8,128)S(1)} %copy.116), channel_id=1, source_target_pairs={{0,1},{1,0},{2,3},{3,2},{4,5},{5,4},{6,7},{7,6},{8,9},{9,8},{10,11... | collective-permute-start | bytes 196616 | tf_op jit(solution)/shard_map/ppermute | solution.py:47
Sparse Core Ops, SparseCore 0:
  78.4 63.3 all-gather.2

commit v3 on v2

--- a/solution.py
+++ b/solution.py
@@ -17,22 +17,19 @@
 
 
 def pack(w_in, b_in, w_out, b_out):
-    n = w_in.shape[0]
+    n, hid = w_in.shape[0], w_in.shape[2]
+    pad = jnp.zeros((n, hid - b_out.shape[1]), b_out.dtype)
     return jnp.concatenate(
-        [w_in.reshape(n, -1), w_out.reshape(n, -1), b_in.reshape(n, -1), b_out.reshape(n, -1)], axis=1
+        [w_in, w_out, b_in[:, None, :], jnp.concatenate([b_out, pad], axis=1)[:, None, :]], axis=1
     )
 
 
 def unpack(flat, f_in, hid, outs):
-    n = flat.shape[0]
-    a = f_in * hid
-    b = a + outs * hid
-    c = b + hid
     return (
-        flat[:, :a].reshape(n, f_in, hid),
-        flat[:, b:c].reshape(n, hid),
-        flat[:, a:b].reshape(n, outs, hid),
-        flat[:, c:].reshape(n, outs),
+        flat[:, :f_in, :],
+        flat[:, f_in + outs, :],
+        flat[:, f_in : f_in + outs, :],
+        flat[:, f_in + outs + 1, :outs],
     )
 
 
@@ -49,16 +46,14 @@
 
 def predict(inputs_pair, own_flat, f_in, hid, outs, parity):
     n_dp = lax.axis_size("dp")
-    a = f_in * hid
-    b = a + outs * hid
-    rounded = own_flat[:, : b + hid].astype(jnp.bfloat16)
-    tiles = jnp.tile(rounded, (n_dp // rounded.shape[0], 1))
+    rows = f_in + outs + 1
+    rounded = own_flat[:, :rows, :].astype(jnp.bfloat16)
+    tiles = jnp.tile(rounded, (n_dp // rounded.shape[0], 1, 1))
     got = lax.all_to_all(tiles, "dp", split_axis=0, concat_axis=0, tiled=True)
-    d = got.shape[0]
-    w_in = got[:, :a].reshape(d, f_in, hid)
-    w_out = got[:, a:b].reshape(d, outs, hid)
-    b_in = got[:, b : b + hid]
-    b_out = jnp.where(parity == 0, own_flat[0, -outs:], own_flat[1, -outs:])
+    w_in = got[:, :f_in, :]
+    w_out = got[:, f_in : f_in + outs, :]
+    b_in = got[:, f_in + outs, :]
+    b_out = jnp.where(parity == 0, own_flat[0, rows, :outs], own_flat[1, rows, :outs])
     pre = jnp.einsum("sf,dfh->sdh", inputs_pair, w_in, preferred_element_type=jnp.float32)
     pre = pre + b_in.astype(jnp.float32)[None]
     hidden = jnp.tanh(pre).astype(jnp.bfloat16)
@@ -106,16 +101,12 @@
         sums = gather_sum(gather_sum(jnp.stack([gram_part, cross_part]), "member"), "dp")
         gain = solve_gain(sums[0] / count, sums[1] / count)
         if update + 1 < UPDATES:
-            moved = lax.dot_general(
-                gain, whole, (((0,), (0,)), ((), ())), precision=lax.Precision.HIGHEST
-            )
+            moved = jnp.einsum("kj,kab->jab", gain, whole, precision=lax.Precision.HIGHEST)
             whole = whole + moved
             own = lax.dynamic_slice_in_dim(whole, first, per_device, 0)
         else:
             columns = lax.dynamic_slice_in_dim(gain, first, per_device, 1)
-            moved = lax.dot_general(
-                columns, whole, (((0,), (0,)), ((), ())), precision=lax.Precision.HIGHEST
-            )
+            moved = jnp.einsum("kj,kab->jab", columns, whole, precision=lax.Precision.HIGHEST)
             own = own + moved
     return unpack(own, f_in, hid, outs)
 

time: 290 us -> 259 us (0.89)
  local copies, waits for them, and re-layouts: 31.3 us -> 10.4 us
  other arithmetic: 35 us -> 21.5 us
    all_to_all x2 -> x0, other arithmetic: 15.1 us -> none  [predict(): got = lax.all_to_all(tiles, 'dp', split_axis=0, concat_axis=0, tiled=True)]
    unnamed x44 -> x30, local copies, waits for them, and re-layouts: 19.3 us -> 4.74 us
    all_to_all x3 -> x0, local copies, waits for them, and re-layouts: 6.56 us -> none  [predict(): got = lax.all_to_all(tiles, 'dp', split_axis=0, concat_axis=0, tiled=True)]
where the time goes in v3:
time: 259 us; the launch traced here: 258 us
  waiting for transfers between devices  87.3 us (34%)
  starting transfers between devices  59.9 us (23%)
  blocking collectives  51.7 us (20%)
  other arithmetic  21.5 us (8%)
  between operations  14.6 us (6%)
  matrix products  12.4 us (5%)
  local copies, waits for them, and re-layouts  10.4 us (4%)
    all_to_all x2, waiting for transfers between devices, predict(): got = lax.all_to_all(tiles, 'dp', split_axis=0, concat_axis=0, tiled=True)  56.7 us
    all_to_all x3, blocking collectives, gather_sum(): lax.all_to_all(tiles, axis, split_axis=0, concat_axis=0, tiled=True)  41.1 us
    all_to_all x2, starting transfers between devices, predict(): got = lax.all_to_all(tiles, 'dp', split_axis=0, concat_axis=0, tiled=True)  34 us
    all_to_all x1, waiting for transfers between devices, gather_sum(): lax.all_to_all(tiles, axis, split_axis=0, concat_axis=0, tiled=True)  12.9 us
    ppermute x3, starting transfers between devices, swap_pair(): return lax.ppermute(x, 'dp', [(i, i ^ 1) for i in range(n)])  11.4 us
    all_to_all x1, blocking collectives, collect(): lax.all_to_all(blocks, 'member', split_axis=0, concat_axis=0, tiled=True)  10.6 us
    all_gather x1, waiting for transfers between devices, on_device(): whole = lax.all_gather(own, 'member', axis=0, tiled=True)  9.42 us
    all_to_all x1, starting transfers between devices, gather_sum(): lax.all_to_all(tiles, axis, split_axis=0, concat_axis=0, tiled=True)  7.51 us
  transfers between devices with their start and end apart: 8, of which 7 were waited for; matrix products, arithmetic and copies ran while one was open for 5% of the time, Pallas kernels for 0%

profile of v3, /device:TPU:1, one launch (start us, length us, event | category | flops | bytes accessed | tf_op | source)
XLA Modules:
  0.0 257.8 jit_solution(17804455706372559865)
XLA Ops:
  7.2 0.7 convert.18
  7.9 0.8 convert.16
  8.7 0.8 convert.17
  9.6 1.1 tile.8
  10.7 14.4 %all-to-all-start = ((bf16[32,129,128]{2,1,0:T(8,128)(2,1)}), bf16[32,129,128]{2,1,0:T(8,128)(2,1)S(1)}, u32[]{:S(2)}, u32[]{:S(2)}) async-start(bf16[32,129,128]{2,1,0:T(8,128)(2,1)} %bitcast.3), calls=%async_computation | async-start | bytes 2228224 | tf_op jit(solution)/shard_map/all_to_all | solution.py:52
  25.2 2.1 collective-permute-start
  27.4 27.3 %all-to-all-done = bf16[32,129,128]{2,1,0:T(8,128)(2,1)S(1)} async-done(((bf16[32,129,128]{2,1,0:T(8,128)(2,1)}), bf16[32,129,128]{2,1,0:T(8,128)(2,1)S(1)}, u32[]{:S(2)}, u32[]{:S(2)}) %all-to-all-start) | async-done | bytes 1056800 | tf_op jit(solution)/shard_map/all_to_all | solution.py:52
  54.8 2.5 fusion.14
  57.2 0.7 reshape.164
  57.9 6.9 %all-to-all-start.1 = ((f32[16,4,512]{2,1,0:T(4,128)}), f32[16,4,512]{2,1,0:T(4,128)S(1)}, u32[]{:S(2)}, u32[]{:S(2)}) async-start(f32[16,4,512]{2,1,0:T(4,128)} %reshape.164), calls=%async_computation.1 | async-start | bytes 262144 | tf_op jit(solution)/shard_map/all_to_all | solution.py:68
  65.0 0.7 pad_maximum_fusion
  65.7 6.7 %all-to-all-done.1 = f32[16,4,512]{2,1,0:T(4,128)S(1)} async-done(((f32[16,4,512]{2,1,0:T(4,128)}), f32[16,4,512]{2,1,0:T(4,128)S(1)}, u32[]{:S(2)}, u32[]{:S(2)}) %all-to-all-start.1) | async-done | bytes 131104 | tf_op jit(solution)/shard_map/all_to_all | solution.py:68
  72.3 4.6 %collective-permute-start.1 = (f32[16,4,256]{2,0,1:T(8,128)S(1)}, f32[16,4,256]{2,0,1:T(8,128)S(1)}, u32[]{:S(2)}, u32[]{:S(2)}) collective-permute-start(f32[16,4,256]{2,0,1:T(8,128)S(1)} %copy.133), channel_id=1, source_target_pairs={{0,1},{1,0},{2,3},{3,2},{4,5},{5,4},{6,7},{7,6},{8,9},{9,8},{10,11... | collective-permute-start | bytes 196616 | tf_op jit(solution)/shard_map/ppermute | solution.py:44
  77.0 0.8 collective-permute-done.1
  79.0 10.8 %all_to_all.40 = f32[16,1,2048]{2,1,0:T(1,128)S(1)} all-to-all(f32[16,1,2048]{2,1,0:T(1,128)S(1)} %reshape.191), channel_id=1, replica_groups=mesh['member'=16,'dp'=32] {'member'}, dimensions={0} | all-to-all | bytes 262144 | tf_op jit(solution)/shard_map/all_to_all | solution.py:39
  89.8 0.5 broadcast.178
  90.3 0.9 reduce.14
  91.6 1.2 reshape.193
  92.8 7.5 %all-to-all-start.3 = ((f32[32,1,2048]{2,1,0:T(1,128)}), f32[32,1,2048]{2,1,0:T(1,128)S(1)}, u32[]{:S(2)}, u32[]{:S(2)}) async-start(f32[32,1,2048]{2,1,0:T(1,128)} %reshape.193), calls=%async_computation.3 | async-start | bytes 524288 | tf_op jit(solution)/shard_map/all_to_all | solution.py:39
  100.3 12.9 %all-to-all-done.3 = f32[32,1,2048]{2,1,0:T(1,128)S(1)} async-done(((f32[32,1,2048]{2,1,0:T(1,128)}), f32[32,1,2048]{2,1,0:T(1,128)S(1)}, u32[]{:S(2)}, u32[]{:S(2)}) %all-to-all-start.3) | async-done | bytes 262176 | tf_op jit(solution)/shard_map/all_to_all | solution.py:39
  113.2 1.3 reduce.15
  115.1 2.9 %cholesky.44 = f32[32,32]{1,0:T(8,128)S(1)} custom-call(f32[32,32]{1,0:T(8,128)S(1)} %fusion.52), custom_call_target="Cholesky" | custom-call | tf_op jit(solution)/shard_map/jit(cholesky)/cholesky | solution.py:14
  118.1 0.6 compare_reduce_fusion.1
  118.7 0.7 fusion.40
  119.4 2.4 custom-call.11
  122.3 9.4 %all-gather.2.cloned.1.call-done = f32[32,130,128]{2,1,0:T(8,128)} async-done(((f32[2,130,128]{2,1,0:T(8,128)}), f32[32,130,128]{2,1,0:T(8,128)}) %all-gather.2.cloned.1.call-update) | async-done | bytes 2129936 | tf_op jit(solution)/shard_map/all_gather | solution.py:86
  131.8 4.5 %copy_add_fusion = f32[32,130,128]{2,0,1:T(8,128)S(1)} fusion(f32[32,130,128]{2,1,0:T(8,128)} %all-gather.2.cloned.1.call-done, f32[32,32,1]{0,1,2:T(8,128)S(1)} %convolution_bitcast_fusion.2), kind=kOutput, calls=%fused_computation.10 | convolution fusion | flops 205004800 | bytes 4263936 | tf_op jit(solution)/shard_map/kj,kab->jab/dot_general | solution.py:104
  136.4 1.1 tile.20
  137.5 19.5 %all-to-all-start.4 = ((bf16[32,129,128]{2,1,0:T(8,128)(2,1)}), bf16[32,129,128]{2,1,0:T(8,128)(2,1)S(1)}, u32[]{:S(2)}, u32[]{:S(2)}) async-start(bf16[32,129,128]{2,1,0:T(8,128)(2,1)} %bitcast.25), calls=%async_computation.4 | async-start | bytes 2228224 | tf_op jit(solution)/shard_map/all_to_all | solution.py:52
  157.1 29.3 %all-to-all-done.4 = bf16[32,129,128]{2,1,0:T(8,128)(2,1)S(1)} async-done(((bf16[32,129,128]{2,1,0:T(8,128)(2,1)}), bf16[32,129,128]{2,1,0:T(8,128)(2,1)S(1)}, u32[]{:S(2)}, u32[]{:S(2)}) %all-to-all-start.4) | async-done | bytes 1056800 | tf_op jit(solution)/shard_map/all_to_all | solution.py:52
  186.4 2.5 fusion.15
  189.0 10.6 %all_to_all.41 = f32[16,4,512]{2,1,0:T(4,128)S(1)} all-to-all(f32[16,4,512]{2,1,0:T(4,128)S(1)} %reshape.165), channel_id=1, replica_groups=mesh['member'=16,'dp'=32] {'member'}, dimensions={0} | all-to-all | bytes 262144 | tf_op jit(solution)/shard_map/all_to_all | solution.py:68
  199.6 4.7 %collective-permute-start.2 = (f32[16,4,256]{2,0,1:T(8,128)S(1)}, f32[16,4,256]{2,0,1:T(8,128)S(1)}, u32[]{:S(2)}, u32[]{:S(2)}) collective-permute-start(f32[16,4,256]{2,0,1:T(8,128)S(1)} %copy.137), channel_id=1, source_target_pairs={{0,1},{1,0},{2,3},{3,2},{4,5},{5,4},{6,7},{7,6},{8,9},{9,8},{10,11... | collective-permute-start | bytes 196616 | tf_op jit(solution)/shard_map/ppermute | solution.py:44
  204.3 0.9 collective-permute-done.2
  206.3 10.2 %all_to_all.42 = f32[16,1,2048]{2,1,0:T(1,128)S(1)} all-to-all(f32[16,1,2048]{2,1,0:T(1,128)S(1)} %reshape.195), channel_id=1, replica_groups=mesh['member'=16,'dp'=32] {'member'}, dimensions={0} | all-to-all | bytes 262144 | tf_op jit(solution)/shard_map/all_to_all | solution.py:39
  216.5 0.9 reduce.16
  217.8 0.5 reshape.197
  218.3 20.0 %all_to_all.43 = f32[32,1,2048]{2,1,0:T(1,128)S(1)} all-to-all(f32[32,1,2048]{2,1,0:T(1,128)S(1)} %reshape.197), channel_id=1, replica_groups=mesh['member'=16,'dp'=32] {'dp'}, dimensions={0} | all-to-all | bytes 524288 | tf_op jit(solution)/shard_map/all_to_all | solution.py:39
  238.3 1.3 reduce.17
  240.2 2.9 %cholesky.55 = f32[32,32]{1,0:T(8,128)S(1)} custom-call(f32[32,32]{1,0:T(8,128)S(1)} %fusion.47), custom_call_target="Cholesky" | custom-call | tf_op jit(solution)/shard_map/jit(cholesky)/cholesky | solution.py:14
  243.2 0.6 compare_reduce_fusion
  243.8 0.7 fusion.41
  244.5 2.4 custom-call.13
  247.5 1.1 convolution_add_fusion
  248.6 0.6 slice_bitcast_fusion
  249.2 0.6 slice_bitcast_fusion.1
  249.7 0.6 copy.129
  250.4 0.6 copy.130
  (82 shorter events, 5.6 us)
Async XLA Ops:
  7.2 18.0 %copy-start.6 = (bf16[256,64]{0,1:T(8,128)(2,1)S(1)}, bf16[256,64]{0,1:T(8,128)(2,1)}, u32[]{:S(2)}) copy-start(bf16[256,64]{0,1:T(8,128)(2,1)} %param.12) | copy-start | bytes 98308
  7.2 20.2 %copy-start.5 = (f32[2,64]{1,0:T(2,128)S(1)}, f32[2,64]{1,0:T(2,128)}, u32[]{:S(2)}) copy-start(f32[2,64]{1,0:T(2,128)} %param.18) | copy-start | bytes 1540
  10.7 44.0 %all-to-all-start = ((bf16[32,129,128]{2,1,0:T(8,128)(2,1)}), bf16[32,129,128]{2,1,0:T(8,128)(2,1)S(1)}, u32[]{:S(2)}, u32[]{:S(2)}) async-start(bf16[32,129,128]{2,1,0:T(8,128)(2,1)} %bitcast.3), calls=%async_computation | async-start | bytes 2228224 | tf_op jit(solution)/shard_map/all_to_all | solution.py:52
  25.2 29.5 %collective-permute-start = (bf16[256,64]{0,1:T(8,128)(2,1)S(1)}, bf16[256,64]{0,1:T(8,128)(2,1)S(1)}, u32[]{:S(2)}, u32[]{:S(2)}) collective-permute-start(bf16[256,64]{0,1:T(8,128)(2,1)S(1)} %copy-done.6), channel_id=1, source_target_pairs={{0,1},{1,0},{2,3},{3,2},{4,5},{5,4},{6,7},{7,6},{8,9},{9,8},{10,11... | collective-permute-start | bytes 98312 | tf_op jit(solution)/shard_map/ppermute | solution.py:44
  54.7 10.2 %copy-start = (f32[2,64,128]{2,1,0:T(8,128)S(1)}, f32[2,64,128]{2,1,0:T(8,128)}, u32[]{:S(2)}) copy-start(f32[2,64,128]{2,1,0:T(8,128)} %param.17) | copy-start | bytes 196612
  54.7 10.2 %copy-start.1 = (f32[2,64,128]{2,1,0:T(8,128)S(1)}, f32[2,64,128]{2,1,0:T(8,128)}, u32[]{:S(2)}) copy-start(f32[2,64,128]{2,1,0:T(8,128)} %param.15) | copy-start | bytes 196612
  54.7 10.2 %copy-start.4 = (f32[2,128]{1,0:T(2,128)S(1)}, f32[2,128]{1,0:T(2,128)}, u32[]{:S(2)}) copy-start(f32[2,128]{1,0:T(2,128)} %param.16) | copy-start | bytes 3076
  54.7 22.2 %copy-start.2 = (bf16[2,32,4,256]{3,2,1,0:T(4,128)(2,1)S(1)}, bf16[2,32,4,256]{3,2,1,0:T(4,128)(2,1)}, u32[]{:S(2)}) copy-start(bf16[2,32,4,256]{3,2,1,0:T(4,128)(2,1)} %param.14) | copy-start | bytes 393220
  54.8 23.1 %copy-start.3 = (f32[4,256]{1,0:T(4,128)S(1)}, f32[4,256]{1,0:T(4,128)}, u32[]{:S(2)}) copy-start(f32[4,256]{1,0:T(4,128)} %param.13) | copy-start | bytes 12292
  57.9 14.4 %all-to-all-start.1 = ((f32[16,4,512]{2,1,0:T(4,128)}), f32[16,4,512]{2,1,0:T(4,128)S(1)}, u32[]{:S(2)}, u32[]{:S(2)}) async-start(f32[16,4,512]{2,1,0:T(4,128)} %reshape.164), calls=%async_computation.1 | async-start | bytes 262144 | tf_op jit(solution)/shard_map/all_to_all | solution.py:68
  64.9 66.9 %all-gather.2.cloned.1.call-start = ((), (), s32[]{:S(2)}) async-start(), calls=%async_computation.8 | async-start | bytes 2367488 | tf_op jit(solution)/shard_map/all_gather | solution.py:86
  72.3 5.4 %collective-permute-start.1 = (f32[16,4,256]{2,0,1:T(8,128)S(1)}, f32[16,4,256]{2,0,1:T(8,128)S(1)}, u32[]{:S(2)}, u32[]{:S(2)}) collective-permute-start(f32[16,4,256]{2,0,1:T(8,128)S(1)} %copy.133), channel_id=1, source_target_pairs={{0,1},{1,0},{2,3},{3,2},{4,5},{5,4},{6,7},{7,6},{8,9},{9,8},{10,11... | collective-permute-start | bytes 196616 | tf_op jit(solution)/shard_map/ppermute | solution.py:44
  92.8 20.5 %all-to-all-start.3 = ((f32[32,1,2048]{2,1,0:T(1,128)}), f32[32,1,2048]{2,1,0:T(1,128)S(1)}, u32[]{:S(2)}, u32[]{:S(2)}) async-start(f32[32,1,2048]{2,1,0:T(1,128)} %reshape.193), calls=%async_computation.3 | async-start | bytes 524288 | tf_op jit(solution)/shard_map/all_to_all | solution.py:39
  137.5 48.9 %all-to-all-start.4 = ((bf16[32,129,128]{2,1,0:T(8,128)(2,1)}), bf16[32,129,128]{2,1,0:T(8,128)(2,1)S(1)}, u32[]{:S(2)}, u32[]{:S(2)}) async-start(bf16[32,129,128]{2,1,0:T(8,128)(2,1)} %bitcast.25), calls=%async_computation.4 | async-start | bytes 2228224 | tf_op jit(solution)/shard_map/all_to_all | solution.py:52
  199.6 5.6 %collective-permute-start.2 = (f32[16,4,256]{2,0,1:T(8,128)S(1)}, f32[16,4,256]{2,0,1:T(8,128)S(1)}, u32[]{:S(2)}, u32[]{:S(2)}) collective-permute-start(f32[16,4,256]{2,0,1:T(8,128)S(1)} %copy.137), channel_id=1, source_target_pairs={{0,1},{1,0},{2,3},{3,2},{4,5},{5,4},{6,7},{7,6},{8,9},{9,8},{10,11... | collective-permute-start | bytes 196616 | tf_op jit(solution)/shard_map/ppermute | solution.py:44
Sparse Core Ops, SparseCore 0:
  67.8 63.9 all-gather.1

commit v4 on v3

--- a/solution.py
+++ b/solution.py
@@ -98,7 +98,10 @@
         cross_part = lax.dot_general(
             anomaly, misfit, (((1,), (1,)), ((), ())), precision=lax.Precision.HIGHEST
         )
-        sums = gather_sum(gather_sum(jnp.stack([gram_part, cross_part]), "member"), "dp")
+        sums = gather_sum(jnp.stack([gram_part, cross_part]), "member")
+        if update == 0:
+            sums = sums + whole[0, 0, 0] * 0
+        sums = gather_sum(sums, "dp")
         gain = solve_gain(sums[0] / count, sums[1] / count)
         if update + 1 < UPDATES:
             moved = jnp.einsum("kj,kab->jab", gain, whole, precision=lax.Precision.HIGHEST)

time: 259 us -> 253 us (0.977)
  blocking collectives: 51.7 us -> 65.6 us
  waiting for transfers between devices: 87.3 us -> 75 us
  starting transfers between devices: 59.9 us -> 50.9 us
    all_to_all x2, starting transfers between devices: 34 us -> 18.6 us  [predict(): got = lax.all_to_all(tiles, 'dp', split_axis=0, concat_axis=0, tiled=True)]
    all_to_all x1 -> x2, blocking collectives: 10.6 us -> 24.5 us  [collect(): lax.all_to_all(blocks, 'member', split_axis=0, concat_axis=0, tiled=True)]
    all_to_all x1, starting transfers between devices: 7.51 us -> 20.4 us  [gather_sum(): lax.all_to_all(tiles, axis, split_axis=0, concat_axis=0, tiled=True)]
    all_to_all x1 -> x0, starting transfers between devices: 6.95 us -> none  [collect(): lax.all_to_all(blocks, 'member', split_axis=0, concat_axis=0, tiled=True)]
    all_to_all x1 -> x0, waiting for transfers between devices: 6.65 us -> none  [collect(): lax.all_to_all(blocks, 'member', split_axis=0, concat_axis=0, tiled=True)]
    all_gather x1, waiting for transfers between devices: 9.42 us -> 4.46 us  [on_device(): whole = lax.all_gather(own, 'member', axis=0, tiled=True)]
  transfers between devices with their start and end apart: 8 -> 7, of which waited for: 7 -> 6; matrix products, arithmetic and copies ran while one was open for 5% -> 2% of each run, Pallas kernels for 0% -> 0%
where the time goes in v4:
time: 253 us; the launch traced here: 252 us
  waiting for transfers between devices  75 us (30%)
  blocking collectives  65.6 us (26%)
  starting transfers between devices  50.9 us (20%)
  other arithmetic  21.5 us (8%)
  between operations  15.3 us (6%)
  matrix products  12.4 us (5%)
  local copies, waits for them, and re-layouts  10.9 us (4%)
    all_to_all x2, waiting for transfers between devices, predict(): got = lax.all_to_all(tiles, 'dp', split_axis=0, concat_axis=0, tiled=True)  55.9 us
    all_to_all x3, blocking collectives, gather_sum(): lax.all_to_all(tiles, axis, split_axis=0, concat_axis=0, tiled=True)  41.1 us
    all_to_all x2, blocking collectives, collect(): lax.all_to_all(blocks, 'member', split_axis=0, concat_axis=0, tiled=True)  24.5 us
    all_to_all x1, starting transfers between devices, gather_sum(): lax.all_to_all(tiles, axis, split_axis=0, concat_axis=0, tiled=True)  20.4 us
    all_to_all x2, starting transfers between devices, predict(): got = lax.all_to_all(tiles, 'dp', split_axis=0, concat_axis=0, tiled=True)  18.6 us
    all_to_all x1, waiting for transfers between devices, gather_sum(): lax.all_to_all(tiles, axis, split_axis=0, concat_axis=0, tiled=True)  12.9 us
    ppermute x3, starting transfers between devices, swap_pair(): return lax.ppermute(x, 'dp', [(i, i ^ 1) for i in range(n)])  11.9 us
    another operation x6, other arithmetic, solve_gain(): factor = jnp.linalg.cholesky(gram + ridge_level * eye)  7.18 us
  transfers between devices with their start and end apart: 7, of which 6 were waited for; matrix products, arithmetic and copies ran while one was open for 2% of the time, Pallas kernels for 0%

profile of v4, /device:TPU:1, one launch (start us, length us, event | category | flops | bytes accessed | tf_op | source)
XLA Modules:
  0.0 251.7 jit_solution(3884905179462617494)
XLA Ops:
  7.2 0.7 convert.18
  8.0 0.8 convert.16
  8.8 0.8 convert.17
  9.7 1.1 tile.8
  10.8 14.4 %all-to-all-start = ((bf16[32,129,128]{2,1,0:T(8,128)(2,1)}), bf16[32,129,128]{2,1,0:T(8,128)(2,1)S(1)}, u32[]{:S(2)}, u32[]{:S(2)}) async-start(bf16[32,129,128]{2,1,0:T(8,128)(2,1)} %bitcast.3), calls=%async_computation | async-start | bytes 2228224 | tf_op jit(solution)/shard_map/all_to_all | solution.py:52
  25.3 0.7 pad_maximum_fusion
  26.0 2.1 collective-permute-start
  28.2 26.6 %all-to-all-done = bf16[32,129,128]{2,1,0:T(8,128)(2,1)S(1)} async-done(((bf16[32,129,128]{2,1,0:T(8,128)(2,1)}), bf16[32,129,128]{2,1,0:T(8,128)(2,1)S(1)}, u32[]{:S(2)}, u32[]{:S(2)}) %all-to-all-start) | async-done | bytes 1056800 | tf_op jit(solution)/shard_map/all_to_all | solution.py:52
  54.8 2.5 fusion.14
  57.3 14.2 %all_to_all.40 = f32[16,4,512]{2,1,0:T(4,128)S(1)} all-to-all(f32[16,4,512]{2,1,0:T(4,128)S(1)} %reshape.168), channel_id=1, replica_groups=mesh['member'=16,'dp'=32] {'member'}, dimensions={0} | all-to-all | bytes 262144 | tf_op jit(solution)/shard_map/all_to_all | solution.py:68
  71.6 5.1 %collective-permute-start.1 = (f32[16,4,256]{2,0,1:T(8,128)S(1)}, f32[16,4,256]{2,0,1:T(8,128)S(1)}, u32[]{:S(2)}, u32[]{:S(2)}) collective-permute-start(f32[16,4,256]{2,0,1:T(8,128)S(1)} %copy.133), channel_id=1, source_target_pairs={{0,1},{1,0},{2,3},{3,2},{4,5},{5,4},{6,7},{7,6},{8,9},{9,8},{10,11... | collective-permute-start | bytes 196616 | tf_op jit(solution)/shard_map/ppermute | solution.py:44
  76.8 0.8 collective-permute-done.1
  78.7 11.0 %all_to_all.41 = f32[16,1,2048]{2,1,0:T(1,128)S(1)} all-to-all(f32[16,1,2048]{2,1,0:T(1,128)S(1)} %reshape.195), channel_id=1, replica_groups=mesh['member'=16,'dp'=32] {'member'}, dimensions={0} | all-to-all | bytes 262144 | tf_op jit(solution)/shard_map/all_to_all | solution.py:39
  89.8 0.5 broadcast.181
  90.3 0.9 reduce.14
  91.5 4.5 %all-gather.2.cloned.1.call-done = f32[32,130,128]{2,1,0:T(8,128)} async-done(((f32[2,130,128]{2,1,0:T(8,128)}), f32[32,130,128]{2,1,0:T(8,128)}) %all-gather.2.cloned.1.call-update) | async-done | bytes 2129936 | tf_op jit(solution)/shard_map/all_gather | solution.py:86
  95.9 1.2 slice.120
  97.9 1.2 reshape.197
  99.1 20.4 %all-to-all-start.3 = ((f32[32,1,2048]{2,1,0:T(1,128)}), f32[32,1,2048]{2,1,0:T(1,128)S(1)}, u32[]{:S(2)}, u32[]{:S(2)}) async-start(f32[32,1,2048]{2,1,0:T(1,128)} %reshape.197), calls=%async_computation.3 | async-start | bytes 524288 | tf_op jit(solution)/shard_map/all_to_all | solution.py:39
  119.5 12.9 %all-to-all-done.3 = f32[32,1,2048]{2,1,0:T(1,128)S(1)} async-done(((f32[32,1,2048]{2,1,0:T(1,128)}), f32[32,1,2048]{2,1,0:T(1,128)S(1)}, u32[]{:S(2)}, u32[]{:S(2)}) %all-to-all-start.3) | async-done | bytes 262176 | tf_op jit(solution)/shard_map/all_to_all | solution.py:39
  132.4 1.3 reduce.15
  134.3 2.9 %cholesky.44 = f32[32,32]{1,0:T(8,128)S(1)} custom-call(f32[32,32]{1,0:T(8,128)S(1)} %fusion.52), custom_call_target="Cholesky" | custom-call | tf_op jit(solution)/shard_map/jit(cholesky)/cholesky | solution.py:14
  137.2 0.6 compare_reduce_fusion.1
  137.9 0.7 fusion.40
  138.5 2.4 custom-call.11
  141.5 4.5 %copy_add_fusion = f32[32,130,128]{2,0,1:T(8,128)S(1)} fusion(f32[32,130,128]{2,1,0:T(8,128)} %all-gather.2.cloned.1.call-done, f32[32,32,1]{0,1,2:T(8,128)S(1)} %convolution_bitcast_fusion.2), kind=kOutput, calls=%fused_computation.10 | convolution fusion | flops 205004800 | bytes 4263936 | tf_op jit(solution)/shard_map/kj,kab->jab/dot_general | solution.py:107
  146.1 1.1 tile.20
  147.3 4.1 %all-to-all-start.4 = ((bf16[32,129,128]{2,1,0:T(8,128)(2,1)}), bf16[32,129,128]{2,1,0:T(8,128)(2,1)S(1)}, u32[]{:S(2)}, u32[]{:S(2)}) async-start(bf16[32,129,128]{2,1,0:T(8,128)(2,1)} %bitcast.26), calls=%async_computation.4 | async-start | bytes 2228224 | tf_op jit(solution)/shard_map/all_to_all | solution.py:52
  151.4 29.3 %all-to-all-done.4 = bf16[32,129,128]{2,1,0:T(8,128)(2,1)S(1)} async-done(((bf16[32,129,128]{2,1,0:T(8,128)(2,1)}), bf16[32,129,128]{2,1,0:T(8,128)(2,1)S(1)}, u32[]{:S(2)}, u32[]{:S(2)}) %all-to-all-start.4) | async-done | bytes 1056800 | tf_op jit(solution)/shard_map/all_to_all | solution.py:52
  180.8 2.5 fusion.15
  183.3 10.3 %all_to_all.42 = f32[16,4,512]{2,1,0:T(4,128)S(1)} all-to-all(f32[16,4,512]{2,1,0:T(4,128)S(1)} %reshape.169), channel_id=1, replica_groups=mesh['member'=16,'dp'=32] {'member'}, dimensions={0} | all-to-all | bytes 262144 | tf_op jit(solution)/shard_map/all_to_all | solution.py:68
  193.6 4.7 %collective-permute-start.2 = (f32[16,4,256]{2,0,1:T(8,128)S(1)}, f32[16,4,256]{2,0,1:T(8,128)S(1)}, u32[]{:S(2)}, u32[]{:S(2)}) collective-permute-start(f32[16,4,256]{2,0,1:T(8,128)S(1)} %copy.137), channel_id=1, source_target_pairs={{0,1},{1,0},{2,3},{3,2},{4,5},{5,4},{6,7},{7,6},{8,9},{9,8},{10,11... | collective-permute-start | bytes 196616 | tf_op jit(solution)/shard_map/ppermute | solution.py:44
  198.4 0.9 collective-permute-done.2
  200.4 10.2 %all_to_all.43 = f32[16,1,2048]{2,1,0:T(1,128)S(1)} all-to-all(f32[16,1,2048]{2,1,0:T(1,128)S(1)} %reshape.199), channel_id=1, replica_groups=mesh['member'=16,'dp'=32] {'member'}, dimensions={0} | all-to-all | bytes 262144 | tf_op jit(solution)/shard_map/all_to_all | solution.py:39
  210.6 0.9 reduce.16
  211.9 0.5 reshape.201
  212.4 19.9 %all_to_all.44 = f32[32,1,2048]{2,1,0:T(1,128)S(1)} all-to-all(f32[32,1,2048]{2,1,0:T(1,128)S(1)} %reshape.201), channel_id=1, replica_groups=mesh['member'=16,'dp'=32] {'dp'}, dimensions={0} | all-to-all | bytes 524288 | tf_op jit(solution)/shard_map/all_to_all | solution.py:39
  232.2 1.3 reduce.17
  233.5 0.3 reshape.202
  234.1 2.9 %cholesky.55 = f32[32,32]{1,0:T(8,128)S(1)} custom-call(f32[32,32]{1,0:T(8,128)S(1)} %fusion.47), custom_call_target="Cholesky" | custom-call | tf_op jit(solution)/shard_map/jit(cholesky)/cholesky | solution.py:14
  237.1 0.6 compare_reduce_fusion
  237.7 0.7 fusion.41
  238.4 2.4 custom-call.13
  241.4 1.1 convolution_add_fusion
  242.5 0.6 slice_bitcast_fusion
  243.1 0.6 slice_bitcast_fusion.1
  243.6 0.6 copy.129
  244.3 0.6 copy.130
  (83 shorter events, 5.3 us)
Async XLA Ops:
  7.2 18.2 %copy-start.4 = (f32[2,128]{1,0:T(2,128)S(1)}, f32[2,128]{1,0:T(2,128)}, u32[]{:S(2)}) copy-start(f32[2,128]{1,0:T(2,128)} %param.16) | copy-start | bytes 3076
  7.2 18.2 %copy-start.1 = (f32[2,64,128]{2,1,0:T(8,128)S(1)}, f32[2,64,128]{2,1,0:T(8,128)}, u32[]{:S(2)}) copy-start(f32[2,64,128]{2,1,0:T(8,128)} %param.15) | copy-start | bytes 196612
  7.2 18.2 %copy-start = (f32[2,64,128]{2,1,0:T(8,128)S(1)}, f32[2,64,128]{2,1,0:T(8,128)}, u32[]{:S(2)}) copy-start(f32[2,64,128]{2,1,0:T(8,128)} %param.17) | copy-start | bytes 196612
  7.2 18.1 %copy-start.5 = (f32[2,64]{1,0:T(2,128)S(1)}, f32[2,64]{1,0:T(2,128)}, u32[]{:S(2)}) copy-start(f32[2,64]{1,0:T(2,128)} %param.18) | copy-start | bytes 1540
  7.2 18.8 %copy-start.6 = (bf16[256,64]{0,1:T(8,128)(2,1)S(1)}, bf16[256,64]{0,1:T(8,128)(2,1)}, u32[]{:S(2)}) copy-start(bf16[256,64]{0,1:T(8,128)(2,1)} %param.12) | copy-start | bytes 98308
  10.8 44.0 %all-to-all-start = ((bf16[32,129,128]{2,1,0:T(8,128)(2,1)}), bf16[32,129,128]{2,1,0:T(8,128)(2,1)S(1)}, u32[]{:S(2)}, u32[]{:S(2)}) async-start(bf16[32,129,128]{2,1,0:T(8,128)(2,1)} %bitcast.3), calls=%async_computation | async-start | bytes 2228224 | tf_op jit(solution)/shard_map/all_to_all | solution.py:52
  25.2 70.7 %all-gather.2.cloned.1.call-start = ((), (), s32[]{:S(2)}) async-start(), calls=%async_computation.8 | async-start | bytes 2367488 | tf_op jit(solution)/shard_map/all_gather | solution.py:86
  26.0 28.8 %collective-permute-start = (bf16[256,64]{0,1:T(8,128)(2,1)S(1)}, bf16[256,64]{0,1:T(8,128)(2,1)S(1)}, u32[]{:S(2)}, u32[]{:S(2)}) collective-permute-start(bf16[256,64]{0,1:T(8,128)(2,1)S(1)} %copy-done.6), channel_id=1, source_target_pairs={{0,1},{1,0},{2,3},{3,2},{4,5},{5,4},{6,7},{7,6},{8,9},{9,8},{10,11... | collective-permute-start | bytes 98312 | tf_op jit(solution)/shard_map/ppermute | solution.py:44
  54.8 21.9 %copy-start.2 = (bf16[2,32,4,256]{3,2,1,0:T(4,128)(2,1)S(1)}, bf16[2,32,4,256]{3,2,1,0:T(4,128)(2,1)}, u32[]{:S(2)}) copy-start(bf16[2,32,4,256]{3,2,1,0:T(4,128)(2,1)} %param.14) | copy-start | bytes 393220
  54.8 22.8 %copy-start.3 = (f32[4,256]{1,0:T(4,128)S(1)}, f32[4,256]{1,0:T(4,128)}, u32[]{:S(2)}) copy-start(f32[4,256]{1,0:T(4,128)} %param.13) | copy-start | bytes 12292
  71.6 6.0 %collective-permute-start.1 = (f32[16,4,256]{2,0,1:T(8,128)S(1)}, f32[16,4,256]{2,0,1:T(8,128)S(1)}, u32[]{:S(2)}, u32[]{:S(2)}) collective-permute-start(f32[16,4,256]{2,0,1:T(8,128)S(1)} %copy.133), channel_id=1, source_target_pairs={{0,1},{1,0},{2,3},{3,2},{4,5},{5,4},{6,7},{7,6},{8,9},{9,8},{10,11... | collective-permute-start | bytes 196616 | tf_op jit(solution)/shard_map/ppermute | solution.py:44
  99.1 33.3 %all-to-all-start.3 = ((f32[32,1,2048]{2,1,0:T(1,128)}), f32[32,1,2048]{2,1,0:T(1,128)S(1)}, u32[]{:S(2)}, u32[]{:S(2)}) async-start(f32[32,1,2048]{2,1,0:T(1,128)} %reshape.197), calls=%async_computation.3 | async-start | bytes 524288 | tf_op jit(solution)/shard_map/all_to_all | solution.py:39
  147.3 33.5 %all-to-all-start.4 = ((bf16[32,129,128]{2,1,0:T(8,128)(2,1)}), bf16[32,129,128]{2,1,0:T(8,128)(2,1)S(1)}, u32[]{:S(2)}, u32[]{:S(2)}) async-start(bf16[32,129,128]{2,1,0:T(8,128)(2,1)} %bitcast.26), calls=%async_computation.4 | async-start | bytes 2228224 | tf_op jit(solution)/shard_map/all_to_all | solution.py:52
  193.6 5.6 %collective-permute-start.2 = (f32[16,4,256]{2,0,1:T(8,128)S(1)}, f32[16,4,256]{2,0,1:T(8,128)S(1)}, u32[]{:S(2)}, u32[]{:S(2)}) collective-permute-start(f32[16,4,256]{2,0,1:T(8,128)S(1)} %copy.137), channel_id=1, source_target_pairs={{0,1},{1,0},{2,3},{3,2},{4,5},{5,4},{6,7},{7,6},{8,9},{9,8},{10,11... | collective-permute-start | bytes 196616 | tf_op jit(solution)/shard_map/ppermute | solution.py:44
Sparse Core Ops, SparseCore 0:
  28.2 67.7 all-gather.1

commit v5 on v4

--- a/solution.py
+++ b/solution.py
@@ -48,7 +48,8 @@
     n_dp = lax.axis_size("dp")
     rows = f_in + outs + 1
     rounded = own_flat[:, :rows, :].astype(jnp.bfloat16)
-    tiles = jnp.tile(rounded, (n_dp // rounded.shape[0], 1, 1))
+    n = rounded.shape[0]
+    tiles = jnp.broadcast_to(rounded[None], (n_dp // n,) + rounded.shape).reshape((n_dp,) + rounded.shape[1:])
     got = lax.all_to_all(tiles, "dp", split_axis=0, concat_axis=0, tiled=True)
     w_in = got[:, :f_in, :]
     w_out = got[:, f_in : f_in + outs, :]
@@ -84,6 +85,7 @@
     inputs_pair = jnp.concatenate([inputs, swap_pair(inputs)], axis=0)
     own = pack(w_in, b_in, w_out, b_out)
     whole = lax.all_gather(own, "member", axis=0, tiled=True)
+    assert UPDATES == 2
     for update in range(UPDATES):
         predicted = predict(inputs_pair, own, f_in, hid, outs, parity)
         collected = collect(predicted, n_samples, parity)
@@ -103,14 +105,15 @@
             sums = sums + whole[0, 0, 0] * 0
         sums = gather_sum(sums, "dp")
         gain = solve_gain(sums[0] / count, sums[1] / count)
-        if update + 1 < UPDATES:
-            moved = jnp.einsum("kj,kab->jab", gain, whole, precision=lax.Precision.HIGHEST)
-            whole = whole + moved
-            own = lax.dynamic_slice_in_dim(whole, first, per_device, 0)
+        if update == 0:
+            first_gain = gain
+            columns = lax.dynamic_slice_in_dim(gain, first, per_device, 1)
+            own = own + jnp.einsum("kj,kab->jab", columns, whole, precision=lax.Precision.HIGHEST)
         else:
-            columns = lax.dynamic_slice_in_dim(gain, first, per_device, 1)
-            moved = jnp.einsum("kj,kab->jab", columns, whole, precision=lax.Precision.HIGHEST)
-            own = own + moved
+            eye = jnp.eye(gain.shape[0], dtype=gain.dtype)
+            through = jnp.dot(eye + first_gain, gain, precision=lax.Precision.HIGHEST)
+            columns = lax.dynamic_slice_in_dim(through, first, per_device, 1)
+            own = own + jnp.einsum("kj,kab->jab", columns, whole, precision=lax.Precision.HIGHEST)
     return unpack(own, f_in, hid, outs)
 
 

time: 253 us -> 255 us (level)
  local copies, waits for them, and re-layouts: 10.9 us -> 13.8 us
    dot_general x1, matrix products: 4.5 us -> 0.21 us  [on_device(): through = jnp.dot(eye + first_gain, gain, precision=lax.Precision.HIGHEST)]
    dot_general x1 -> x2, matrix products: 1.11 us -> 4.47 us  [on_device(): jnp.einsum('kj,kab->jab', columns, whole, precision=lax.Precision.HIGHEST)]
    unnamed x30 -> x48, local copies, waits for them, and re-layouts: 4.74 us -> 5.43 us
  transfers between devices with their start and end apart: 7 -> 7, of which waited for: 6 -> 6; matrix products, arithmetic and copies ran while one was open for 2% -> 3% of each run, Pallas kernels for 0% -> 0%
where the time goes in v5:
time: 255 us; the launch traced here: 254 us
  waiting for transfers between devices  73.6 us (29%)
  blocking collectives  65.9 us (26%)
  starting transfers between devices  50.7 us (20%)
  other arithmetic  21.5 us (8%)
  between operations  15.4 us (6%)
  local copies, waits for them, and re-layouts  13.8 us (5%)
  matrix products  12.9 us (5%)
    all_to_all x2, waiting for transfers between devices, predict(): got = lax.all_to_all(tiles, 'dp', split_axis=0, concat_axis=0, tiled=True)  55.2 us
    all_to_all x3, blocking collectives, gather_sum(): lax.all_to_all(tiles, axis, split_axis=0, concat_axis=0, tiled=True)  40.8 us
    all_to_all x2, blocking collectives, collect(): lax.all_to_all(blocks, 'member', split_axis=0, concat_axis=0, tiled=True)  25.1 us
    all_to_all x1, starting transfers between devices, gather_sum(): lax.all_to_all(tiles, axis, split_axis=0, concat_axis=0, tiled=True)  20.1 us
    all_to_all x2, starting transfers between devices, predict(): got = lax.all_to_all(tiles, 'dp', split_axis=0, concat_axis=0, tiled=True)  18.6 us
    all_to_all x1, waiting for transfers between devices, gather_sum(): lax.all_to_all(tiles, axis, split_axis=0, concat_axis=0, tiled=True)  12.9 us
    ppermute x3, starting transfers between devices, swap_pair(): return lax.ppermute(x, 'dp', [(i, i ^ 1) for i in range(n)])  11.9 us
    another operation x6, other arithmetic, solve_gain(): factor = jnp.linalg.cholesky(gram + ridge_level * eye)  7.18 us
  transfers between devices with their start and end apart: 7, of which 6 were waited for; matrix products, arithmetic and copies ran while one was open for 3% of the time, Pallas kernels for 0%

profile of v5, /device:TPU:1, one launch (start us, length us, event | category | flops | bytes accessed | tf_op | source)
XLA Modules:
  0.0 253.7 jit_solution(15658817216880809875)
XLA Ops:
  7.2 0.9 convert.16
  8.1 0.8 convert.17
  8.9 0.7 bitcast_convert_fusion
  9.7 1.1 broadcast_in_dim.18
  10.8 14.4 %all-to-all-start = ((bf16[32,129,128]{2,1,0:T(8,128)(2,1)}), bf16[32,129,128]{2,1,0:T(8,128)(2,1)S(1)}, u32[]{:S(2)}, u32[]{:S(2)}) async-start(bf16[32,129,128]{2,1,0:T(8,128)(2,1)} %bitcast.2), calls=%async_computation | async-start | bytes 2228224 | tf_op jit(solution)/shard_map/all_to_all | solution.py:53
  25.5 0.5 copy-done.2
  26.1 0.7 copy.121
  26.8 2.1 collective-permute-start
  29.0 25.8 %all-to-all-done = bf16[32,129,128]{2,1,0:T(8,128)(2,1)S(1)} async-done(((bf16[32,129,128]{2,1,0:T(8,128)(2,1)}), bf16[32,129,128]{2,1,0:T(8,128)(2,1)S(1)}, u32[]{:S(2)}, u32[]{:S(2)}) %all-to-all-start) | async-done | bytes 1056800 | tf_op jit(solution)/shard_map/all_to_all | solution.py:53
  54.8 2.5 fusion.20
  57.3 14.2 %all_to_all.40 = f32[16,4,512]{2,1,0:T(4,128)S(1)} all-to-all(f32[16,4,512]{2,1,0:T(4,128)S(1)} %reshape.169), channel_id=1, replica_groups=mesh['member'=16,'dp'=32] {'member'}, dimensions={0} | all-to-all | bytes 262144 | tf_op jit(solution)/shard_map/all_to_all | solution.py:69
  71.6 5.1 %collective-permute-start.1 = (f32[16,4,256]{2,0,1:T(8,128)S(1)}, f32[16,4,256]{2,0,1:T(8,128)S(1)}, u32[]{:S(2)}, u32[]{:S(2)}) collective-permute-start(f32[16,4,256]{2,0,1:T(8,128)S(1)} %copy.143), channel_id=1, source_target_pairs={{0,1},{1,0},{2,3},{3,2},{4,5},{5,4},{6,7},{7,6},{8,9},{9,8},{10,11... | collective-permute-start | bytes 196616 | tf_op jit(solution)/shard_map/ppermute | solution.py:44
  76.7 0.7 fusion.83
  78.7 11.1 %all_to_all.41 = f32[16,1,2048]{2,1,0:T(1,128)S(1)} all-to-all(f32[16,1,2048]{2,1,0:T(1,128)S(1)} %reshape.197), channel_id=1, replica_groups=mesh['member'=16,'dp'=32] {'member'}, dimensions={0} | all-to-all | bytes 262144 | tf_op jit(solution)/shard_map/all_to_all | solution.py:39
  90.3 1.0 reduce.14
  91.5 4.4 %all-gather.2.cloned.1.call-done = f32[32,130,128]{2,1,0:T(8,128)} async-done(((f32[2,130,128]{2,1,0:T(8,128)}), f32[32,130,128]{2,1,0:T(8,128)}) %all-gather.2.cloned.1.call-update) | async-done | bytes 2129936 | tf_op jit(solution)/shard_map/all_gather | solution.py:87
  95.9 1.2 slice.120
  97.9 1.2 reshape.199
  99.1 20.1 %all-to-all-start.3 = ((f32[32,1,2048]{2,1,0:T(1,128)}), f32[32,1,2048]{2,1,0:T(1,128)S(1)}, u32[]{:S(2)}, u32[]{:S(2)}) async-start(f32[32,1,2048]{2,1,0:T(1,128)} %reshape.199), calls=%async_computation.3 | async-start | bytes 524288 | tf_op jit(solution)/shard_map/all_to_all | solution.py:39
  119.2 12.9 %all-to-all-done.3 = f32[32,1,2048]{2,1,0:T(1,128)S(1)} async-done(((f32[32,1,2048]{2,1,0:T(1,128)}), f32[32,1,2048]{2,1,0:T(1,128)S(1)}, u32[]{:S(2)}, u32[]{:S(2)}) %all-to-all-start.3) | async-done | bytes 262176 | tf_op jit(solution)/shard_map/all_to_all | solution.py:39
  132.1 1.3 reduce.15
  134.0 2.9 %cholesky.44 = f32[32,32]{1,0:T(8,128)S(1)} custom-call(f32[32,32]{1,0:T(8,128)S(1)} %fusion.59), custom_call_target="Cholesky" | custom-call | tf_op jit(solution)/shard_map/jit(cholesky)/cholesky | solution.py:14
  137.0 0.6 compare_reduce_fusion.1
  137.6 0.7 fusion.46
  138.3 2.4 custom-call.11
  141.2 2.2 fusion.12
  143.6 1.1 broadcast_in_dim.22
  144.7 4.1 %all-to-all-start.4 = ((bf16[32,129,128]{2,1,0:T(8,128)(2,1)}), bf16[32,129,128]{2,1,0:T(8,128)(2,1)S(1)}, u32[]{:S(2)}, u32[]{:S(2)}) async-start(bf16[32,129,128]{2,1,0:T(8,128)(2,1)} %bitcast.25), calls=%async_computation.4 | async-start | bytes 2228224 | tf_op jit(solution)/shard_map/all_to_all | solution.py:53
  148.9 29.4 %all-to-all-done.4 = bf16[32,129,128]{2,1,0:T(8,128)(2,1)S(1)} async-done(((bf16[32,129,128]{2,1,0:T(8,128)(2,1)}), bf16[32,129,128]{2,1,0:T(8,128)(2,1)S(1)}, u32[]{:S(2)}, u32[]{:S(2)}) %all-to-all-start.4) | async-done | bytes 1056800 | tf_op jit(solution)/shard_map/all_to_all | solution.py:53
  178.2 0.6 slice_convert_fusion.1
  178.8 3.9 %fusion.21 = f32[64,512]{1,0:T(8,128)} fusion(f32[32,128]{1,0:T(8,128)} %bitcast.117, bf16[32,129,128]{2,1,0:T(8,128)(2,1)S(1)} %all-to-all-done.4, f32[64]{0:T(128)S(1)} %fusion.72, bf16[256,64]{0,1:T(8,128)(2,1)} %copy-done.14, bf16[256,64]{0,1:T(8,128)(2,1)} %param.12), kind=kOutput, calls=%fused_computation.17 | convolution fusion | flops 541229056 | bytes 1262080 | tf_op jit(solution)/shard_map/doh,sdh->os/dot_general | solution.py:61
  182.7 0.9 reshape.171
  183.7 10.9 %all_to_all.42 = f32[16,4,512]{2,1,0:T(4,128)S(1)} all-to-all(f32[16,4,512]{2,1,0:T(4,128)S(1)} %reshape.171), channel_id=1, replica_groups=mesh['member'=16,'dp'=32] {'member'}, dimensions={0} | all-to-all | bytes 262144 | tf_op jit(solution)/shard_map/all_to_all | solution.py:69
  194.7 4.7 %collective-permute-start.2 = (f32[16,4,256]{2,0,1:T(8,128)S(1)}, f32[16,4,256]{2,0,1:T(8,128)S(1)}, u32[]{:S(2)}, u32[]{:S(2)}) collective-permute-start(f32[16,4,256]{2,0,1:T(8,128)S(1)} %copy.147), channel_id=1, source_target_pairs={{0,1},{1,0},{2,3},{3,2},{4,5},{5,4},{6,7},{7,6},{8,9},{9,8},{10,11... | collective-permute-start | bytes 196616 | tf_op jit(solution)/shard_map/ppermute | solution.py:44
  199.4 0.9 collective-permute-done.2
  201.4 10.2 %all_to_all.43 = f32[16,1,2048]{2,1,0:T(1,128)S(1)} all-to-all(f32[16,1,2048]{2,1,0:T(1,128)S(1)} %reshape.201), channel_id=1, replica_groups=mesh['member'=16,'dp'=32] {'member'}, dimensions={0} | all-to-all | bytes 262144 | tf_op jit(solution)/shard_map/all_to_all | solution.py:39
  211.6 0.9 reduce.16
  213.4 19.5 %all_to_all.44 = f32[32,1,2048]{2,1,0:T(1,128)S(1)} all-to-all(f32[32,1,2048]{2,1,0:T(1,128)S(1)} %reshape.203), channel_id=1, replica_groups=mesh['member'=16,'dp'=32] {'dp'}, dimensions={0} | all-to-all | bytes 524288 | tf_op jit(solution)/shard_map/all_to_all | solution.py:39
  232.9 1.3 reduce.17
  234.8 2.9 %cholesky.55 = f32[32,32]{1,0:T(8,128)S(1)} custom-call(f32[32,32]{1,0:T(8,128)S(1)} %fusion.53), custom_call_target="Cholesky" | custom-call | tf_op jit(solution)/shard_map/jit(cholesky)/cholesky | solution.py:14
  237.8 0.6 compare_reduce_fusion
  238.4 0.7 fusion.47
  239.1 2.4 custom-call.13
  242.2 2.3 fusion.15
  244.5 0.6 slice_bitcast_fusion
  245.1 0.6 slice_bitcast_fusion.1
  245.6 0.6 copy.140
  246.3 0.6 copy.141
  (104 shorter events, 7.0 us)
Async XLA Ops:
  7.2 18.1 %copy-start.4 = (f32[2,64,128]{2,1,0:T(8,128)S(1)}, f32[2,64,128]{2,1,0:T(8,128)}, u32[]{:S(2)}) copy-start(f32[2,64,128]{2,1,0:T(8,128)} %param.15) | copy-start | bytes 196612
  7.2 18.2 %copy-start.5 = (f32[2,64,128]{2,1,0:T(8,128)S(1)}, f32[2,64,128]{2,1,0:T(8,128)}, u32[]{:S(2)}) copy-start(f32[2,64,128]{2,1,0:T(8,128)} %param.17) | copy-start | bytes 196612
  7.2 18.8 %copy-start.11 = (f32[2,128]{1,0:T(2,128)S(1)}, f32[2,128]{1,0:T(2,128)}, u32[]{:S(2)}) copy-start(f32[2,128]{1,0:T(2,128)} %param.16) | copy-start | bytes 3076
  7.2 18.3 %copy-start.12 = (f32[2,64]{1,0:T(2,128)S(1)}, f32[2,64]{1,0:T(2,128)}, u32[]{:S(2)}) copy-start(f32[2,64]{1,0:T(2,128)} %param.18) | copy-start | bytes 1540
  9.6 17.1 %copy-start.13 = (bf16[256,64]{0,1:T(8,128)(2,1)S(1)}, bf16[256,64]{0,1:T(8,128)(2,1)}, u32[]{:S(2)}) copy-start(bf16[256,64]{0,1:T(8,128)(2,1)} %param.12) | copy-start | bytes 98308
  10.8 44.0 %all-to-all-start = ((bf16[32,129,128]{2,1,0:T(8,128)(2,1)}), bf16[32,129,128]{2,1,0:T(8,128)(2,1)S(1)}, u32[]{:S(2)}, u32[]{:S(2)}) async-start(bf16[32,129,128]{2,1,0:T(8,128)(2,1)} %bitcast.2), calls=%async_computation | async-start | bytes 2228224 | tf_op jit(solution)/shard_map/all_to_all | solution.py:53
  25.2 70.7 %all-gather.2.cloned.1.call-start = ((), (), s32[]{:S(2)}) async-start(), calls=%async_computation.8 | async-start | bytes 2367488 | tf_op jit(solution)/shard_map/all_gather | solution.py:87
  25.4 0.6 copy-start.2
  25.5 0.6 copy-start.3
  26.8 28.0 %collective-permute-start = (bf16[256,64]{0,1:T(8,128)(2,1)S(1)}, bf16[256,64]{0,1:T(8,128)(2,1)S(1)}, u32[]{:S(2)}, u32[]{:S(2)}) collective-permute-start(bf16[256,64]{0,1:T(8,128)(2,1)S(1)} %copy-done.13), channel_id=1, source_target_pairs={{0,1},{1,0},{2,3},{3,2},{4,5},{5,4},{6,7},{7,6},{8,9},{9,8},{10,11... | collective-permute-start | bytes 98312 | tf_op jit(solution)/shard_map/ppermute | solution.py:44
  54.8 2.5 copy-start.14
  54.8 21.9 %copy-start.7 = (bf16[2,32,4,256]{3,2,1,0:T(4,128)(2,1)S(1)}, bf16[2,32,4,256]{3,2,1,0:T(4,128)(2,1)}, u32[]{:S(2)}) copy-start(bf16[2,32,4,256]{3,2,1,0:T(4,128)(2,1)} %param.14) | copy-start | bytes 393220
  54.8 22.8 %copy-start.10 = (f32[4,256]{1,0:T(4,128)S(1)}, f32[4,256]{1,0:T(4,128)}, u32[]{:S(2)}) copy-start(f32[4,256]{1,0:T(4,128)} %param.13) | copy-start | bytes 12292
  71.6 6.0 %collective-permute-start.1 = (f32[16,4,256]{2,0,1:T(8,128)S(1)}, f32[16,4,256]{2,0,1:T(8,128)S(1)}, u32[]{:S(2)}, u32[]{:S(2)}) collective-permute-start(f32[16,4,256]{2,0,1:T(8,128)S(1)} %copy.143), channel_id=1, source_target_pairs={{0,1},{1,0},{2,3},{3,2},{4,5},{5,4},{6,7},{7,6},{8,9},{9,8},{10,11... | collective-permute-start | bytes 196616 | tf_op jit(solution)/shard_map/ppermute | solution.py:44
  99.1 42.2 %copy-start = (f32[32,130,128]{2,1,0:T(8,128)S(1)}, f32[32,130,128]{2,1,0:T(8,128)}, u32[]{:S(2)}) copy-start(f32[32,130,128]{2,1,0:T(8,128)} %all-gather.2.cloned.1.call-done) | copy-start | bytes 6389764
  99.1 33.0 %all-to-all-start.3 = ((f32[32,1,2048]{2,1,0:T(1,128)}), f32[32,1,2048]{2,1,0:T(1,128)S(1)}, u32[]{:S(2)}, u32[]{:S(2)}) async-start(f32[32,1,2048]{2,1,0:T(1,128)} %reshape.199), calls=%async_computation.3 | async-start | bytes 524288 | tf_op jit(solution)/shard_map/all_to_all | solution.py:39
  141.2 3.5 %copy-start.8 = (f32[32,32]{0,1:T(8,128)}, f32[32,32]{0,1:T(8,128)S(1)}, u32[]{:S(2)}) copy-start(f32[32,32]{0,1:T(8,128)S(1)} %fusion.57) | copy-start | bytes 12292
  143.5 39.3 %copy-start.1 = (f32[2,130,128]{2,0,1:T(2,128)}, f32[2,130,128]{2,0,1:T(2,128)S(1)}, u32[]{:S(2)}) copy-start(f32[2,130,128]{2,0,1:T(2,128)S(1)} %fusion.12) | copy-start | bytes 399364
  144.7 33.5 %all-to-all-start.4 = ((bf16[32,129,128]{2,1,0:T(8,128)(2,1)}), bf16[32,129,128]{2,1,0:T(8,128)(2,1)S(1)}, u32[]{:S(2)}, u32[]{:S(2)}) async-start(bf16[32,129,128]{2,1,0:T(8,128)(2,1)} %bitcast.25), calls=%async_computation.4 | async-start | bytes 2228224 | tf_op jit(solution)/shard_map/all_to_all | solution.py:53
  178.8 20.5 %copy-start.6 = (bf16[1,32,4,256]{3,2,1,0:T(4,128)(2,1)S(1)}, bf16[1,32,4,256]{3,2,1,0:T(4,128)(2,1)}, u32[]{:S(2)}) copy-start(bf16[1,32,4,256]{3,2,1,0:T(4,128)(2,1)} %get-tuple-element.43) | copy-start | bytes 196612
  194.7 5.6 %collective-permute-start.2 = (f32[16,4,256]{2,0,1:T(8,128)S(1)}, f32[16,4,256]{2,0,1:T(8,128)S(1)}, u32[]{:S(2)}, u32[]{:S(2)}) collective-permute-start(f32[16,4,256]{2,0,1:T(8,128)S(1)} %copy.147), channel_id=1, source_target_pairs={{0,1},{1,0},{2,3},{3,2},{4,5},{5,4},{6,7},{7,6},{8,9},{9,8},{10,11... | collective-permute-start | bytes 196616 | tf_op jit(solution)/shard_map/ppermute | solution.py:44
  213.4 28.6 %copy-start.9 = (f32[32,32]{0,1:T(8,128)S(1)}, f32[32,32]{0,1:T(8,128)}, u32[]{:S(2)}) copy-start(f32[32,32]{0,1:T(8,128)} %copy-done.8) | copy-start | bytes 12292
Sparse Core Ops, SparseCore 0:
  28.2 67.7 all-gather.1

commit v6 on v5

--- a/solution.py
+++ b/solution.py
@@ -1,6 +1,7 @@
 import jax
 import jax.numpy as jnp
 from jax import lax
+from jax.experimental import pallas as pl
 from jax.sharding import PartitionSpec as P
 
 UPDATES = 2
@@ -15,6 +16,32 @@
     middle = lax.linalg.triangular_solve(factor, cross, left_side=True, lower=True)
     return lax.linalg.triangular_solve(factor, middle, left_side=True, lower=True, transpose_a=True)
 
+
+def _eliminate(a_ref, b_ref, o_ref):
+    n = a_ref.shape[0]
+    a = a_ref[...]
+    b = b_ref[...]
+    rows = lax.broadcasted_iota(jnp.int32, a.shape, 0)
+    cols = lax.broadcasted_iota(jnp.int32, a.shape, 1)
+    rows_b = lax.broadcasted_iota(jnp.int32, b.shape, 0)
+
+    def step(k, carry):
+        a, b = carry
+        row_a = jnp.sum(jnp.where(rows == k, a, 0.0), axis=0, keepdims=True)
+        row_b = jnp.sum(jnp.where(rows_b == k, b, 0.0), axis=0, keepdims=True)
+        col = jnp.sum(jnp.where(cols == k, a, 0.0), axis=1, keepdims=True)
+        pivot = jnp.sum(jnp.where(cols[:1] == k, row_a, 0.0), axis=1, keepdims=True)
+        ra = row_a / pivot
+        rb = row_b / pivot
+        a = jnp.where(rows == k, ra, a - col * ra)
+        b = jnp.where(rows_b == k, rb, b - col * rb)
+        return a, b
+
+    a, b = lax.fori_loop(0, n, step, (a, b))
+    o_ref[...] = b
+
+def solve_spd(a, b):
+    return pl.pallas_call(_eliminate, out_shape=jax.ShapeDtypeStruct(b.shape, b.dtype))(a, b)
 
 def pack(w_in, b_in, w_out, b_out):
     n, hid = w_in.shape[0], w_in.shape[2]
@@ -104,7 +131,8 @@
         if update == 0:
             sums = sums + whole[0, 0, 0] * 0
         sums = gather_sum(sums, "dp")
-        gain = solve_gain(sums[0] / count, sums[1] / count)
+        eye = jnp.eye(sums.shape[1], dtype=sums.dtype)
+        gain = solve_spd(sums[0] / count + ridge_level * eye, sums[1] / count)
         if update == 0:
             first_gain = gain
             columns = lax.dynamic_slice_in_dim(gain, first, per_device, 1)

time: 255 us -> 252 us (0.988)
  other arithmetic: 21.5 us -> 10.5 us
  Pallas kernels: 0 us -> 8.93 us
    another operation x13 -> x3, other arithmetic: 15.8 us -> 2.42 us  [the longest x6 7.18 us: solve_gain(): factor = jnp.linalg.cholesky(gram + ridge_level * eye)]
    pallas_call x0 -> x2, Pallas kernels: none -> 8.93 us  [solve_spd(): pl.pallas_call(_eliminate, out_shape=jax.ShapeDtypeStruct(b.shape, b.dtype))]
    unnamed x48 -> x42, local copies, waits for them, and re-layouts: 5.43 us -> 5.12 us
where the time goes in v6:
time: 252 us; the launch traced here: 251 us
  waiting for transfers between devices  73.6 us (29%)
  blocking collectives  65.9 us (26%)
  starting transfers between devices  50.5 us (20%)
  between operations  15.3 us (6%)
  local copies, waits for them, and re-layouts  13.3 us (5%)
  matrix products  12.9 us (5%)
  other arithmetic  10.5 us (4%)
  Pallas kernels  8.93 us (4%)
    all_to_all x2, waiting for transfers between devices, predict(): got = lax.all_to_all(tiles, 'dp', split_axis=0, concat_axis=0, tiled=True)  55.3 us
    all_to_all x3, blocking collectives, gather_sum(): lax.all_to_all(tiles, axis, split_axis=0, concat_axis=0, tiled=True)  40.8 us
    all_to_all x2, blocking collectives, collect(): lax.all_to_all(blocks, 'member', split_axis=0, concat_axis=0, tiled=True)  25.1 us
    all_to_all x1, starting transfers between devices, gather_sum(): lax.all_to_all(tiles, axis, split_axis=0, concat_axis=0, tiled=True)  20 us
    all_to_all x2, starting transfers between devices, predict(): got = lax.all_to_all(tiles, 'dp', split_axis=0, concat_axis=0, tiled=True)  18.6 us
    all_to_all x1, waiting for transfers between devices, gather_sum(): lax.all_to_all(tiles, axis, split_axis=0, concat_axis=0, tiled=True)  12.9 us
    ppermute x3, starting transfers between devices, swap_pair(): return lax.ppermute(x, 'dp', [(i, i ^ 1) for i in range(n)])  12 us
    pallas_call x2, Pallas kernels, solve_spd(): pl.pallas_call(_eliminate, out_shape=jax.ShapeDtypeStruct(b.shape, b.dtype))  8.93 us
  transfers between devices with their start and end apart: 7, of which 6 were waited for; matrix products, arithmetic and copies ran while one was open for 3% of the time, Pallas kernels for 0%

profile of v6, /device:TPU:1, one launch (start us, length us, event | category | flops | bytes accessed | tf_op | source)
XLA Modules:
  0.0 251.0 jit_solution(3656886811214374537)
XLA Ops:
  7.2 0.9 convert.16
  8.1 0.8 convert.17
  8.9 0.7 bitcast_convert_fusion
  9.7 1.1 broadcast_in_dim.18
  10.8 14.4 %all-to-all-start = ((bf16[32,129,128]{2,1,0:T(8,128)(2,1)}), bf16[32,129,128]{2,1,0:T(8,128)(2,1)S(1)}, u32[]{:S(2)}, u32[]{:S(2)}) async-start(bf16[32,129,128]{2,1,0:T(8,128)(2,1)} %bitcast.2), calls=%async_computation | async-start | bytes 2228224 | tf_op jit(solution)/shard_map/all_to_all | solution.py:80
  25.5 0.5 copy-done.2
  26.1 0.7 copy.104
  26.8 2.1 collective-permute-start
  29.0 25.8 %all-to-all-done = bf16[32,129,128]{2,1,0:T(8,128)(2,1)S(1)} async-done(((bf16[32,129,128]{2,1,0:T(8,128)(2,1)}), bf16[32,129,128]{2,1,0:T(8,128)(2,1)S(1)}, u32[]{:S(2)}, u32[]{:S(2)}) %all-to-all-start) | async-done | bytes 1056800 | tf_op jit(solution)/shard_map/all_to_all | solution.py:80
  54.8 2.5 fusion.20
  57.3 14.2 %all_to_all.40 = f32[16,4,512]{2,1,0:T(4,128)S(1)} all-to-all(f32[16,4,512]{2,1,0:T(4,128)S(1)} %reshape.152), channel_id=1, replica_groups=mesh['member'=16,'dp'=32] {'member'}, dimensions={0} | all-to-all | bytes 262144 | tf_op jit(solution)/shard_map/all_to_all | solution.py:96
  71.6 5.1 %collective-permute-start.1 = (f32[16,4,256]{2,0,1:T(8,128)S(1)}, f32[16,4,256]{2,0,1:T(8,128)S(1)}, u32[]{:S(2)}, u32[]{:S(2)}) collective-permute-start(f32[16,4,256]{2,0,1:T(8,128)S(1)} %copy.123), channel_id=1, source_target_pairs={{0,1},{1,0},{2,3},{3,2},{4,5},{5,4},{6,7},{7,6},{8,9},{9,8},{10,11... | collective-permute-start | bytes 196616 | tf_op jit(solution)/shard_map/ppermute | solution.py:71
  76.7 0.7 fusion.67
  78.7 11.1 %all_to_all.41 = f32[16,1,2048]{2,1,0:T(1,128)S(1)} all-to-all(f32[16,1,2048]{2,1,0:T(1,128)S(1)} %reshape.168), channel_id=1, replica_groups=mesh['member'=16,'dp'=32] {'member'}, dimensions={0} | all-to-all | bytes 262144 | tf_op jit(solution)/shard_map/all_to_all | solution.py:66
  89.8 0.5 broadcast.113
  90.3 1.0 reduce.10
  91.5 4.4 %all-gather.2.cloned.1.call-done = f32[32,130,128]{2,1,0:T(8,128)} async-done(((f32[2,130,128]{2,1,0:T(8,128)}), f32[32,130,128]{2,1,0:T(8,128)}) %all-gather.2.cloned.1.call-update) | async-done | bytes 2129936 | tf_op jit(solution)/shard_map/all_gather | solution.py:114
  95.9 1.2 slice.112
  97.9 1.1 reshape.170
  99.1 20.0 %all-to-all-start.3 = ((f32[32,1,2048]{2,1,0:T(1,128)}), f32[32,1,2048]{2,1,0:T(1,128)S(1)}, u32[]{:S(2)}, u32[]{:S(2)}) async-start(f32[32,1,2048]{2,1,0:T(1,128)} %reshape.170), calls=%async_computation.3 | async-start | bytes 524288 | tf_op jit(solution)/shard_map/all_to_all | solution.py:66
  119.0 12.9 %all-to-all-done.3 = f32[32,1,2048]{2,1,0:T(1,128)S(1)} async-done(((f32[32,1,2048]{2,1,0:T(1,128)}), f32[32,1,2048]{2,1,0:T(1,128)S(1)}, u32[]{:S(2)}, u32[]{:S(2)}) %all-to-all-start.3) | async-done | bytes 262176 | tf_op jit(solution)/shard_map/all_to_all | solution.py:66
  132.0 1.3 reduce.11
  133.7 0.6 fusion.48.b_ref
  134.3 0.6 select_add_fusion.1.a_ref
  134.9 4.5 %shard_map.102 = f32[32,32]{1,0:T(8,128)} custom-call(f32[32,32]{1,0:T(8,128)} %select_add_fusion.1.a_ref, f32[32,32]{1,0:T(8,128)} %fusion.48.b_ref), custom_call_target="tpu_custom_call" | custom-call | tf_op jit(solution)/shard_map/pallas_call | solution.py:44
  139.4 2.3 fusion.15
  141.8 1.1 broadcast_in_dim.21
  142.9 4.1 %all-to-all-start.4 = ((bf16[32,129,128]{2,1,0:T(8,128)(2,1)}), bf16[32,129,128]{2,1,0:T(8,128)(2,1)S(1)}, u32[]{:S(2)}, u32[]{:S(2)}) async-start(bf16[32,129,128]{2,1,0:T(8,128)(2,1)} %bitcast.20), calls=%async_computation.4 | async-start | bytes 2228224 | tf_op jit(solution)/shard_map/all_to_all | solution.py:80
  147.1 29.5 %all-to-all-done.4 = bf16[32,129,128]{2,1,0:T(8,128)(2,1)S(1)} async-done(((bf16[32,129,128]{2,1,0:T(8,128)(2,1)}), bf16[32,129,128]{2,1,0:T(8,128)(2,1)S(1)}, u32[]{:S(2)}, u32[]{:S(2)}) %all-to-all-start.4) | async-done | bytes 1056800 | tf_op jit(solution)/shard_map/all_to_all | solution.py:80
  176.6 0.6 slice_convert_fusion.1
  177.2 3.9 %fusion.21 = f32[64,512]{1,0:T(8,128)} fusion(f32[32,128]{1,0:T(8,128)} %bitcast.87, bf16[32,129,128]{2,1,0:T(8,128)(2,1)S(1)} %all-to-all-done.4, f32[64]{0:T(128)S(1)} %fusion.58, bf16[256,64]{0,1:T(8,128)(2,1)} %copy-done.13, bf16[256,64]{0,1:T(8,128)(2,1)} %param.7), kind=kOutput, calls=%fused_computation.17 | convolution fusion | flops 541229056 | bytes 1262080 | tf_op jit(solution)/shard_map/doh,sdh->os/dot_general | solution.py:88
  181.1 0.9 reshape.154
  182.1 10.9 %all_to_all.42 = f32[16,4,512]{2,1,0:T(4,128)S(1)} all-to-all(f32[16,4,512]{2,1,0:T(4,128)S(1)} %reshape.154), channel_id=1, replica_groups=mesh['member'=16,'dp'=32] {'member'}, dimensions={0} | all-to-all | bytes 262144 | tf_op jit(solution)/shard_map/all_to_all | solution.py:96
  193.0 4.7 %collective-permute-start.2 = (f32[16,4,256]{2,0,1:T(8,128)S(1)}, f32[16,4,256]{2,0,1:T(8,128)S(1)}, u32[]{:S(2)}, u32[]{:S(2)}) collective-permute-start(f32[16,4,256]{2,0,1:T(8,128)S(1)} %copy.125), channel_id=1, source_target_pairs={{0,1},{1,0},{2,3},{3,2},{4,5},{5,4},{6,7},{7,6},{8,9},{9,8},{10,11... | collective-permute-start | bytes 196616 | tf_op jit(solution)/shard_map/ppermute | solution.py:71
  197.8 0.7 collective-permute-done.2
  199.6 10.2 %all_to_all.43 = f32[16,1,2048]{2,1,0:T(1,128)S(1)} all-to-all(f32[16,1,2048]{2,1,0:T(1,128)S(1)} %reshape.172), channel_id=1, replica_groups=mesh['member'=16,'dp'=32] {'member'}, dimensions={0} | all-to-all | bytes 262144 | tf_op jit(solution)/shard_map/all_to_all | solution.py:66
  209.8 0.9 reduce.12
  211.6 19.5 %all_to_all.44 = f32[32,1,2048]{2,1,0:T(1,128)S(1)} all-to-all(f32[32,1,2048]{2,1,0:T(1,128)S(1)} %reshape.174), channel_id=1, replica_groups=mesh['member'=16,'dp'=32] {'dp'}, dimensions={0} | all-to-all | bytes 524288 | tf_op jit(solution)/shard_map/all_to_all | solution.py:66
  231.1 1.3 reduce.13
  232.9 0.6 fusion.46.b_ref
  233.5 0.6 select_add_fusion.a_ref
  234.1 4.5 %shard_map.103 = f32[32,32]{1,0:T(8,128)} custom-call(f32[32,32]{1,0:T(8,128)} %select_add_fusion.a_ref, f32[32,32]{1,0:T(8,128)} %fusion.46.b_ref), custom_call_target="tpu_custom_call" | custom-call | tf_op jit(solution)/shard_map/pallas_call | solution.py:44
  238.5 0.9 fusion.51
  239.5 2.3 fusion.12
  241.8 0.6 slice_bitcast_fusion
  242.3 0.6 slice_bitcast_fusion.1
  242.9 0.6 copy.118
  243.5 0.6 copy.119
  (82 shorter events, 4.9 us)
Async XLA Ops:
  7.2 18.1 %copy-start.4 = (f32[2,64,128]{2,1,0:T(8,128)S(1)}, f32[2,64,128]{2,1,0:T(8,128)}, u32[]{:S(2)}) copy-start(f32[2,64,128]{2,1,0:T(8,128)} %param.10) | copy-start | bytes 196612
  7.2 18.2 %copy-start.5 = (f32[2,64,128]{2,1,0:T(8,128)S(1)}, f32[2,64,128]{2,1,0:T(8,128)}, u32[]{:S(2)}) copy-start(f32[2,64,128]{2,1,0:T(8,128)} %param.12) | copy-start | bytes 196612
  7.2 18.8 %copy-start.10 = (f32[2,128]{1,0:T(2,128)S(1)}, f32[2,128]{1,0:T(2,128)}, u32[]{:S(2)}) copy-start(f32[2,128]{1,0:T(2,128)} %param.11) | copy-start | bytes 3076
  7.2 18.3 %copy-start.11 = (f32[2,64]{1,0:T(2,128)S(1)}, f32[2,64]{1,0:T(2,128)}, u32[]{:S(2)}) copy-start(f32[2,64]{1,0:T(2,128)} %param.13) | copy-start | bytes 1540
  9.6 17.1 %copy-start.12 = (bf16[256,64]{0,1:T(8,128)(2,1)S(1)}, bf16[256,64]{0,1:T(8,128)(2,1)}, u32[]{:S(2)}) copy-start(bf16[256,64]{0,1:T(8,128)(2,1)} %param.7) | copy-start | bytes 98308
  10.8 44.0 %all-to-all-start = ((bf16[32,129,128]{2,1,0:T(8,128)(2,1)}), bf16[32,129,128]{2,1,0:T(8,128)(2,1)S(1)}, u32[]{:S(2)}, u32[]{:S(2)}) async-start(bf16[32,129,128]{2,1,0:T(8,128)(2,1)} %bitcast.2), calls=%async_computation | async-start | bytes 2228224 | tf_op jit(solution)/shard_map/all_to_all | solution.py:80
  25.2 70.7 %all-gather.2.cloned.1.call-start = ((), (), s32[]{:S(2)}) async-start(), calls=%async_computation.8 | async-start | bytes 2367488 | tf_op jit(solution)/shard_map/all_gather | solution.py:114
  25.4 0.6 copy-start.2
  25.5 0.6 copy-start.3
  26.8 28.0 %collective-permute-start = (bf16[256,64]{0,1:T(8,128)(2,1)S(1)}, bf16[256,64]{0,1:T(8,128)(2,1)S(1)}, u32[]{:S(2)}, u32[]{:S(2)}) collective-permute-start(bf16[256,64]{0,1:T(8,128)(2,1)S(1)} %copy-done.12), channel_id=1, source_target_pairs={{0,1},{1,0},{2,3},{3,2},{4,5},{5,4},{6,7},{7,6},{8,9},{9,8},{10,11... | collective-permute-start | bytes 98312 | tf_op jit(solution)/shard_map/ppermute | solution.py:71
  54.8 2.5 copy-start.13
  54.8 21.9 %copy-start.8 = (bf16[2,32,4,256]{3,2,1,0:T(4,128)(2,1)S(1)}, bf16[2,32,4,256]{3,2,1,0:T(4,128)(2,1)}, u32[]{:S(2)}) copy-start(bf16[2,32,4,256]{3,2,1,0:T(4,128)(2,1)} %param.9) | copy-start | bytes 393220
  54.8 22.8 %copy-start.9 = (f32[4,256]{1,0:T(4,128)S(1)}, f32[4,256]{1,0:T(4,128)}, u32[]{:S(2)}) copy-start(f32[4,256]{1,0:T(4,128)} %param.8) | copy-start | bytes 12292
  71.6 6.0 %collective-permute-start.1 = (f32[16,4,256]{2,0,1:T(8,128)S(1)}, f32[16,4,256]{2,0,1:T(8,128)S(1)}, u32[]{:S(2)}, u32[]{:S(2)}) collective-permute-start(f32[16,4,256]{2,0,1:T(8,128)S(1)} %copy.123), channel_id=1, source_target_pairs={{0,1},{1,0},{2,3},{3,2},{4,5},{5,4},{6,7},{7,6},{8,9},{9,8},{10,11... | collective-permute-start | bytes 196616 | tf_op jit(solution)/shard_map/ppermute | solution.py:71
  97.9 41.5 %copy-start = (f32[32,130,128]{2,1,0:T(8,128)S(1)}, f32[32,130,128]{2,1,0:T(8,128)}, u32[]{:S(2)}) copy-start(f32[32,130,128]{2,1,0:T(8,128)} %all-gather.2.cloned.1.call-done) | copy-start | bytes 6389764
  99.1 32.9 %all-to-all-start.3 = ((f32[32,1,2048]{2,1,0:T(1,128)}), f32[32,1,2048]{2,1,0:T(1,128)S(1)}, u32[]{:S(2)}, u32[]{:S(2)}) async-start(f32[32,1,2048]{2,1,0:T(1,128)} %reshape.170), calls=%async_computation.3 | async-start | bytes 524288 | tf_op jit(solution)/shard_map/all_to_all | solution.py:66
  141.7 39.4 %copy-start.1 = (f32[2,130,128]{2,0,1:T(2,128)}, f32[2,130,128]{2,0,1:T(2,128)S(1)}, u32[]{:S(2)}) copy-start(f32[2,130,128]{2,0,1:T(2,128)S(1)} %fusion.15) | copy-start | bytes 399364
  142.9 33.7 %all-to-all-start.4 = ((bf16[32,129,128]{2,1,0:T(8,128)(2,1)}), bf16[32,129,128]{2,1,0:T(8,128)(2,1)S(1)}, u32[]{:S(2)}, u32[]{:S(2)}) async-start(bf16[32,129,128]{2,1,0:T(8,128)(2,1)} %bitcast.20), calls=%async_computation.4 | async-start | bytes 2228224 | tf_op jit(solution)/shard_map/all_to_all | solution.py:80
  177.2 20.6 %copy-start.6 = (bf16[1,32,4,256]{3,2,1,0:T(4,128)(2,1)S(1)}, bf16[1,32,4,256]{3,2,1,0:T(4,128)(2,1)}, u32[]{:S(2)}) copy-start(bf16[1,32,4,256]{3,2,1,0:T(4,128)(2,1)} %get-tuple-element.40) | copy-start | bytes 196612
  193.0 5.4 %collective-permute-start.2 = (f32[16,4,256]{2,0,1:T(8,128)S(1)}, f32[16,4,256]{2,0,1:T(8,128)S(1)}, u32[]{:S(2)}, u32[]{:S(2)}) collective-permute-start(f32[16,4,256]{2,0,1:T(8,128)S(1)} %copy.125), channel_id=1, source_target_pairs={{0,1},{1,0},{2,3},{3,2},{4,5},{5,4},{6,7},{7,6},{8,9},{9,8},{10,11... | collective-permute-start | bytes 196616 | tf_op jit(solution)/shard_map/ppermute | solution.py:71
  211.1 27.4 %copy-start.7 = (f32[32,32]{1,0:T(8,128)S(1)}, f32[32,32]{1,0:T(8,128)}, u32[]{:S(2)}) copy-start(f32[32,32]{1,0:T(8,128)} %shard_map.102) | copy-start | bytes 12292
Sparse Core Ops, SparseCore 0:
  28.2 67.7 all-gather.1

commit v7 on v6

--- a/solution.py
+++ b/solution.py
@@ -37,7 +37,7 @@
         b = jnp.where(rows_b == k, rb, b - col * rb)
         return a, b
 
-    a, b = lax.fori_loop(0, n, step, (a, b))
+    a, b = lax.fori_loop(0, n, step, (a, b), unroll=True)
     o_ref[...] = b
 
 def solve_spd(a, b):
@@ -127,21 +127,20 @@
         cross_part = lax.dot_general(
             anomaly, misfit, (((1,), (1,)), ((), ())), precision=lax.Precision.HIGHEST
         )
-        sums = gather_sum(jnp.stack([gram_part, cross_part]), "member")
+        sums = gather_sum(gather_sum(jnp.stack([gram_part, cross_part]), "member"), "dp")
         if update == 0:
             sums = sums + whole[0, 0, 0] * 0
-        sums = gather_sum(sums, "dp")
         eye = jnp.eye(sums.shape[1], dtype=sums.dtype)
         gain = solve_spd(sums[0] / count + ridge_level * eye, sums[1] / count)
         if update == 0:
             first_gain = gain
             columns = lax.dynamic_slice_in_dim(gain, first, per_device, 1)
-            own = own + jnp.einsum("kj,kab->jab", columns, whole, precision=lax.Precision.HIGHEST)
+            own = own + jnp.einsum("kj,kab->jab", columns, whole, precision=lax.Precision.HIGH)
         else:
             eye = jnp.eye(gain.shape[0], dtype=gain.dtype)
             through = jnp.dot(eye + first_gain, gain, precision=lax.Precision.HIGHEST)
             columns = lax.dynamic_slice_in_dim(through, first, per_device, 1)
-            own = own + jnp.einsum("kj,kab->jab", columns, whole, precision=lax.Precision.HIGHEST)
+            own = own + jnp.einsum("kj,kab->jab", columns, whole, precision=lax.Precision.HIGH)
     return unpack(own, f_in, hid, outs)
 
 

time: 252 us -> 233 us (0.925)
  starting transfers between devices: 50.5 us -> 38.8 us
  waiting for transfers between devices: 73.6 us -> 70.5 us
    all_to_all x1, starting transfers between devices: 20 us -> 8.23 us  [gather_sum(): lax.all_to_all(tiles, axis, split_axis=0, concat_axis=0, tiled=True)]
    all_gather x1, waiting for transfers between devices: 4.43 us -> 0.02 us  [on_device(): whole = lax.all_gather(own, 'member', axis=0, tiled=True)]
    unnamed x42 -> x34, local copies, waits for them, and re-layouts: 5.12 us -> 4.57 us
  transfers between devices with their start and end apart: 7 -> 7, of which waited for: 6 -> 5; matrix products, arithmetic and copies ran while one was open for 3% -> 4% of each run, Pallas kernels for 0% -> 0%
where the time goes in v7:
time: 233 us; the launch traced here: 232 us
  waiting for transfers between devices  70.5 us (30%)
  blocking collectives  66.2 us (28%)
  starting transfers between devices  38.8 us (17%)
  between operations  15.3 us (7%)
  local copies, waits for them, and re-layouts  11.3 us (5%)
  matrix products  11.2 us (5%)
  other arithmetic  9.93 us (4%)
  Pallas kernels  9.15 us (4%)
    all_to_all x2, waiting for transfers between devices, predict(): got = lax.all_to_all(tiles, 'dp', split_axis=0, concat_axis=0, tiled=True)  55.9 us
    all_to_all x3, blocking collectives, gather_sum(): lax.all_to_all(tiles, axis, split_axis=0, concat_axis=0, tiled=True)  40.9 us
    all_to_all x2, blocking collectives, collect(): lax.all_to_all(blocks, 'member', split_axis=0, concat_axis=0, tiled=True)  25.3 us
    all_to_all x2, starting transfers between devices, predict(): got = lax.all_to_all(tiles, 'dp', split_axis=0, concat_axis=0, tiled=True)  18.6 us
    all_to_all x1, waiting for transfers between devices, gather_sum(): lax.all_to_all(tiles, axis, split_axis=0, concat_axis=0, tiled=True)  12.9 us
    ppermute x3, starting transfers between devices, swap_pair(): return lax.ppermute(x, 'dp', [(i, i ^ 1) for i in range(n)])  12 us
    pallas_call x2, Pallas kernels, solve_spd(): pl.pallas_call(_eliminate, out_shape=jax.ShapeDtypeStruct(b.shape, b.dtype))  9.15 us
    all_to_all x1, starting transfers between devices, gather_sum(): lax.all_to_all(tiles, axis, split_axis=0, concat_axis=0, tiled=True)  8.23 us
  transfers between devices with their start and end apart: 7, of which 5 were waited for; matrix products, arithmetic and copies ran while one was open for 4% of the time, Pallas kernels for 0%

profile of v7, /device:TPU:1, one launch (start us, length us, event | category | flops | bytes accessed | tf_op | source)
XLA Modules:
  0.0 232.3 jit_solution(2221359186849998882)
XLA Ops:
  7.2 0.9 convert.16
  8.1 0.8 convert.17
  8.9 0.7 bitcast_convert_fusion
  9.7 1.1 broadcast_in_dim.18
  10.8 14.4 %all-to-all-start = ((bf16[32,129,128]{2,1,0:T(8,128)(2,1)}), bf16[32,129,128]{2,1,0:T(8,128)(2,1)S(1)}, u32[]{:S(2)}, u32[]{:S(2)}) async-start(bf16[32,129,128]{2,1,0:T(8,128)(2,1)} %bitcast.2), calls=%async_computation | async-start | bytes 2228224 | tf_op jit(solution)/shard_map/all_to_all | solution.py:80
  25.5 0.7 copy.104
  26.2 2.1 collective-permute-start
  28.4 26.4 %all-to-all-done = bf16[32,129,128]{2,1,0:T(8,128)(2,1)S(1)} async-done(((bf16[32,129,128]{2,1,0:T(8,128)(2,1)}), bf16[32,129,128]{2,1,0:T(8,128)(2,1)S(1)}, u32[]{:S(2)}, u32[]{:S(2)}) %all-to-all-start) | async-done | bytes 1056800 | tf_op jit(solution)/shard_map/all_to_all | solution.py:80
  54.8 2.5 %fusion.20 = f32[64,512]{1,0:T(8,128)S(1)} fusion(f32[32,128]{1,0:T(8,128)S(1)} %bitcast.86, bf16[32,129,128]{2,1,0:T(8,128)(2,1)S(1)} %all-to-all-done, f32[64]{0:T(128)S(1)} %fusion.57, bf16[256,64]{0,1:T(8,128)(2,1)S(1)} %collective-permute-done, bf16[256,64]{0,1:T(8,128)(2,1)S(1)} %copy-done.9), kind=kOutput, calls=%fused_computation.16 | convolution fusion | flops 541229056 | bytes 1262080 | tf_op jit(solution)/shard_map/doh,sdh->os/dot_general | solution.py:88
  57.3 14.2 %all_to_all.40 = f32[16,4,512]{2,1,0:T(4,128)S(1)} all-to-all(f32[16,4,512]{2,1,0:T(4,128)S(1)} %reshape.150), channel_id=1, replica_groups=mesh['member'=16,'dp'=32] {'member'}, dimensions={0} | all-to-all | bytes 262144 | tf_op jit(solution)/shard_map/all_to_all | solution.py:96
  71.6 5.1 %collective-permute-start.1 = (f32[16,4,256]{2,0,1:T(8,128)S(1)}, f32[16,4,256]{2,0,1:T(8,128)S(1)}, u32[]{:S(2)}, u32[]{:S(2)}) collective-permute-start(f32[16,4,256]{2,0,1:T(8,128)S(1)} %copy.123), channel_id=1, source_target_pairs={{0,1},{1,0},{2,3},{3,2},{4,5},{5,4},{6,7},{7,6},{8,9},{9,8},{10,11... | collective-permute-start | bytes 196616 | tf_op jit(solution)/shard_map/ppermute | solution.py:71
  76.8 0.8 collective-permute-done.1
  78.1 0.3 convolution_bitcast_fusion.2
  78.7 11.0 %all_to_all.41 = f32[16,1,2048]{2,1,0:T(1,128)S(1)} all-to-all(f32[16,1,2048]{2,1,0:T(1,128)S(1)} %reshape.166), channel_id=1, replica_groups=mesh['member'=16,'dp'=32] {'member'}, dimensions={0} | all-to-all | bytes 262144 | tf_op jit(solution)/shard_map/all_to_all | solution.py:66
  89.8 0.5 broadcast.110
  90.3 1.0 reduce.10
  91.6 1.2 reshape.168
  92.7 8.2 %all-to-all-start.3 = ((f32[32,1,2048]{2,1,0:T(1,128)}), f32[32,1,2048]{2,1,0:T(1,128)S(1)}, u32[]{:S(2)}, u32[]{:S(2)}) async-start(f32[32,1,2048]{2,1,0:T(1,128)} %reshape.168), calls=%async_computation.3 | async-start | bytes 524288 | tf_op jit(solution)/shard_map/all_to_all | solution.py:66
  101.0 12.9 %all-to-all-done.3 = f32[32,1,2048]{2,1,0:T(1,128)S(1)} async-done(((f32[32,1,2048]{2,1,0:T(1,128)}), f32[32,1,2048]{2,1,0:T(1,128)S(1)}, u32[]{:S(2)}, u32[]{:S(2)}) %all-to-all-start.3) | async-done | bytes 262176 | tf_op jit(solution)/shard_map/all_to_all | solution.py:66
  113.9 1.3 reduce.11
  115.2 0.3 reshape.169
  115.6 1.2 slice.112
  117.5 0.6 fusion.48.b_ref
  118.1 0.6 select_add_fusion.1.a_ref
  118.7 4.6 %shard_map.102 = f32[32,32]{1,0:T(8,128)} custom-call(f32[32,32]{1,0:T(8,128)} %select_add_fusion.1.a_ref, f32[32,32]{1,0:T(8,128)} %fusion.48.b_ref), custom_call_target="tpu_custom_call" | custom-call | tf_op jit(solution)/shard_map/pallas_call | solution.py:44
  123.3 2.6 %fusion.15 = f32[2,130,128]{2,0,1:T(2,128)S(1)} fusion(f32[32,130,128]{2,1,0:T(8,128)} %all-gather.2.cloned.1.call-done, f32[32,32]{1,0:T(8,128)} %shard_map.102, s32[]{:T(128)S(6)} %select_n.64, f32[2,1,128]{2,0,1:T(2,128)S(1)} %pad_bitcast_fusion, f32[2,1,128]{2,0,1:T(2,128)S(1)} %bitcast.89, f32[2,64,128]{2,0,1:T(2,128)S(1)} %copy.93, ...), kind=kOutput, calls=%fused_computation.13 | convolution fusion | flops 6522880 | bytes 2400260 | tf_op jit(solution)/shard_map/kj,kab->jab/dot_general | solution.py:138
  126.0 1.1 broadcast_in_dim.21
  127.1 4.1 %all-to-all-start.4 = ((bf16[32,129,128]{2,1,0:T(8,128)(2,1)}), bf16[32,129,128]{2,1,0:T(8,128)(2,1)S(1)}, u32[]{:S(2)}, u32[]{:S(2)}) async-start(bf16[32,129,128]{2,1,0:T(8,128)(2,1)} %bitcast.20), calls=%async_computation.4 | async-start | bytes 2228224 | tf_op jit(solution)/shard_map/all_to_all | solution.py:80
  131.3 29.5 %all-to-all-done.4 = bf16[32,129,128]{2,1,0:T(8,128)(2,1)S(1)} async-done(((bf16[32,129,128]{2,1,0:T(8,128)(2,1)}), bf16[32,129,128]{2,1,0:T(8,128)(2,1)S(1)}, u32[]{:S(2)}, u32[]{:S(2)}) %all-to-all-start.4) | async-done | bytes 1056800 | tf_op jit(solution)/shard_map/all_to_all | solution.py:80
  160.8 2.5 %fusion.21 = f32[64,512]{1,0:T(8,128)S(1)} fusion(f32[32,128]{1,0:T(8,128)S(1)} %bitcast.87, bf16[32,129,128]{2,1,0:T(8,128)(2,1)S(1)} %all-to-all-done.4, f32[64]{0:T(128)S(1)} %fusion.58, bf16[256,64]{0,1:T(8,128)(2,1)S(1)} %collective-permute-done, bf16[256,64]{0,1:T(8,128)(2,1)S(1)} %copy-done.9), kind=kOutput, calls=%fused_computation.17 | convolution fusion | flops 541229056 | bytes 1262080 | tf_op jit(solution)/shard_map/doh,sdh->os/dot_general | solution.py:88
  163.3 11.1 %all_to_all.42 = f32[16,4,512]{2,1,0:T(4,128)S(1)} all-to-all(f32[16,4,512]{2,1,0:T(4,128)S(1)} %reshape.152), channel_id=1, replica_groups=mesh['member'=16,'dp'=32] {'member'}, dimensions={0} | all-to-all | bytes 262144 | tf_op jit(solution)/shard_map/all_to_all | solution.py:96
  174.4 4.7 %collective-permute-start.2 = (f32[16,4,256]{2,0,1:T(8,128)S(1)}, f32[16,4,256]{2,0,1:T(8,128)S(1)}, u32[]{:S(2)}, u32[]{:S(2)}) collective-permute-start(f32[16,4,256]{2,0,1:T(8,128)S(1)} %copy.125), channel_id=1, source_target_pairs={{0,1},{1,0},{2,3},{3,2},{4,5},{5,4},{6,7},{7,6},{8,9},{9,8},{10,11... | collective-permute-start | bytes 196616 | tf_op jit(solution)/shard_map/ppermute | solution.py:71
  179.2 0.9 collective-permute-done.2
  181.2 10.2 %all_to_all.43 = f32[16,1,2048]{2,1,0:T(1,128)S(1)} all-to-all(f32[16,1,2048]{2,1,0:T(1,128)S(1)} %reshape.170), channel_id=1, replica_groups=mesh['member'=16,'dp'=32] {'member'}, dimensions={0} | all-to-all | bytes 262144 | tf_op jit(solution)/shard_map/all_to_all | solution.py:66
  191.4 0.9 reduce.12
  192.7 0.5 reshape.172
  193.2 19.6 %all_to_all.44 = f32[32,1,2048]{2,1,0:T(1,128)S(1)} all-to-all(f32[32,1,2048]{2,1,0:T(1,128)S(1)} %reshape.172), channel_id=1, replica_groups=mesh['member'=16,'dp'=32] {'dp'}, dimensions={0} | all-to-all | bytes 524288 | tf_op jit(solution)/shard_map/all_to_all | solution.py:66
  212.8 1.3 reduce.13
  214.1 0.3 reshape.173
  214.5 0.6 fusion.46.b_ref
  215.2 0.6 select_add_fusion.a_ref
  215.8 4.6 %shard_map.103 = f32[32,32]{1,0:T(8,128)} custom-call(f32[32,32]{1,0:T(8,128)} %select_add_fusion.a_ref, f32[32,32]{1,0:T(8,128)} %fusion.46.b_ref), custom_call_target="tpu_custom_call" | custom-call | tf_op jit(solution)/shard_map/pallas_call | solution.py:44
  220.3 0.9 fusion.51
  221.3 1.7 fusion.12
  223.1 0.6 slice_bitcast_fusion
  223.6 0.6 slice_bitcast_fusion.1
  224.2 0.6 copy.118
  224.8 0.6 copy.119
  (74 shorter events, 3.4 us)
Async XLA Ops:
  7.2 18.1 %copy-start.2 = (f32[2,64,128]{2,1,0:T(8,128)S(1)}, f32[2,64,128]{2,1,0:T(8,128)}, u32[]{:S(2)}) copy-start(f32[2,64,128]{2,1,0:T(8,128)} %param.10) | copy-start | bytes 196612
  7.2 18.2 %copy-start.3 = (f32[2,64,128]{2,1,0:T(8,128)S(1)}, f32[2,64,128]{2,1,0:T(8,128)}, u32[]{:S(2)}) copy-start(f32[2,64,128]{2,1,0:T(8,128)} %param.12) | copy-start | bytes 196612
  7.2 18.3 %copy-start.7 = (f32[2,128]{1,0:T(2,128)S(1)}, f32[2,128]{1,0:T(2,128)}, u32[]{:S(2)}) copy-start(f32[2,128]{1,0:T(2,128)} %param.11) | copy-start | bytes 3076
  7.2 18.2 %copy-start.8 = (f32[2,64]{1,0:T(2,128)S(1)}, f32[2,64]{1,0:T(2,128)}, u32[]{:S(2)}) copy-start(f32[2,64]{1,0:T(2,128)} %param.13) | copy-start | bytes 1540
  9.6 16.6 %copy-start.9 = (bf16[256,64]{0,1:T(8,128)(2,1)S(1)}, bf16[256,64]{0,1:T(8,128)(2,1)}, u32[]{:S(2)}) copy-start(bf16[256,64]{0,1:T(8,128)(2,1)} %param.7) | copy-start | bytes 98308
  10.8 44.0 %all-to-all-start = ((bf16[32,129,128]{2,1,0:T(8,128)(2,1)}), bf16[32,129,128]{2,1,0:T(8,128)(2,1)S(1)}, u32[]{:S(2)}, u32[]{:S(2)}) async-start(bf16[32,129,128]{2,1,0:T(8,128)(2,1)} %bitcast.2), calls=%async_computation | async-start | bytes 2228224 | tf_op jit(solution)/shard_map/all_to_all | solution.py:80
  25.2 90.4 %all-gather.2.cloned.1.call-start = ((), (), s32[]{:S(2)}) async-start(), calls=%async_computation.8 | async-start | bytes 2367488 | tf_op jit(solution)/shard_map/all_gather | solution.py:114
  26.2 28.6 %collective-permute-start = (bf16[256,64]{0,1:T(8,128)(2,1)S(1)}, bf16[256,64]{0,1:T(8,128)(2,1)S(1)}, u32[]{:S(2)}, u32[]{:S(2)}) collective-permute-start(bf16[256,64]{0,1:T(8,128)(2,1)S(1)} %copy-done.9), channel_id=1, source_target_pairs={{0,1},{1,0},{2,3},{3,2},{4,5},{5,4},{6,7},{7,6},{8,9},{9,8},{10,11... | collective-permute-start | bytes 98312 | tf_op jit(solution)/shard_map/ppermute | solution.py:71
  54.8 21.9 %copy-start.5 = (bf16[2,32,4,256]{3,2,1,0:T(4,128)(2,1)S(1)}, bf16[2,32,4,256]{3,2,1,0:T(4,128)(2,1)}, u32[]{:S(2)}) copy-start(bf16[2,32,4,256]{3,2,1,0:T(4,128)(2,1)} %param.9) | copy-start | bytes 393220
  54.8 22.8 %copy-start.6 = (f32[4,256]{1,0:T(4,128)S(1)}, f32[4,256]{1,0:T(4,128)}, u32[]{:S(2)}) copy-start(f32[4,256]{1,0:T(4,128)} %param.8) | copy-start | bytes 12292
  71.6 6.0 %collective-permute-start.1 = (f32[16,4,256]{2,0,1:T(8,128)S(1)}, f32[16,4,256]{2,0,1:T(8,128)S(1)}, u32[]{:S(2)}, u32[]{:S(2)}) collective-permute-start(f32[16,4,256]{2,0,1:T(8,128)S(1)} %copy.123), channel_id=1, source_target_pairs={{0,1},{1,0},{2,3},{3,2},{4,5},{5,4},{6,7},{7,6},{8,9},{9,8},{10,11... | collective-permute-start | bytes 196616 | tf_op jit(solution)/shard_map/ppermute | solution.py:71
  92.7 21.2 %all-to-all-start.3 = ((f32[32,1,2048]{2,1,0:T(1,128)}), f32[32,1,2048]{2,1,0:T(1,128)S(1)}, u32[]{:S(2)}, u32[]{:S(2)}) async-start(f32[32,1,2048]{2,1,0:T(1,128)} %reshape.168), calls=%async_computation.3 | async-start | bytes 524288 | tf_op jit(solution)/shard_map/all_to_all | solution.py:66
  125.9 37.4 %copy-start.1 = (f32[2,130,128]{2,0,1:T(2,128)}, f32[2,130,128]{2,0,1:T(2,128)S(1)}, u32[]{:S(2)}) copy-start(f32[2,130,128]{2,0,1:T(2,128)S(1)} %fusion.15) | copy-start | bytes 399364
  127.1 33.7 %all-to-all-start.4 = ((bf16[32,129,128]{2,1,0:T(8,128)(2,1)}), bf16[32,129,128]{2,1,0:T(8,128)(2,1)S(1)}, u32[]{:S(2)}, u32[]{:S(2)}) async-start(bf16[32,129,128]{2,1,0:T(8,128)(2,1)} %bitcast.20), calls=%async_computation.4 | async-start | bytes 2228224 | tf_op jit(solution)/shard_map/all_to_all | solution.py:80
  174.4 5.6 %collective-permute-start.2 = (f32[16,4,256]{2,0,1:T(8,128)S(1)}, f32[16,4,256]{2,0,1:T(8,128)S(1)}, u32[]{:S(2)}, u32[]{:S(2)}) collective-permute-start(f32[16,4,256]{2,0,1:T(8,128)S(1)} %copy.125), channel_id=1, source_target_pairs={{0,1},{1,0},{2,3},{3,2},{4,5},{5,4},{6,7},{7,6},{8,9},{9,8},{10,11... | collective-permute-start | bytes 196616 | tf_op jit(solution)/shard_map/ppermute | solution.py:71
  192.7 27.6 %copy-start.4 = (f32[32,32]{1,0:T(8,128)S(1)}, f32[32,32]{1,0:T(8,128)}, u32[]{:S(2)}) copy-start(f32[32,32]{1,0:T(8,128)} %shard_map.102) | copy-start | bytes 12292
  193.2 28.1 %copy-start = (f32[32,130,128]{2,1,0:T(8,128)S(1)}, f32[32,130,128]{2,1,0:T(8,128)}, u32[]{:S(2)}) copy-start(f32[32,130,128]{2,1,0:T(8,128)} %all-gather.2.cloned.1.call-done) | copy-start | bytes 6389764
Sparse Core Ops, SparseCore 0:
  28.2 67.4 all-gather.1

commit v8 on v7

--- a/solution.py
+++ b/solution.py
@@ -62,8 +62,10 @@
 
 def gather_sum(x, axis):
     n = lax.axis_size(axis)
-    tiles = jnp.broadcast_to(x[None], (n,) + x.shape)
-    return jnp.sum(lax.all_to_all(tiles, axis, split_axis=0, concat_axis=0, tiled=True), axis=0)
+    flat = x.reshape(-1, 128)
+    tiles = jnp.broadcast_to(flat[None], (n,) + flat.shape)
+    got = lax.all_to_all(tiles, axis, split_axis=0, concat_axis=0, tiled=True)
+    return jnp.sum(got, axis=0).reshape(x.shape)
 
 
 def swap_pair(x):
@@ -140,7 +142,19 @@
             eye = jnp.eye(gain.shape[0], dtype=gain.dtype)
             through = jnp.dot(eye + first_gain, gain, precision=lax.Precision.HIGHEST)
             columns = lax.dynamic_slice_in_dim(through, first, per_device, 1)
-            own = own + jnp.einsum("kj,kab->jab", columns, whole, precision=lax.Precision.HIGH)
+
+            def part(rows, cut=None):
+                base, src = own[:, rows], whole[:, rows]
+                if cut is not None:
+                    base, src = base[..., :cut], src[..., :cut]
+                return base + jnp.einsum("kj,k...->j...", columns, src, precision=lax.Precision.HIGH)
+
+            return (
+                part(slice(0, f_in)),
+                part(f_in + outs),
+                part(slice(f_in, f_in + outs)),
+                part(f_in + outs + 1, outs),
+            )
     return unpack(own, f_in, hid, outs)
 
 

time: 233 us -> 228 us (0.979)
  blocking collectives: 66.2 us -> 46.3 us
  waiting for transfers between devices: 70.5 us -> 82.4 us
  starting transfers between devices: 38.8 us -> 45.9 us
  other arithmetic: 9.93 us -> 4.14 us
    all_to_all x3 -> x2, blocking collectives: 40.9 us -> 21.2 us  [gather_sum(): got = lax.all_to_all(tiles, axis, split_axis=0, concat_axis=0, tiled=True)]
    all_to_all x1 -> x2, waiting for transfers between devices: 12.9 us -> 24.8 us  [gather_sum(): got = lax.all_to_all(tiles, axis, split_axis=0, concat_axis=0, tiled=True)]
    all_to_all x1 -> x2, starting transfers between devices: 8.23 us -> 15.2 us  [gather_sum(): got = lax.all_to_all(tiles, axis, split_axis=0, concat_axis=0, tiled=True)]
    all_to_all x4 -> x0, other arithmetic: 4.42 us -> none  [gather_sum(): lax.all_to_all(tiles, axis, split_axis=0, concat_axis=0, tiled=True)]
    dot_general x2 -> x1, matrix products: 4.31 us -> 0.77 us  [on_device(): jnp.einsum('kj,kab->jab', columns, whole, precision=lax.Precision.HIGH)]
    unnamed x34 -> x22, local copies, waits for them, and re-layouts: 4.57 us -> 1.45 us
  transfers between devices with their start and end apart: 7 -> 8, of which waited for: 5 -> 6; matrix products, arithmetic and copies ran while one was open for 4% -> 3% of each run, Pallas kernels for 0% -> 0%
where the time goes in v8:
time: 228 us; the launch traced here: 227 us
  waiting for transfers between devices  82.4 us (36%)
  blocking collectives  46.3 us (20%)
  starting transfers between devices  45.9 us (20%)
  between operations  15.2 us (7%)
  local copies, waits for them, and re-layouts  13.3 us (6%)
  matrix products  10.4 us (5%)
  Pallas kernels  9.15 us (4%)
  other arithmetic  4.14 us (2%)
    all_to_all x2, waiting for transfers between devices, predict(): got = lax.all_to_all(tiles, 'dp', split_axis=0, concat_axis=0, tiled=True)  55.9 us
    all_to_all x2, blocking collectives, collect(): lax.all_to_all(blocks, 'member', split_axis=0, concat_axis=0, tiled=True)  25.1 us
    all_to_all x2, waiting for transfers between devices, gather_sum(): got = lax.all_to_all(tiles, axis, split_axis=0, concat_axis=0, tiled=True)  24.8 us
    all_to_all x2, blocking collectives, gather_sum(): got = lax.all_to_all(tiles, axis, split_axis=0, concat_axis=0, tiled=True)  21.2 us
    all_to_all x2, starting transfers between devices, predict(): got = lax.all_to_all(tiles, 'dp', split_axis=0, concat_axis=0, tiled=True)  19 us
    all_to_all x2, starting transfers between devices, gather_sum(): got = lax.all_to_all(tiles, axis, split_axis=0, concat_axis=0, tiled=True)  15.2 us
    ppermute x3, starting transfers between devices, swap_pair(): return lax.ppermute(x, 'dp', [(i, i ^ 1) for i in range(n)])  11.7 us
    pallas_call x2, Pallas kernels, solve_spd(): pl.pallas_call(_eliminate, out_shape=jax.ShapeDtypeStruct(b.shape, b.dtype))  9.15 us
  transfers between devices with their start and end apart: 8, of which 6 were waited for; matrix products, arithmetic and copies ran while one was open for 3% of the time, Pallas kernels for 0%

profile of v8, /device:TPU:1, one launch (start us, length us, event | category | flops | bytes accessed | tf_op | source)
XLA Modules:
  0.0 226.8 jit_solution(5568358006338132556)
XLA Ops:
  7.2 0.7 bitcast_convert_fusion
  7.9 0.8 convert.16
  8.8 0.8 convert.17
  9.7 1.1 broadcast_in_dim.22
  10.8 14.4 %all-to-all-start = ((bf16[32,129,128]{2,1,0:T(8,128)(2,1)}), bf16[32,129,128]{2,1,0:T(8,128)(2,1)S(1)}, u32[]{:S(2)}, u32[]{:S(2)}) async-start(bf16[32,129,128]{2,1,0:T(8,128)(2,1)} %bitcast.2), calls=%async_computation | async-start | bytes 2228224 | tf_op jit(solution)/shard_map/all_to_all | solution.py:82
  25.5 0.7 copy.108
  26.2 2.1 collective-permute-start
  28.4 26.4 %all-to-all-done = bf16[32,129,128]{2,1,0:T(8,128)(2,1)S(1)} async-done(((bf16[32,129,128]{2,1,0:T(8,128)(2,1)}), bf16[32,129,128]{2,1,0:T(8,128)(2,1)S(1)}, u32[]{:S(2)}, u32[]{:S(2)}) %all-to-all-start) | async-done | bytes 1056800 | tf_op jit(solution)/shard_map/all_to_all | solution.py:82
  54.8 2.5 %fusion.10 = f32[64,512]{1,0:T(8,128)S(1)} fusion(f32[32,128]{1,0:T(8,128)S(1)} %bitcast.84, bf16[32,129,128]{2,1,0:T(8,128)(2,1)S(1)} %all-to-all-done, f32[64]{0:T(128)S(1)} %fusion.46, bf16[256,64]{0,1:T(8,128)(2,1)S(1)} %collective-permute-done, bf16[256,64]{0,1:T(8,128)(2,1)S(1)} %copy-done.7), kind=kOutput, calls=%fused_computation.11 | convolution fusion | flops 541229056 | bytes 1262080 | tf_op jit(solution)/shard_map/doh,sdh->os/dot_general | solution.py:90
  57.3 14.3 %all_to_all.40 = f32[16,4,512]{2,1,0:T(4,128)S(1)} all-to-all(f32[16,4,512]{2,1,0:T(4,128)S(1)} %reshape.166), channel_id=1, replica_groups=mesh['member'=16,'dp'=32] {'member'}, dimensions={0} | all-to-all | bytes 262144 | tf_op jit(solution)/shard_map/all_to_all | solution.py:98
  71.6 5.0 %collective-permute-start.1 = (f32[16,4,256]{2,0,1:T(8,128)S(1)}, f32[16,4,256]{2,0,1:T(8,128)S(1)}, u32[]{:S(2)}, u32[]{:S(2)}) collective-permute-start(f32[16,4,256]{2,0,1:T(8,128)S(1)} %copy.128), channel_id=1, source_target_pairs={{0,1},{1,0},{2,3},{3,2},{4,5},{5,4},{6,7},{7,6},{8,9},{9,8},{10,11... | collective-permute-start | bytes 196616 | tf_op jit(solution)/shard_map/ppermute | solution.py:73
  76.8 0.8 collective-permute-done.1
  77.9 0.2 convolution_bitcast_fusion.3
  78.1 0.3 convolution_bitcast_fusion.2
  78.5 11.0 %all_to_all.41 = f32[16,16,128]{2,1,0:T(8,128)S(1)} all-to-all(f32[16,16,128]{2,1,0:T(8,128)S(1)} %broadcast_in_dim.24), channel_id=1, replica_groups=mesh['member'=16,'dp'=32] {'member'}, dimensions={0} | all-to-all | bytes 262144 | tf_op jit(solution)/shard_map/all_to_all | solution.py:67
  89.5 0.7 broadcast_in_dim.25
  90.3 8.2 %all-to-all-start.3 = ((f32[32,16,128]{2,1,0:T(8,128)}), f32[32,16,128]{2,1,0:T(8,128)S(1)}, u32[]{:S(2)}, u32[]{:S(2)}) async-start(f32[32,16,128]{2,1,0:T(8,128)} %broadcast_in_dim.25), calls=%async_computation.3 | async-start | bytes 524288 | tf_op jit(solution)/shard_map/all_to_all | solution.py:67
  98.5 12.9 %all-to-all-done.3 = f32[32,16,128]{2,1,0:T(8,128)S(1)} async-done(((f32[32,16,128]{2,1,0:T(8,128)}), f32[32,16,128]{2,1,0:T(8,128)S(1)}, u32[]{:S(2)}, u32[]{:S(2)}) %all-to-all-start.3) | async-done | bytes 262176 | tf_op jit(solution)/shard_map/all_to_all | solution.py:67
  111.5 1.2 slice.140
  113.3 0.7 div.30.b_ref
  114.1 0.6 select_add_fusion.1.a_ref
  114.7 4.6 %shard_map.102 = f32[32,32]{1,0:T(8,128)} custom-call(f32[32,32]{1,0:T(8,128)} %select_add_fusion.1.a_ref, f32[32,32]{1,0:T(8,128)} %div.30.b_ref), custom_call_target="tpu_custom_call" | custom-call | tf_op jit(solution)/shard_map/pallas_call | solution.py:44
  119.3 2.1 copy.110
  121.3 0.8 convolution_add_fusion
  122.2 1.1 broadcast_in_dim.26
  123.3 4.6 %all-to-all-start.4 = ((bf16[32,129,128]{2,1,0:T(8,128)(2,1)}), bf16[32,129,128]{2,1,0:T(8,128)(2,1)S(1)}, u32[]{:S(2)}, u32[]{:S(2)}) async-start(bf16[32,129,128]{2,1,0:T(8,128)(2,1)} %bitcast.18), calls=%async_computation.4 | async-start | bytes 2228224 | tf_op jit(solution)/shard_map/all_to_all | solution.py:82
  127.9 29.5 %all-to-all-done.4 = bf16[32,129,128]{2,1,0:T(8,128)(2,1)S(1)} async-done(((bf16[32,129,128]{2,1,0:T(8,128)(2,1)}), bf16[32,129,128]{2,1,0:T(8,128)(2,1)S(1)}, u32[]{:S(2)}, u32[]{:S(2)}) %all-to-all-start.4) | async-done | bytes 1056800 | tf_op jit(solution)/shard_map/all_to_all | solution.py:82
  157.5 3.1 %fusion.11 = f32[64,512]{1,0:T(8,128)} fusion(f32[32,128]{1,0:T(8,128)S(1)} %bitcast.85, bf16[32,129,128]{2,1,0:T(8,128)(2,1)S(1)} %all-to-all-done.4, f32[64]{0:T(128)S(1)} %fusion.47, bf16[256,64]{0,1:T(8,128)(2,1)S(1)} %collective-permute-done, bf16[256,64]{0,1:T(8,128)(2,1)S(1)} %copy-done.7), kind=kOutput, calls=%fused_computation.12 | convolution fusion | flops 541229056 | bytes 1262080 | tf_op jit(solution)/shard_map/doh,sdh->os/dot_general | solution.py:90
  160.6 0.9 reshape.168
  161.5 10.9 %all_to_all.42 = f32[16,4,512]{2,1,0:T(4,128)S(1)} all-to-all(f32[16,4,512]{2,1,0:T(4,128)S(1)} %reshape.168), channel_id=1, replica_groups=mesh['member'=16,'dp'=32] {'member'}, dimensions={0} | all-to-all | bytes 262144 | tf_op jit(solution)/shard_map/all_to_all | solution.py:98
  172.4 4.5 %collective-permute-start.2 = (f32[16,4,256]{2,0,1:T(8,128)S(1)}, f32[16,4,256]{2,0,1:T(8,128)S(1)}, u32[]{:S(2)}, u32[]{:S(2)}) collective-permute-start(f32[16,4,256]{2,0,1:T(8,128)S(1)} %copy.130), channel_id=1, source_target_pairs={{0,1},{1,0},{2,3},{3,2},{4,5},{5,4},{6,7},{7,6},{8,9},{9,8},{10,11... | collective-permute-start | bytes 196616 | tf_op jit(solution)/shard_map/ppermute | solution.py:73
  177.0 0.9 collective-permute-done.2
  178.4 0.3 convolution_bitcast_fusion
  178.8 10.2 %all_to_all.43 = f32[16,16,128]{2,1,0:T(8,128)S(1)} all-to-all(f32[16,16,128]{2,1,0:T(8,128)S(1)} %broadcast_in_dim.28), channel_id=1, replica_groups=mesh['member'=16,'dp'=32] {'member'}, dimensions={0} | all-to-all | bytes 262144 | tf_op jit(solution)/shard_map/all_to_all | solution.py:67
  189.0 0.7 broadcast_in_dim.29
  189.7 7.0 %all-to-all-start.7 = ((f32[32,16,128]{2,1,0:T(8,128)}), f32[32,16,128]{2,1,0:T(8,128)S(1)}, u32[]{:S(2)}, u32[]{:S(2)}) async-start(f32[32,16,128]{2,1,0:T(8,128)} %broadcast_in_dim.29), calls=%async_computation.7 | async-start | bytes 524288 | tf_op jit(solution)/shard_map/all_to_all | solution.py:67
  196.7 1.0 fusion.53
  197.7 11.9 %all-to-all-done.7 = f32[32,16,128]{2,1,0:T(8,128)S(1)} async-done(((f32[32,16,128]{2,1,0:T(8,128)}), f32[32,16,128]{2,1,0:T(8,128)S(1)}, u32[]{:S(2)}, u32[]{:S(2)}) %all-to-all-start.7) | async-done | bytes 262176 | tf_op jit(solution)/shard_map/all_to_all | solution.py:67
  209.7 0.7 div.35.b_ref
  210.5 0.6 select_add_fusion.a_ref
  211.1 4.6 %shard_map.103 = f32[32,32]{1,0:T(8,128)} custom-call(f32[32,32]{1,0:T(8,128)} %select_add_fusion.a_ref, f32[32,32]{1,0:T(8,128)} %div.35.b_ref), custom_call_target="tpu_custom_call" | custom-call | tf_op jit(solution)/shard_map/pallas_call | solution.py:44
  215.6 0.9 fusion.40
  216.6 0.4 convolution_add_fusion.1
  217.0 0.4 convolution_add_fusion.2
  217.3 0.7 convolution_add_fusion.4
  218.0 0.6 copy.123
  218.7 0.6 copy.124
  219.3 0.7 convolution_add_fusion.3
  (67 shorter events, 1.8 us)
Async XLA Ops:
  7.2 18.3 %copy-start.5 = (f32[2,128]{1,0:T(2,128)S(1)}, f32[2,128]{1,0:T(2,128)}, u32[]{:S(2)}) copy-start(f32[2,128]{1,0:T(2,128)} %param.11) | copy-start | bytes 3076
  7.2 18.1 %copy-start = (f32[2,64,128]{2,1,0:T(8,128)S(1)}, f32[2,64,128]{2,1,0:T(8,128)}, u32[]{:S(2)}) copy-start(f32[2,64,128]{2,1,0:T(8,128)} %param.10) | copy-start | bytes 196612
  7.2 18.2 %copy-start.1 = (f32[2,64,128]{2,1,0:T(8,128)S(1)}, f32[2,64,128]{2,1,0:T(8,128)}, u32[]{:S(2)}) copy-start(f32[2,64,128]{2,1,0:T(8,128)} %param.12) | copy-start | bytes 196612
  7.2 18.2 %copy-start.6 = (f32[2,64]{1,0:T(2,128)S(1)}, f32[2,64]{1,0:T(2,128)}, u32[]{:S(2)}) copy-start(f32[2,64]{1,0:T(2,128)} %param.13) | copy-start | bytes 1540
  9.6 16.6 %copy-start.7 = (bf16[256,64]{0,1:T(8,128)(2,1)S(1)}, bf16[256,64]{0,1:T(8,128)(2,1)}, u32[]{:S(2)}) copy-start(bf16[256,64]{0,1:T(8,128)(2,1)} %param.7) | copy-start | bytes 98308
  10.8 44.0 %all-to-all-start = ((bf16[32,129,128]{2,1,0:T(8,128)(2,1)}), bf16[32,129,128]{2,1,0:T(8,128)(2,1)S(1)}, u32[]{:S(2)}, u32[]{:S(2)}) async-start(bf16[32,129,128]{2,1,0:T(8,128)(2,1)} %bitcast.2), calls=%async_computation | async-start | bytes 2228224 | tf_op jit(solution)/shard_map/all_to_all | solution.py:82
  25.2 86.2 %all-gather.2.cloned.1.call-start = ((), (), s32[]{:S(2)}) async-start(), calls=%async_computation.8 | async-start | bytes 2367488 | tf_op jit(solution)/shard_map/all_gather | solution.py:116
  26.2 28.6 %collective-permute-start = (bf16[256,64]{0,1:T(8,128)(2,1)S(1)}, bf16[256,64]{0,1:T(8,128)(2,1)S(1)}, u32[]{:S(2)}, u32[]{:S(2)}) collective-permute-start(bf16[256,64]{0,1:T(8,128)(2,1)S(1)} %copy-done.7), channel_id=1, source_target_pairs={{0,1},{1,0},{2,3},{3,2},{4,5},{5,4},{6,7},{7,6},{8,9},{9,8},{10,11... | collective-permute-start | bytes 98312 | tf_op jit(solution)/shard_map/ppermute | solution.py:73
  54.8 21.9 %copy-start.3 = (bf16[2,32,4,256]{3,2,1,0:T(4,128)(2,1)S(1)}, bf16[2,32,4,256]{3,2,1,0:T(4,128)(2,1)}, u32[]{:S(2)}) copy-start(bf16[2,32,4,256]{3,2,1,0:T(4,128)(2,1)} %param.9) | copy-start | bytes 393220
  54.8 22.8 %copy-start.4 = (f32[4,256]{1,0:T(4,128)S(1)}, f32[4,256]{1,0:T(4,128)}, u32[]{:S(2)}) copy-start(f32[4,256]{1,0:T(4,128)} %param.8) | copy-start | bytes 12292
  71.6 5.9 %collective-permute-start.1 = (f32[16,4,256]{2,0,1:T(8,128)S(1)}, f32[16,4,256]{2,0,1:T(8,128)S(1)}, u32[]{:S(2)}, u32[]{:S(2)}) collective-permute-start(f32[16,4,256]{2,0,1:T(8,128)S(1)} %copy.128), channel_id=1, source_target_pairs={{0,1},{1,0},{2,3},{3,2},{4,5},{5,4},{6,7},{7,6},{8,9},{9,8},{10,11... | collective-permute-start | bytes 196616 | tf_op jit(solution)/shard_map/ppermute | solution.py:73
  90.3 21.1 %all-to-all-start.3 = ((f32[32,16,128]{2,1,0:T(8,128)}), f32[32,16,128]{2,1,0:T(8,128)S(1)}, u32[]{:S(2)}, u32[]{:S(2)}) async-start(f32[32,16,128]{2,1,0:T(8,128)} %broadcast_in_dim.25), calls=%async_computation.3 | async-start | bytes 524288 | tf_op jit(solution)/shard_map/all_to_all | solution.py:67
  119.3 2.1 copy-start.2
  123.3 34.1 %all-to-all-start.4 = ((bf16[32,129,128]{2,1,0:T(8,128)(2,1)}), bf16[32,129,128]{2,1,0:T(8,128)(2,1)S(1)}, u32[]{:S(2)}, u32[]{:S(2)}) async-start(bf16[32,129,128]{2,1,0:T(8,128)(2,1)} %bitcast.18), calls=%async_computation.4 | async-start | bytes 2228224 | tf_op jit(solution)/shard_map/all_to_all | solution.py:82
  172.4 5.4 %collective-permute-start.2 = (f32[16,4,256]{2,0,1:T(8,128)S(1)}, f32[16,4,256]{2,0,1:T(8,128)S(1)}, u32[]{:S(2)}, u32[]{:S(2)}) collective-permute-start(f32[16,4,256]{2,0,1:T(8,128)S(1)} %copy.130), channel_id=1, source_target_pairs={{0,1},{1,0},{2,3},{3,2},{4,5},{5,4},{6,7},{7,6},{8,9},{9,8},{10,11... | collective-permute-start | bytes 196616 | tf_op jit(solution)/shard_map/ppermute | solution.py:73
  189.7 19.9 %all-to-all-start.7 = ((f32[32,16,128]{2,1,0:T(8,128)}), f32[32,16,128]{2,1,0:T(8,128)S(1)}, u32[]{:S(2)}, u32[]{:S(2)}) async-start(f32[32,16,128]{2,1,0:T(8,128)} %broadcast_in_dim.29), calls=%async_computation.7 | async-start | bytes 524288 | tf_op jit(solution)/shard_map/all_to_all | solution.py:67
Sparse Core Ops, SparseCore 0:
  28.2 67.6 all-gather.1

commit v9 on v8

--- a/solution.py
+++ b/solution.py
@@ -1,3 +1,5 @@
+import functools
+
 import jax
 import jax.numpy as jnp
 from jax import lax
@@ -17,31 +19,25 @@
     return lax.linalg.triangular_solve(factor, middle, left_side=True, lower=True, transpose_a=True)
 
 
-def _eliminate(a_ref, b_ref, o_ref):
-    n = a_ref.shape[0]
-    a = a_ref[...]
-    b = b_ref[...]
+def _eliminate(s_ref, o_ref, *, scale, ridge):
+    a = s_ref[0] * scale
+    b = s_ref[1] * scale
+    n = a.shape[0]
     rows = lax.broadcasted_iota(jnp.int32, a.shape, 0)
     cols = lax.broadcasted_iota(jnp.int32, a.shape, 1)
-    rows_b = lax.broadcasted_iota(jnp.int32, b.shape, 0)
-
-    def step(k, carry):
-        a, b = carry
-        row_a = jnp.sum(jnp.where(rows == k, a, 0.0), axis=0, keepdims=True)
-        row_b = jnp.sum(jnp.where(rows_b == k, b, 0.0), axis=0, keepdims=True)
-        col = jnp.sum(jnp.where(cols == k, a, 0.0), axis=1, keepdims=True)
-        pivot = jnp.sum(jnp.where(cols[:1] == k, row_a, 0.0), axis=1, keepdims=True)
-        ra = row_a / pivot
-        rb = row_b / pivot
+    a = jnp.where(rows == cols, a + ridge, a)
+    for k in range(n):
+        pivot = a[k : k + 1, k : k + 1]
+        ra = a[k : k + 1, :] / pivot
+        rb = b[k : k + 1, :] / pivot
+        col = a[:, k : k + 1]
         a = jnp.where(rows == k, ra, a - col * ra)
-        b = jnp.where(rows_b == k, rb, b - col * rb)
-        return a, b
-
-    a, b = lax.fori_loop(0, n, step, (a, b), unroll=True)
+        b = jnp.where(rows == k, rb, b - col * rb)
     o_ref[...] = b
 
-def solve_spd(a, b):
-    return pl.pallas_call(_eliminate, out_shape=jax.ShapeDtypeStruct(b.shape, b.dtype))(a, b)
+def solve_spd(sums, scale, ridge):
+    kernel = functools.partial(_eliminate, scale=scale, ridge=ridge)
+    return pl.pallas_call(kernel, out_shape=jax.ShapeDtypeStruct(sums.shape[1:], sums.dtype))(sums)
 
 def pack(w_in, b_in, w_out, b_out):
     n, hid = w_in.shape[0], w_in.shape[2]
@@ -132,8 +128,7 @@
         sums = gather_sum(gather_sum(jnp.stack([gram_part, cross_part]), "member"), "dp")
         if update == 0:
             sums = sums + whole[0, 0, 0] * 0
-        eye = jnp.eye(sums.shape[1], dtype=sums.dtype)
-        gain = solve_spd(sums[0] / count + ridge_level * eye, sums[1] / count)
+        gain = solve_spd(sums, 1.0 / count, ridge_level)
         if update == 0:
             first_gain = gain
             columns = lax.dynamic_slice_in_dim(gain, first, per_device, 1)

time: 228 us -> 225 us (0.987)
  no operation moved by 1% of the time
where the time goes in v9:
time: 225 us; the launch traced here: 224 us
  waiting for transfers between devices  82.4 us (37%)
  blocking collectives  46.3 us (21%)
  starting transfers between devices  45.9 us (20%)
  between operations  15.2 us (7%)
  local copies, waits for them, and re-layouts  13.1 us (6%)
  matrix products  10.4 us (5%)
  Pallas kernels  8.01 us (4%)
  other arithmetic  2.9 us (1%)
    all_to_all x2, waiting for transfers between devices, predict(): got = lax.all_to_all(tiles, 'dp', split_axis=0, concat_axis=0, tiled=True)  55.9 us
    all_to_all x2, blocking collectives, collect(): lax.all_to_all(blocks, 'member', split_axis=0, concat_axis=0, tiled=True)  25.1 us
    all_to_all x2, waiting for transfers between devices, gather_sum(): got = lax.all_to_all(tiles, axis, split_axis=0, concat_axis=0, tiled=True)  24.8 us
    all_to_all x2, blocking collectives, gather_sum(): got = lax.all_to_all(tiles, axis, split_axis=0, concat_axis=0, tiled=True)  21.2 us
    all_to_all x2, starting transfers between devices, predict(): got = lax.all_to_all(tiles, 'dp', split_axis=0, concat_axis=0, tiled=True)  19 us
    all_to_all x2, starting transfers between devices, gather_sum(): got = lax.all_to_all(tiles, axis, split_axis=0, concat_axis=0, tiled=True)  15.2 us
    ppermute x3, starting transfers between devices, swap_pair(): return lax.ppermute(x, 'dp', [(i, i ^ 1) for i in range(n)])  11.7 us
    pallas_call x2, Pallas kernels, solve_spd(): pl.pallas_call(kernel, out_shape=jax.ShapeDtypeStruct(sums.shape[1:], sum...  8.01 us
  transfers between devices with their start and end apart: 8, of which 6 were waited for; matrix products, arithmetic and copies ran while one was open for 3% of the time, Pallas kernels for 0%

profile of v9, /device:TPU:1, one launch (start us, length us, event | category | flops | bytes accessed | tf_op | source)
XLA Modules:
  0.0 224.3 jit_solution(12712020081994514263)
XLA Ops:
  7.2 0.7 bitcast_convert_fusion
  7.9 0.8 convert.16
  8.8 0.8 convert.17
  9.7 1.1 broadcast_in_dim.22
  10.8 14.4 %all-to-all-start = ((bf16[32,129,128]{2,1,0:T(8,128)(2,1)}), bf16[32,129,128]{2,1,0:T(8,128)(2,1)S(1)}, u32[]{:S(2)}, u32[]{:S(2)}) async-start(bf16[32,129,128]{2,1,0:T(8,128)(2,1)} %bitcast.2), calls=%async_computation | async-start | bytes 2228224 | tf_op jit(solution)/shard_map/all_to_all | solution.py:78
  25.5 0.7 copy.108
  26.2 2.1 collective-permute-start
  28.4 26.4 %all-to-all-done = bf16[32,129,128]{2,1,0:T(8,128)(2,1)S(1)} async-done(((bf16[32,129,128]{2,1,0:T(8,128)(2,1)}), bf16[32,129,128]{2,1,0:T(8,128)(2,1)S(1)}, u32[]{:S(2)}, u32[]{:S(2)}) %all-to-all-start) | async-done | bytes 1056800 | tf_op jit(solution)/shard_map/all_to_all | solution.py:78
  54.8 2.5 %fusion.10 = f32[64,512]{1,0:T(8,128)S(1)} fusion(f32[32,128]{1,0:T(8,128)S(1)} %bitcast.84, bf16[32,129,128]{2,1,0:T(8,128)(2,1)S(1)} %all-to-all-done, f32[64]{0:T(128)S(1)} %fusion.46, bf16[256,64]{0,1:T(8,128)(2,1)S(1)} %collective-permute-done, bf16[256,64]{0,1:T(8,128)(2,1)S(1)} %copy-done.7), kind=kOutput, calls=%fused_computation.11 | convolution fusion | flops 541229056 | bytes 1262080 | tf_op jit(solution)/shard_map/doh,sdh->os/dot_general | solution.py:86
  57.3 14.3 %all_to_all.40 = f32[16,4,512]{2,1,0:T(4,128)S(1)} all-to-all(f32[16,4,512]{2,1,0:T(4,128)S(1)} %reshape.148), channel_id=1, replica_groups=mesh['member'=16,'dp'=32] {'member'}, dimensions={0} | all-to-all | bytes 262144 | tf_op jit(solution)/shard_map/all_to_all | solution.py:94
  71.6 5.0 %collective-permute-start.1 = (f32[16,4,256]{2,0,1:T(8,128)S(1)}, f32[16,4,256]{2,0,1:T(8,128)S(1)}, u32[]{:S(2)}, u32[]{:S(2)}) collective-permute-start(f32[16,4,256]{2,0,1:T(8,128)S(1)} %copy.128), channel_id=1, source_target_pairs={{0,1},{1,0},{2,3},{3,2},{4,5},{5,4},{6,7},{7,6},{8,9},{9,8},{10,11... | collective-permute-start | bytes 196616 | tf_op jit(solution)/shard_map/ppermute | solution.py:69
  76.8 0.8 collective-permute-done.1
  77.7 0.1 copy.101
  77.9 0.2 convolution_bitcast_fusion.3
  78.1 0.3 convolution_bitcast_fusion.2
  78.5 11.0 %all_to_all.41 = f32[16,16,128]{2,1,0:T(8,128)S(1)} all-to-all(f32[16,16,128]{2,1,0:T(8,128)S(1)} %broadcast_in_dim.24), channel_id=1, replica_groups=mesh['member'=16,'dp'=32] {'member'}, dimensions={0} | all-to-all | bytes 262144 | tf_op jit(solution)/shard_map/all_to_all | solution.py:63
  89.5 0.7 broadcast_in_dim.25
  90.2 8.2 %all-to-all-start.3 = ((f32[32,16,128]{2,1,0:T(8,128)}), f32[32,16,128]{2,1,0:T(8,128)S(1)}, u32[]{:S(2)}, u32[]{:S(2)}) async-start(f32[32,16,128]{2,1,0:T(8,128)} %broadcast_in_dim.25), calls=%async_computation.3 | async-start | bytes 524288 | tf_op jit(solution)/shard_map/all_to_all | solution.py:63
  98.4 12.9 %all-to-all-done.3 = f32[32,16,128]{2,1,0:T(8,128)S(1)} async-done(((f32[32,16,128]{2,1,0:T(8,128)}), f32[32,16,128]{2,1,0:T(8,128)S(1)}, u32[]{:S(2)}, u32[]{:S(2)}) %all-to-all-start.3) | async-done | bytes 262176 | tf_op jit(solution)/shard_map/all_to_all | solution.py:63
  111.4 1.2 slice.120
  113.3 0.7 add.105.s_ref
  114.0 4.0 %shard_map.102 = f32[32,32]{1,0:T(8,128)} custom-call(f32[2,32,32]{2,1,0:T(8,128)} %add.105.s_ref), custom_call_target="tpu_custom_call" | custom-call | tf_op jit(solution)/shard_map/pallas_call | solution.py:40
  118.0 2.1 copy.110
  120.1 0.8 convolution_add_fusion
  120.9 1.1 broadcast_in_dim.26
  122.0 4.6 %all-to-all-start.4 = ((bf16[32,129,128]{2,1,0:T(8,128)(2,1)}), bf16[32,129,128]{2,1,0:T(8,128)(2,1)S(1)}, u32[]{:S(2)}, u32[]{:S(2)}) async-start(bf16[32,129,128]{2,1,0:T(8,128)(2,1)} %bitcast.18), calls=%async_computation.4 | async-start | bytes 2228224 | tf_op jit(solution)/shard_map/all_to_all | solution.py:78
  126.6 29.5 %all-to-all-done.4 = bf16[32,129,128]{2,1,0:T(8,128)(2,1)S(1)} async-done(((bf16[32,129,128]{2,1,0:T(8,128)(2,1)}), bf16[32,129,128]{2,1,0:T(8,128)(2,1)S(1)}, u32[]{:S(2)}, u32[]{:S(2)}) %all-to-all-start.4) | async-done | bytes 1056800 | tf_op jit(solution)/shard_map/all_to_all | solution.py:78
  156.2 3.1 %fusion.11 = f32[64,512]{1,0:T(8,128)} fusion(f32[32,128]{1,0:T(8,128)S(1)} %bitcast.85, bf16[32,129,128]{2,1,0:T(8,128)(2,1)S(1)} %all-to-all-done.4, f32[64]{0:T(128)S(1)} %fusion.47, bf16[256,64]{0,1:T(8,128)(2,1)S(1)} %collective-permute-done, bf16[256,64]{0,1:T(8,128)(2,1)S(1)} %copy-done.7), kind=kOutput, calls=%fused_computation.12 | convolution fusion | flops 541229056 | bytes 1262080 | tf_op jit(solution)/shard_map/doh,sdh->os/dot_general | solution.py:86
  159.3 0.9 reshape.150
  160.2 10.9 %all_to_all.42 = f32[16,4,512]{2,1,0:T(4,128)S(1)} all-to-all(f32[16,4,512]{2,1,0:T(4,128)S(1)} %reshape.150), channel_id=1, replica_groups=mesh['member'=16,'dp'=32] {'member'}, dimensions={0} | all-to-all | bytes 262144 | tf_op jit(solution)/shard_map/all_to_all | solution.py:94
  171.1 4.5 %collective-permute-start.2 = (f32[16,4,256]{2,0,1:T(8,128)S(1)}, f32[16,4,256]{2,0,1:T(8,128)S(1)}, u32[]{:S(2)}, u32[]{:S(2)}) collective-permute-start(f32[16,4,256]{2,0,1:T(8,128)S(1)} %copy.130), channel_id=1, source_target_pairs={{0,1},{1,0},{2,3},{3,2},{4,5},{5,4},{6,7},{7,6},{8,9},{9,8},{10,11... | collective-permute-start | bytes 196616 | tf_op jit(solution)/shard_map/ppermute | solution.py:69
  175.7 0.9 collective-permute-done.2
  176.8 0.2 convolution_bitcast_fusion.1
  177.1 0.3 convolution_bitcast_fusion
  177.5 10.2 %all_to_all.43 = f32[16,16,128]{2,1,0:T(8,128)S(1)} all-to-all(f32[16,16,128]{2,1,0:T(8,128)S(1)} %broadcast_in_dim.28), channel_id=1, replica_groups=mesh['member'=16,'dp'=32] {'member'}, dimensions={0} | all-to-all | bytes 262144 | tf_op jit(solution)/shard_map/all_to_all | solution.py:63
  187.7 0.7 broadcast_in_dim.29
  188.4 7.0 %all-to-all-start.7 = ((f32[32,16,128]{2,1,0:T(8,128)}), f32[32,16,128]{2,1,0:T(8,128)S(1)}, u32[]{:S(2)}, u32[]{:S(2)}) async-start(f32[32,16,128]{2,1,0:T(8,128)} %broadcast_in_dim.29), calls=%async_computation.7 | async-start | bytes 524288 | tf_op jit(solution)/shard_map/all_to_all | solution.py:63
  195.4 1.0 fusion.53
  196.4 11.9 %all-to-all-done.7 = f32[32,16,128]{2,1,0:T(8,128)S(1)} async-done(((f32[32,16,128]{2,1,0:T(8,128)}), f32[32,16,128]{2,1,0:T(8,128)S(1)}, u32[]{:S(2)}, u32[]{:S(2)}) %all-to-all-start.7) | async-done | bytes 262176 | tf_op jit(solution)/shard_map/all_to_all | solution.py:63
  208.4 0.7 reshape.151.s_ref
  209.1 4.0 %shard_map.103 = f32[32,32]{1,0:T(8,128)} custom-call(f32[2,32,32]{2,1,0:T(8,128)} %reshape.151.s_ref), custom_call_target="tpu_custom_call" | custom-call | tf_op jit(solution)/shard_map/pallas_call | solution.py:40
  213.1 0.9 fusion.40
  214.0 0.4 convolution_add_fusion.1
  214.4 0.4 convolution_add_fusion.2
  214.8 0.7 convolution_add_fusion.4
  215.5 0.6 copy.123
  216.1 0.6 copy.124
  216.8 0.7 convolution_add_fusion.3
  (61 shorter events, 1.4 us)
Async XLA Ops:
  7.2 18.3 %copy-start.5 = (f32[2,128]{1,0:T(2,128)S(1)}, f32[2,128]{1,0:T(2,128)}, u32[]{:S(2)}) copy-start(f32[2,128]{1,0:T(2,128)} %param.11) | copy-start | bytes 3076
  7.2 18.1 %copy-start = (f32[2,64,128]{2,1,0:T(8,128)S(1)}, f32[2,64,128]{2,1,0:T(8,128)}, u32[]{:S(2)}) copy-start(f32[2,64,128]{2,1,0:T(8,128)} %param.10) | copy-start | bytes 196612
  7.2 18.2 %copy-start.1 = (f32[2,64,128]{2,1,0:T(8,128)S(1)}, f32[2,64,128]{2,1,0:T(8,128)}, u32[]{:S(2)}) copy-start(f32[2,64,128]{2,1,0:T(8,128)} %param.12) | copy-start | bytes 196612
  7.2 18.2 %copy-start.6 = (f32[2,64]{1,0:T(2,128)S(1)}, f32[2,64]{1,0:T(2,128)}, u32[]{:S(2)}) copy-start(f32[2,64]{1,0:T(2,128)} %param.13) | copy-start | bytes 1540
  9.6 16.6 %copy-start.7 = (bf16[256,64]{0,1:T(8,128)(2,1)S(1)}, bf16[256,64]{0,1:T(8,128)(2,1)}, u32[]{:S(2)}) copy-start(bf16[256,64]{0,1:T(8,128)(2,1)} %param.7) | copy-start | bytes 98308
  10.8 44.0 %all-to-all-start = ((bf16[32,129,128]{2,1,0:T(8,128)(2,1)}), bf16[32,129,128]{2,1,0:T(8,128)(2,1)S(1)}, u32[]{:S(2)}, u32[]{:S(2)}) async-start(bf16[32,129,128]{2,1,0:T(8,128)(2,1)} %bitcast.2), calls=%async_computation | async-start | bytes 2228224 | tf_op jit(solution)/shard_map/all_to_all | solution.py:78
  25.2 86.2 %all-gather.2.cloned.1.call-start = ((), (), s32[]{:S(2)}) async-start(), calls=%async_computation.8 | async-start | bytes 2367488 | tf_op jit(solution)/shard_map/all_gather | solution.py:112
  26.2 28.6 %collective-permute-start = (bf16[256,64]{0,1:T(8,128)(2,1)S(1)}, bf16[256,64]{0,1:T(8,128)(2,1)S(1)}, u32[]{:S(2)}, u32[]{:S(2)}) collective-permute-start(bf16[256,64]{0,1:T(8,128)(2,1)S(1)} %copy-done.7), channel_id=1, source_target_pairs={{0,1},{1,0},{2,3},{3,2},{4,5},{5,4},{6,7},{7,6},{8,9},{9,8},{10,11... | collective-permute-start | bytes 98312 | tf_op jit(solution)/shard_map/ppermute | solution.py:69
  54.8 21.9 %copy-start.3 = (bf16[2,32,4,256]{3,2,1,0:T(4,128)(2,1)S(1)}, bf16[2,32,4,256]{3,2,1,0:T(4,128)(2,1)}, u32[]{:S(2)}) copy-start(bf16[2,32,4,256]{3,2,1,0:T(4,128)(2,1)} %param.9) | copy-start | bytes 393220
  54.8 22.8 %copy-start.4 = (f32[4,256]{1,0:T(4,128)S(1)}, f32[4,256]{1,0:T(4,128)}, u32[]{:S(2)}) copy-start(f32[4,256]{1,0:T(4,128)} %param.8) | copy-start | bytes 12292
  71.6 5.9 %collective-permute-start.1 = (f32[16,4,256]{2,0,1:T(8,128)S(1)}, f32[16,4,256]{2,0,1:T(8,128)S(1)}, u32[]{:S(2)}, u32[]{:S(2)}) collective-permute-start(f32[16,4,256]{2,0,1:T(8,128)S(1)} %copy.128), channel_id=1, source_target_pairs={{0,1},{1,0},{2,3},{3,2},{4,5},{5,4},{6,7},{7,6},{8,9},{9,8},{10,11... | collective-permute-start | bytes 196616 | tf_op jit(solution)/shard_map/ppermute | solution.py:69
  90.2 21.1 %all-to-all-start.3 = ((f32[32,16,128]{2,1,0:T(8,128)}), f32[32,16,128]{2,1,0:T(8,128)S(1)}, u32[]{:S(2)}, u32[]{:S(2)}) async-start(f32[32,16,128]{2,1,0:T(8,128)} %broadcast_in_dim.25), calls=%async_computation.3 | async-start | bytes 524288 | tf_op jit(solution)/shard_map/all_to_all | solution.py:63
  118.0 2.1 copy-start.2
  122.0 34.1 %all-to-all-start.4 = ((bf16[32,129,128]{2,1,0:T(8,128)(2,1)}), bf16[32,129,128]{2,1,0:T(8,128)(2,1)S(1)}, u32[]{:S(2)}, u32[]{:S(2)}) async-start(bf16[32,129,128]{2,1,0:T(8,128)(2,1)} %bitcast.18), calls=%async_computation.4 | async-start | bytes 2228224 | tf_op jit(solution)/shard_map/all_to_all | solution.py:78
  171.1 5.4 %collective-permute-start.2 = (f32[16,4,256]{2,0,1:T(8,128)S(1)}, f32[16,4,256]{2,0,1:T(8,128)S(1)}, u32[]{:S(2)}, u32[]{:S(2)}) collective-permute-start(f32[16,4,256]{2,0,1:T(8,128)S(1)} %copy.130), channel_id=1, source_target_pairs={{0,1},{1,0},{2,3},{3,2},{4,5},{5,4},{6,7},{7,6},{8,9},{9,8},{10,11... | collective-permute-start | bytes 196616 | tf_op jit(solution)/shard_map/ppermute | solution.py:69
  188.4 19.9 %all-to-all-start.7 = ((f32[32,16,128]{2,1,0:T(8,128)}), f32[32,16,128]{2,1,0:T(8,128)S(1)}, u32[]{:S(2)}, u32[]{:S(2)}) async-start(f32[32,16,128]{2,1,0:T(8,128)} %broadcast_in_dim.29), calls=%async_computation.7 | async-start | bytes 524288 | tf_op jit(solution)/shard_map/all_to_all | solution.py:63
Sparse Core Ops, SparseCore 0:
  28.2 67.6 all-gather.1

commit v10 on v9

--- a/solution.py
+++ b/solution.py
@@ -62,6 +62,11 @@
     tiles = jnp.broadcast_to(flat[None], (n,) + flat.shape)
     got = lax.all_to_all(tiles, axis, split_axis=0, concat_axis=0, tiled=True)
     return jnp.sum(got, axis=0).reshape(x.shape)
+
+
+def combine(columns, stack):
+    expand = (slice(None), slice(None)) + (None,) * (stack.ndim - 1)
+    return jnp.sum(columns[expand] * stack[:, None], axis=0)
 
 
 def swap_pair(x):
@@ -132,7 +137,7 @@
         if update == 0:
             first_gain = gain
             columns = lax.dynamic_slice_in_dim(gain, first, per_device, 1)
-            own = own + jnp.einsum("kj,kab->jab", columns, whole, precision=lax.Precision.HIGH)
+            own = own + combine(columns, whole)
         else:
             eye = jnp.eye(gain.shape[0], dtype=gain.dtype)
             through = jnp.dot(eye + first_gain, gain, precision=lax.Precision.HIGHEST)
@@ -142,7 +147,7 @@
                 base, src = own[:, rows], whole[:, rows]
                 if cut is not None:
                     base, src = base[..., :cut], src[..., :cut]
-                return base + jnp.einsum("kj,k...->j...", columns, src, precision=lax.Precision.HIGH)
+                return base + combine(columns, src)
 
             return (
                 part(slice(0, f_in)),

time: 225 us -> 230 us (1.022)
  blocking collectives: 46.3 us -> 36.9 us
  other arithmetic: 2.9 us -> 10.8 us
  waiting for transfers between devices: 82.4 us -> 88.6 us
  matrix products: 10.4 us -> 6.84 us
  starting transfers between devices: 45.9 us -> 49.4 us
    all_to_all x2 -> x1, blocking collectives: 21.2 us -> 11.3 us  [gather_sum(): got = lax.all_to_all(tiles, axis, split_axis=0, concat_axis=0, tiled=True)]
    all_to_all x2 -> x3, waiting for transfers between devices: 24.8 us -> 30.8 us  [gather_sum(): got = lax.all_to_all(tiles, axis, split_axis=0, concat_axis=0, tiled=True)]
    reduce_sum x0 -> x4, other arithmetic: none -> 4.08 us  [combine(): return jnp.sum(columns[expand] * stack[:, None], axis=0)]
    all_to_all x2 -> x3, starting transfers between devices: 15.2 us -> 18.4 us  [gather_sum(): got = lax.all_to_all(tiles, axis, split_axis=0, concat_axis=0, tiled=True)]
    add x0 -> x4, other arithmetic: none -> 3.17 us  [the longest x3 3.15 us: part(): return base + combine(columns, src)]
    dot_general x5 -> x0, matrix products: 2.89 us -> none  [the longest x4 2.13 us: part(): jnp.einsum('kj,k...->j...', columns, src, precision=lax.Precision.HIGH)]
  transfers between devices with their start and end apart: 8 -> 9, of which waited for: 6 -> 7; matrix products, arithmetic and copies ran while one was open for 3% -> 3% of each run, Pallas kernels for 0% -> 0%
where the time goes in v10:
time: 230 us; the launch traced here: 229 us
  waiting for transfers between devices  88.6 us (39%)
  starting transfers between devices  49.4 us (21%)
  blocking collectives  36.9 us (16%)
  between operations  15.2 us (7%)
  local copies, waits for them, and re-layouts  13.2 us (6%)
  other arithmetic  10.8 us (5%)
  Pallas kernels  8 us (3%)
  matrix products  6.84 us (3%)
    all_to_all x2, waiting for transfers between devices, predict(): got = lax.all_to_all(tiles, 'dp', split_axis=0, concat_axis=0, tiled=True)  56.1 us
    all_to_all x3, waiting for transfers between devices, gather_sum(): got = lax.all_to_all(tiles, axis, split_axis=0, concat_axis=0, tiled=True)  30.8 us
    all_to_all x2, blocking collectives, collect(): lax.all_to_all(blocks, 'member', split_axis=0, concat_axis=0, tiled=True)  25.6 us
    all_to_all x2, starting transfers between devices, predict(): got = lax.all_to_all(tiles, 'dp', split_axis=0, concat_axis=0, tiled=True)  19.1 us
    all_to_all x3, starting transfers between devices, gather_sum(): got = lax.all_to_all(tiles, axis, split_axis=0, concat_axis=0, tiled=True)  18.4 us
    ppermute x3, starting transfers between devices, swap_pair(): return lax.ppermute(x, 'dp', [(i, i ^ 1) for i in range(n)])  11.8 us
    all_to_all x1, blocking collectives, gather_sum(): got = lax.all_to_all(tiles, axis, split_axis=0, concat_axis=0, tiled=True)  11.3 us
    pallas_call x2, Pallas kernels, solve_spd(): pl.pallas_call(kernel, out_shape=jax.ShapeDtypeStruct(sums.shape[1:], sum...  8 us
  transfers between devices with their start and end apart: 9, of which 7 were waited for; matrix products, arithmetic and copies ran while one was open for 3% of the time, Pallas kernels for 0%

profile of v10, /device:TPU:1, one launch (start us, length us, event | category | flops | bytes accessed | tf_op | source)
XLA Modules:
  0.0 228.9 jit_solution(15055980137328243986)
XLA Ops:
  7.2 0.7 convert.18
  8.0 0.8 convert.16
  8.8 0.8 convert.17
  9.7 1.1 broadcast_in_dim.22
  10.8 14.4 %all-to-all-start = ((bf16[32,129,128]{2,1,0:T(8,128)(2,1)}), bf16[32,129,128]{2,1,0:T(8,128)(2,1)S(1)}, u32[]{:S(2)}, u32[]{:S(2)}) async-start(bf16[32,129,128]{2,1,0:T(8,128)(2,1)} %bitcast.2), calls=%async_computation | async-start | bytes 2228224 | tf_op jit(solution)/shard_map/all_to_all | solution.py:83
  25.3 0.7 pad_maximum_fusion
  26.0 2.1 collective-permute-start
  28.2 26.6 %all-to-all-done = bf16[32,129,128]{2,1,0:T(8,128)(2,1)S(1)} async-done(((bf16[32,129,128]{2,1,0:T(8,128)(2,1)}), bf16[32,129,128]{2,1,0:T(8,128)(2,1)S(1)}, u32[]{:S(2)}, u32[]{:S(2)}) %all-to-all-start) | async-done | bytes 1056800 | tf_op jit(solution)/shard_map/all_to_all | solution.py:83
  54.8 2.5 %fusion.10 = f32[64,512]{1,0:T(8,128)S(1)} fusion(f32[32,128]{1,0:T(8,128)S(1)} %bitcast.72, bf16[32,129,128]{2,1,0:T(8,128)(2,1)S(1)} %all-to-all-done, f32[64]{0:T(128)S(1)} %fusion.39, bf16[256,64]{0,1:T(8,128)(2,1)S(1)} %collective-permute-done, bf16[256,64]{0,1:T(8,128)(2,1)S(1)} %copy-done.10), kind=kOutput, calls=%fused_computation.13 | convolution fusion | flops 541229056 | bytes 1262080 | tf_op jit(solution)/shard_map/doh,sdh->os/dot_general | solution.py:91
  57.3 14.2 %all_to_all.40 = f32[16,4,512]{2,1,0:T(4,128)S(1)} all-to-all(f32[16,4,512]{2,1,0:T(4,128)S(1)} %reshape.155), channel_id=1, replica_groups=mesh['member'=16,'dp'=32] {'member'}, dimensions={0} | all-to-all | bytes 262144 | tf_op jit(solution)/shard_map/all_to_all | solution.py:99
  71.6 5.1 %collective-permute-start.1 = (f32[16,4,256]{2,0,1:T(8,128)S(1)}, f32[16,4,256]{2,0,1:T(8,128)S(1)}, u32[]{:S(2)}, u32[]{:S(2)}) collective-permute-start(f32[16,4,256]{2,0,1:T(8,128)S(1)} %copy.91), channel_id=1, source_target_pairs={{0,1},{1,0},{2,3},{3,2},{4,5},{5,4},{6,7},{7,6},{8,9},{9,8},{10,11... | collective-permute-start | bytes 196616 | tf_op jit(solution)/shard_map/ppermute | solution.py:74
  76.7 0.8 collective-permute-done.1
  78.5 11.3 %all_to_all.41 = f32[16,16,128]{2,1,0:T(8,128)S(1)} all-to-all(f32[16,16,128]{2,1,0:T(8,128)S(1)} %broadcast_in_dim.24), channel_id=1, replica_groups=mesh['member'=16,'dp'=32] {'member'}, dimensions={0} | all-to-all | bytes 262144 | tf_op jit(solution)/shard_map/all_to_all | solution.py:63
  89.8 0.7 broadcast_in_dim.25
  90.5 8.0 %all-to-all-start.3 = ((f32[32,16,128]{2,1,0:T(8,128)}), f32[32,16,128]{2,1,0:T(8,128)S(1)}, u32[]{:S(2)}, u32[]{:S(2)}) async-start(f32[32,16,128]{2,1,0:T(8,128)} %broadcast_in_dim.25), calls=%async_computation.3 | async-start | bytes 524288 | tf_op jit(solution)/shard_map/all_to_all | solution.py:63
  98.5 12.9 %all-to-all-done.3 = f32[32,16,128]{2,1,0:T(8,128)S(1)} async-done(((f32[32,16,128]{2,1,0:T(8,128)}), f32[32,16,128]{2,1,0:T(8,128)S(1)}, u32[]{:S(2)}, u32[]{:S(2)}) %all-to-all-start.3) | async-done | bytes 262176 | tf_op jit(solution)/shard_map/all_to_all | solution.py:63
  111.5 1.2 slice.122
  113.3 0.7 add.105.s_ref
  114.0 4.0 %shard_map.102 = f32[32,32]{1,0:T(8,128)} custom-call(f32[2,32,32]{2,1,0:T(8,128)} %add.105.s_ref), custom_call_target="tpu_custom_call" | custom-call | tf_op jit(solution)/shard_map/pallas_call | solution.py:40
  118.0 0.8 constant_dynamic-slice_fusion.1
  118.9 2.0 copy.79
  121.0 0.9 multiply_reduce_fusion
  121.9 1.1 broadcast_in_dim.26
  123.1 4.7 %all-to-all-start.4 = ((bf16[32,129,128]{2,1,0:T(8,128)(2,1)}), bf16[32,129,128]{2,1,0:T(8,128)(2,1)S(1)}, u32[]{:S(2)}, u32[]{:S(2)}) async-start(bf16[32,129,128]{2,1,0:T(8,128)(2,1)} %bitcast.17), calls=%async_computation.4 | async-start | bytes 2228224 | tf_op jit(solution)/shard_map/all_to_all | solution.py:83
  127.8 29.5 %all-to-all-done.4 = bf16[32,129,128]{2,1,0:T(8,128)(2,1)S(1)} async-done(((bf16[32,129,128]{2,1,0:T(8,128)(2,1)}), bf16[32,129,128]{2,1,0:T(8,128)(2,1)S(1)}, u32[]{:S(2)}, u32[]{:S(2)}) %all-to-all-start.4) | async-done | bytes 1056800 | tf_op jit(solution)/shard_map/all_to_all | solution.py:83
  157.3 2.5 %fusion.11 = f32[64,512]{1,0:T(8,128)S(1)} fusion(f32[32,128]{1,0:T(8,128)S(1)} %bitcast.73, bf16[32,129,128]{2,1,0:T(8,128)(2,1)S(1)} %all-to-all-done.4, f32[64]{0:T(128)S(1)} %fusion.40, bf16[256,64]{0,1:T(8,128)(2,1)S(1)} %collective-permute-done, bf16[256,64]{0,1:T(8,128)(2,1)S(1)} %copy-done.10), kind=kOutput, calls=%fused_computation.14 | convolution fusion | flops 541229056 | bytes 1262080 | tf_op jit(solution)/shard_map/doh,sdh->os/dot_general | solution.py:91
  159.8 11.4 %all_to_all.42 = f32[16,4,512]{2,1,0:T(4,128)S(1)} all-to-all(f32[16,4,512]{2,1,0:T(4,128)S(1)} %reshape.157), channel_id=1, replica_groups=mesh['member'=16,'dp'=32] {'member'}, dimensions={0} | all-to-all | bytes 262144 | tf_op jit(solution)/shard_map/all_to_all | solution.py:99
  171.3 4.5 %collective-permute-start.2 = (f32[16,4,256]{2,0,1:T(8,128)S(1)}, f32[16,4,256]{2,0,1:T(8,128)S(1)}, u32[]{:S(2)}, u32[]{:S(2)}) collective-permute-start(f32[16,4,256]{2,0,1:T(8,128)S(1)} %copy.93), channel_id=1, source_target_pairs={{0,1},{1,0},{2,3},{3,2},{4,5},{5,4},{6,7},{7,6},{8,9},{9,8},{10,11... | collective-permute-start | bytes 196616 | tf_op jit(solution)/shard_map/ppermute | solution.py:74
  175.9 0.9 collective-permute-done.2
  177.3 0.3 convolution_bitcast_fusion
  177.6 0.7 broadcast_in_dim.28
  178.3 3.5 %all-to-all-start.6 = ((f32[16,16,128]{2,1,0:T(8,128)}), f32[16,16,128]{2,1,0:T(8,128)S(1)}, u32[]{:S(2)}, u32[]{:S(2)}) async-start(f32[16,16,128]{2,1,0:T(8,128)} %broadcast_in_dim.28), calls=%async_computation.6 | async-start | bytes 262144 | tf_op jit(solution)/shard_map/all_to_all | solution.py:63
  181.8 0.6 fusion.46
  182.5 6.8 %all-to-all-done.6 = f32[16,16,128]{2,1,0:T(8,128)S(1)} async-done(((f32[16,16,128]{2,1,0:T(8,128)}), f32[16,16,128]{2,1,0:T(8,128)S(1)}, u32[]{:S(2)}, u32[]{:S(2)}) %all-to-all-start.6) | async-done | bytes 131104 | tf_op jit(solution)/shard_map/all_to_all | solution.py:63
  189.3 0.7 broadcast_in_dim.29
  190.0 6.9 %all-to-all-start.7 = ((f32[32,16,128]{2,1,0:T(8,128)}), f32[32,16,128]{2,1,0:T(8,128)S(1)}, u32[]{:S(2)}, u32[]{:S(2)}) async-start(f32[32,16,128]{2,1,0:T(8,128)} %broadcast_in_dim.29), calls=%async_computation.7 | async-start | bytes 524288 | tf_op jit(solution)/shard_map/all_to_all | solution.py:63
  197.0 0.6 fusion.48
  197.5 1.3 fusion.47
  198.8 11.1 %all-to-all-done.7 = f32[32,16,128]{2,1,0:T(8,128)S(1)} async-done(((f32[32,16,128]{2,1,0:T(8,128)}), f32[32,16,128]{2,1,0:T(8,128)S(1)}, u32[]{:S(2)}, u32[]{:S(2)}) %all-to-all-start.7) | async-done | bytes 262176 | tf_op jit(solution)/shard_map/all_to_all | solution.py:63
  209.9 0.7 reshape.158.s_ref
  210.6 4.0 %shard_map.103 = f32[32,32]{1,0:T(8,128)} custom-call(f32[2,32,32]{2,1,0:T(8,128)} %reshape.158.s_ref), custom_call_target="tpu_custom_call" | custom-call | tf_op jit(solution)/shard_map/pallas_call | solution.py:40
  214.6 0.9 fusion.36
  215.6 0.8 multiply_reduce_fusion.3
  216.5 0.8 multiply_reduce_fusion.4
  217.3 1.2 slice_add_fusion.2
  218.5 1.2 add.115
  219.7 1.6 multiply_reduce_fusion.1
  221.3 0.7 slice_add_fusion
  (69 shorter events, 2.2 us)
Async XLA Ops:
  7.2 18.2 %copy-start.8 = (f32[2,128]{1,0:T(2,128)S(1)}, f32[2,128]{1,0:T(2,128)}, u32[]{:S(2)}) copy-start(f32[2,128]{1,0:T(2,128)} %param.11) | copy-start | bytes 3076
  7.2 18.2 %copy-start.4 = (f32[2,64,128]{2,1,0:T(8,128)S(1)}, f32[2,64,128]{2,1,0:T(8,128)}, u32[]{:S(2)}) copy-start(f32[2,64,128]{2,1,0:T(8,128)} %param.10) | copy-start | bytes 196612
  7.2 18.2 %copy-start.3 = (f32[2,64,128]{2,1,0:T(8,128)S(1)}, f32[2,64,128]{2,1,0:T(8,128)}, u32[]{:S(2)}) copy-start(f32[2,64,128]{2,1,0:T(8,128)} %param.12) | copy-start | bytes 196612
  7.2 18.1 %copy-start.9 = (f32[2,64]{1,0:T(2,128)S(1)}, f32[2,64]{1,0:T(2,128)}, u32[]{:S(2)}) copy-start(f32[2,64]{1,0:T(2,128)} %param.13) | copy-start | bytes 1540
  7.2 18.8 %copy-start.10 = (bf16[256,64]{0,1:T(8,128)(2,1)S(1)}, bf16[256,64]{0,1:T(8,128)(2,1)}, u32[]{:S(2)}) copy-start(bf16[256,64]{0,1:T(8,128)(2,1)} %param.7) | copy-start | bytes 98308
  10.8 44.0 %all-to-all-start = ((bf16[32,129,128]{2,1,0:T(8,128)(2,1)}), bf16[32,129,128]{2,1,0:T(8,128)(2,1)S(1)}, u32[]{:S(2)}, u32[]{:S(2)}) async-start(bf16[32,129,128]{2,1,0:T(8,128)(2,1)} %bitcast.2), calls=%async_computation | async-start | bytes 2228224 | tf_op jit(solution)/shard_map/all_to_all | solution.py:83
  25.2 86.2 %all-gather.2.cloned.1.call-start = ((), (), s32[]{:S(2)}) async-start(), calls=%async_computation.8 | async-start | bytes 2367488 | tf_op jit(solution)/shard_map/all_gather | solution.py:117
  26.0 28.7 %collective-permute-start = (bf16[256,64]{0,1:T(8,128)(2,1)S(1)}, bf16[256,64]{0,1:T(8,128)(2,1)S(1)}, u32[]{:S(2)}, u32[]{:S(2)}) collective-permute-start(bf16[256,64]{0,1:T(8,128)(2,1)S(1)} %copy-done.10), channel_id=1, source_target_pairs={{0,1},{1,0},{2,3},{3,2},{4,5},{5,4},{6,7},{7,6},{8,9},{9,8},{10,11... | collective-permute-start | bytes 98312 | tf_op jit(solution)/shard_map/ppermute | solution.py:74
  54.8 21.9 %copy-start.6 = (bf16[2,32,4,256]{3,2,1,0:T(4,128)(2,1)S(1)}, bf16[2,32,4,256]{3,2,1,0:T(4,128)(2,1)}, u32[]{:S(2)}) copy-start(bf16[2,32,4,256]{3,2,1,0:T(4,128)(2,1)} %param.9) | copy-start | bytes 393220
  54.8 22.8 %copy-start.7 = (f32[4,256]{1,0:T(4,128)S(1)}, f32[4,256]{1,0:T(4,128)}, u32[]{:S(2)}) copy-start(f32[4,256]{1,0:T(4,128)} %param.8) | copy-start | bytes 12292
  71.6 6.0 %collective-permute-start.1 = (f32[16,4,256]{2,0,1:T(8,128)S(1)}, f32[16,4,256]{2,0,1:T(8,128)S(1)}, u32[]{:S(2)}, u32[]{:S(2)}) collective-permute-start(f32[16,4,256]{2,0,1:T(8,128)S(1)} %copy.91), channel_id=1, source_target_pairs={{0,1},{1,0},{2,3},{3,2},{4,5},{5,4},{6,7},{7,6},{8,9},{9,8},{10,11... | collective-permute-start | bytes 196616 | tf_op jit(solution)/shard_map/ppermute | solution.py:74
  90.5 21.0 %all-to-all-start.3 = ((f32[32,16,128]{2,1,0:T(8,128)}), f32[32,16,128]{2,1,0:T(8,128)S(1)}, u32[]{:S(2)}, u32[]{:S(2)}) async-start(f32[32,16,128]{2,1,0:T(8,128)} %broadcast_in_dim.25), calls=%async_computation.3 | async-start | bytes 524288 | tf_op jit(solution)/shard_map/all_to_all | solution.py:63
  121.9 75.1 %copy-start.1 = (f32[2,130,128]{2,1,0:T(8,128)}, f32[2,130,128]{2,1,0:T(8,128)S(1)}, u32[]{:S(2)}) copy-start(f32[2,130,128]{2,1,0:T(8,128)S(1)} %fusion.45) | copy-start | bytes 399364
  123.1 34.2 %all-to-all-start.4 = ((bf16[32,129,128]{2,1,0:T(8,128)(2,1)}), bf16[32,129,128]{2,1,0:T(8,128)(2,1)S(1)}, u32[]{:S(2)}, u32[]{:S(2)}) async-start(bf16[32,129,128]{2,1,0:T(8,128)(2,1)} %bitcast.17), calls=%async_computation.4 | async-start | bytes 2228224 | tf_op jit(solution)/shard_map/all_to_all | solution.py:83
  159.8 22.0 %copy-start = (f32[32,130,128]{2,1,0:T(8,128)S(1)}, f32[32,130,128]{2,1,0:T(8,128)}, u32[]{:S(2)}) copy-start(f32[32,130,128]{2,1,0:T(8,128)} %all-gather.2.cloned.1.call-done) | copy-start | bytes 6389764
  171.3 5.4 %collective-permute-start.2 = (f32[16,4,256]{2,0,1:T(8,128)S(1)}, f32[16,4,256]{2,0,1:T(8,128)S(1)}, u32[]{:S(2)}, u32[]{:S(2)}) collective-permute-start(f32[16,4,256]{2,0,1:T(8,128)S(1)} %copy.93), channel_id=1, source_target_pairs={{0,1},{1,0},{2,3},{3,2},{4,5},{5,4},{6,7},{7,6},{8,9},{9,8},{10,11... | collective-permute-start | bytes 196616 | tf_op jit(solution)/shard_map/ppermute | solution.py:74
  178.3 11.0 %all-to-all-start.6 = ((f32[16,16,128]{2,1,0:T(8,128)}), f32[16,16,128]{2,1,0:T(8,128)S(1)}, u32[]{:S(2)}, u32[]{:S(2)}) async-start(f32[16,16,128]{2,1,0:T(8,128)} %broadcast_in_dim.28), calls=%async_computation.6 | async-start | bytes 262144 | tf_op jit(solution)/shard_map/all_to_all | solution.py:63
  190.0 19.8 %all-to-all-start.7 = ((f32[32,16,128]{2,1,0:T(8,128)}), f32[32,16,128]{2,1,0:T(8,128)S(1)}, u32[]{:S(2)}, u32[]{:S(2)}) async-start(f32[32,16,128]{2,1,0:T(8,128)} %broadcast_in_dim.29), calls=%async_computation.7 | async-start | bytes 524288 | tf_op jit(solution)/shard_map/all_to_all | solution.py:63
  197.5 17.1 %copy-start.5 = (f32[32,32]{1,0:T(8,128)S(1)}, f32[32,32]{1,0:T(8,128)}, u32[]{:S(2)}) copy-start(f32[32,32]{1,0:T(8,128)} %shard_map.102) | copy-start | bytes 12292
  198.8 22.5 %copy-start.2 = (f32[2,130,128]{2,1,0:T(8,128)S(1)}, f32[2,130,128]{2,1,0:T(8,128)}, u32[]{:S(2)}) copy-start(f32[2,130,128]{2,1,0:T(8,128)} %copy-done.1) | copy-start | bytes 399364
Sparse Core Ops, SparseCore 0:
  28.2 67.8 all-gather.1

commit v11 on v9

--- a/solution.py
+++ b/solution.py
@@ -125,7 +125,7 @@
         cross_part = lax.dot_general(
             anomaly, misfit, (((1,), (1,)), ((), ())), precision=lax.Precision.HIGHEST
         )
-        sums = gather_sum(gather_sum(jnp.stack([gram_part, cross_part]), "member"), "dp")
+        sums = gather_sum(gather_sum(jnp.stack([gram_part, cross_part]), "dp"), "member")
         if update == 0:
             sums = sums + whole[0, 0, 0] * 0
         gain = solve_spd(sums, 1.0 / count, ridge_level)

time: 225 us -> 224 us (level)
  blocking collectives: 46.3 us -> 61.8 us
  waiting for transfers between devices: 82.4 us -> 71.4 us
  starting transfers between devices: 45.9 us -> 40.3 us
    all_to_all x2, blocking collectives: 21.2 us -> 37 us  [gather_sum(): got = lax.all_to_all(tiles, axis, split_axis=0, concat_axis=0, tiled=True)]
    all_to_all x2, waiting for transfers between devices: 24.8 us -> 13.9 us  [gather_sum(): got = lax.all_to_all(tiles, axis, split_axis=0, concat_axis=0, tiled=True)]
    all_to_all x2, starting transfers between devices: 15.2 us -> 7.23 us  [gather_sum(): got = lax.all_to_all(tiles, axis, split_axis=0, concat_axis=0, tiled=True)]
    all_to_all x2, starting transfers between devices: 19 us -> 21.3 us  [predict(): got = lax.all_to_all(tiles, 'dp', split_axis=0, concat_axis=0, tiled=True)]
where the time goes in v11:
time: 224 us; the launch traced here: 223 us
  waiting for transfers between devices  71.4 us (32%)
  blocking collectives  61.8 us (28%)
  starting transfers between devices  40.3 us (18%)
  between operations  15.2 us (7%)
  local copies, waits for them, and re-layouts  13 us (6%)
  matrix products  10.4 us (5%)
  Pallas kernels  8.01 us (4%)
  other arithmetic  2.9 us (1%)
    all_to_all x2, waiting for transfers between devices, predict(): got = lax.all_to_all(tiles, 'dp', split_axis=0, concat_axis=0, tiled=True)  55.9 us
    all_to_all x2, blocking collectives, gather_sum(): got = lax.all_to_all(tiles, axis, split_axis=0, concat_axis=0, tiled=True)  37 us
    all_to_all x2, blocking collectives, collect(): lax.all_to_all(blocks, 'member', split_axis=0, concat_axis=0, tiled=True)  24.8 us
    all_to_all x2, starting transfers between devices, predict(): got = lax.all_to_all(tiles, 'dp', split_axis=0, concat_axis=0, tiled=True)  21.3 us
    all_to_all x2, waiting for transfers between devices, gather_sum(): got = lax.all_to_all(tiles, axis, split_axis=0, concat_axis=0, tiled=True)  13.9 us
    ppermute x3, starting transfers between devices, swap_pair(): return lax.ppermute(x, 'dp', [(i, i ^ 1) for i in range(n)])  11.7 us
    pallas_call x2, Pallas kernels, solve_spd(): pl.pallas_call(kernel, out_shape=jax.ShapeDtypeStruct(sums.shape[1:], sum...  8.01 us
    all_to_all x2, starting transfers between devices, gather_sum(): got = lax.all_to_all(tiles, axis, split_axis=0, concat_axis=0, tiled=True)  7.23 us
  transfers between devices with their start and end apart: 8, of which 6 were waited for; matrix products, arithmetic and copies ran while one was open for 3% of the time, Pallas kernels for 0%

profile of v11, /device:TPU:1, one launch (start us, length us, event | category | flops | bytes accessed | tf_op | source)
XLA Modules:
  0.0 223.1 jit_solution(13351389010327541071)
XLA Ops:
  7.2 0.7 bitcast_convert_fusion
  7.9 0.8 convert.16
  8.8 0.8 convert.17
  9.7 1.1 broadcast_in_dim.22
  10.8 14.4 %all-to-all-start = ((bf16[32,129,128]{2,1,0:T(8,128)(2,1)}), bf16[32,129,128]{2,1,0:T(8,128)(2,1)S(1)}, u32[]{:S(2)}, u32[]{:S(2)}) async-start(bf16[32,129,128]{2,1,0:T(8,128)(2,1)} %bitcast.2), calls=%async_computation | async-start | bytes 2228224 | tf_op jit(solution)/shard_map/all_to_all | solution.py:78
  25.5 0.7 copy.108
  26.2 2.1 collective-permute-start
  28.4 26.4 %all-to-all-done = bf16[32,129,128]{2,1,0:T(8,128)(2,1)S(1)} async-done(((bf16[32,129,128]{2,1,0:T(8,128)(2,1)}), bf16[32,129,128]{2,1,0:T(8,128)(2,1)S(1)}, u32[]{:S(2)}, u32[]{:S(2)}) %all-to-all-start) | async-done | bytes 1056800 | tf_op jit(solution)/shard_map/all_to_all | solution.py:78
  54.8 2.5 %fusion.10 = f32[64,512]{1,0:T(8,128)S(1)} fusion(f32[32,128]{1,0:T(8,128)S(1)} %bitcast.84, bf16[32,129,128]{2,1,0:T(8,128)(2,1)S(1)} %all-to-all-done, f32[64]{0:T(128)S(1)} %fusion.46, bf16[256,64]{0,1:T(8,128)(2,1)S(1)} %collective-permute-done, bf16[256,64]{0,1:T(8,128)(2,1)S(1)} %copy-done.7), kind=kOutput, calls=%fused_computation.11 | convolution fusion | flops 541229056 | bytes 1262080 | tf_op jit(solution)/shard_map/doh,sdh->os/dot_general | solution.py:86
  57.3 14.3 %all_to_all.40 = f32[16,4,512]{2,1,0:T(4,128)S(1)} all-to-all(f32[16,4,512]{2,1,0:T(4,128)S(1)} %reshape.148), channel_id=1, replica_groups=mesh['member'=16,'dp'=32] {'member'}, dimensions={0} | all-to-all | bytes 262144 | tf_op jit(solution)/shard_map/all_to_all | solution.py:94
  71.6 5.0 %collective-permute-start.1 = (f32[16,4,256]{2,0,1:T(8,128)S(1)}, f32[16,4,256]{2,0,1:T(8,128)S(1)}, u32[]{:S(2)}, u32[]{:S(2)}) collective-permute-start(f32[16,4,256]{2,0,1:T(8,128)S(1)} %copy.128), channel_id=1, source_target_pairs={{0,1},{1,0},{2,3},{3,2},{4,5},{5,4},{6,7},{7,6},{8,9},{9,8},{10,11... | collective-permute-start | bytes 196616 | tf_op jit(solution)/shard_map/ppermute | solution.py:69
  76.8 0.8 collective-permute-done.1
  77.7 0.1 copy.101
  77.9 0.2 convolution_bitcast_fusion.3
  78.1 0.3 convolution_bitcast_fusion.2
  78.5 18.5 %all_to_all.41 = f32[32,16,128]{2,1,0:T(8,128)S(1)} all-to-all(f32[32,16,128]{2,1,0:T(8,128)S(1)} %broadcast_in_dim.24), channel_id=1, replica_groups=mesh['member'=16,'dp'=32] {'dp'}, dimensions={0} | all-to-all | bytes 524288 | tf_op jit(solution)/shard_map/all_to_all | solution.py:63
  97.0 0.7 broadcast_in_dim.25
  97.7 3.7 %all-to-all-start.3 = ((f32[16,16,128]{2,1,0:T(8,128)}), f32[16,16,128]{2,1,0:T(8,128)S(1)}, u32[]{:S(2)}, u32[]{:S(2)}) async-start(f32[16,16,128]{2,1,0:T(8,128)} %broadcast_in_dim.25), calls=%async_computation.3 | async-start | bytes 262144 | tf_op jit(solution)/shard_map/all_to_all | solution.py:63
  101.4 7.4 %all-to-all-done.3 = f32[16,16,128]{2,1,0:T(8,128)S(1)} async-done(((f32[16,16,128]{2,1,0:T(8,128)}), f32[16,16,128]{2,1,0:T(8,128)S(1)}, u32[]{:S(2)}, u32[]{:S(2)}) %all-to-all-start.3) | async-done | bytes 131104 | tf_op jit(solution)/shard_map/all_to_all | solution.py:63
  108.9 1.2 slice.120
  110.8 0.7 add.105.s_ref
  111.4 4.0 %shard_map.102 = f32[32,32]{1,0:T(8,128)} custom-call(f32[2,32,32]{2,1,0:T(8,128)} %add.105.s_ref), custom_call_target="tpu_custom_call" | custom-call | tf_op jit(solution)/shard_map/pallas_call | solution.py:40
  115.4 2.1 copy.110
  117.5 0.8 convolution_add_fusion
  118.4 1.1 broadcast_in_dim.26
  119.5 6.9 %all-to-all-start.4 = ((bf16[32,129,128]{2,1,0:T(8,128)(2,1)}), bf16[32,129,128]{2,1,0:T(8,128)(2,1)S(1)}, u32[]{:S(2)}, u32[]{:S(2)}) async-start(bf16[32,129,128]{2,1,0:T(8,128)(2,1)} %bitcast.18), calls=%async_computation.4 | async-start | bytes 2228224 | tf_op jit(solution)/shard_map/all_to_all | solution.py:78
  126.4 29.5 %all-to-all-done.4 = bf16[32,129,128]{2,1,0:T(8,128)(2,1)S(1)} async-done(((bf16[32,129,128]{2,1,0:T(8,128)(2,1)}), bf16[32,129,128]{2,1,0:T(8,128)(2,1)S(1)}, u32[]{:S(2)}, u32[]{:S(2)}) %all-to-all-start.4) | async-done | bytes 1056800 | tf_op jit(solution)/shard_map/all_to_all | solution.py:78
  156.0 3.1 %fusion.11 = f32[64,512]{1,0:T(8,128)} fusion(f32[32,128]{1,0:T(8,128)S(1)} %bitcast.85, bf16[32,129,128]{2,1,0:T(8,128)(2,1)S(1)} %all-to-all-done.4, f32[64]{0:T(128)S(1)} %fusion.47, bf16[256,64]{0,1:T(8,128)(2,1)S(1)} %collective-permute-done, bf16[256,64]{0,1:T(8,128)(2,1)S(1)} %copy-done.7), kind=kOutput, calls=%fused_computation.12 | convolution fusion | flops 541229056 | bytes 1262080 | tf_op jit(solution)/shard_map/doh,sdh->os/dot_general | solution.py:86
  159.1 0.9 reshape.150
  160.0 10.6 %all_to_all.42 = f32[16,4,512]{2,1,0:T(4,128)S(1)} all-to-all(f32[16,4,512]{2,1,0:T(4,128)S(1)} %reshape.150), channel_id=1, replica_groups=mesh['member'=16,'dp'=32] {'member'}, dimensions={0} | all-to-all | bytes 262144 | tf_op jit(solution)/shard_map/all_to_all | solution.py:94
  170.6 4.5 %collective-permute-start.2 = (f32[16,4,256]{2,0,1:T(8,128)S(1)}, f32[16,4,256]{2,0,1:T(8,128)S(1)}, u32[]{:S(2)}, u32[]{:S(2)}) collective-permute-start(f32[16,4,256]{2,0,1:T(8,128)S(1)} %copy.130), channel_id=1, source_target_pairs={{0,1},{1,0},{2,3},{3,2},{4,5},{5,4},{6,7},{7,6},{8,9},{9,8},{10,11... | collective-permute-start | bytes 196616 | tf_op jit(solution)/shard_map/ppermute | solution.py:69
  175.2 0.9 collective-permute-done.2
  176.3 0.2 convolution_bitcast_fusion.1
  176.6 0.3 convolution_bitcast_fusion
  177.0 18.5 %all_to_all.43 = f32[32,16,128]{2,1,0:T(8,128)S(1)} all-to-all(f32[32,16,128]{2,1,0:T(8,128)S(1)} %broadcast_in_dim.28), channel_id=1, replica_groups=mesh['member'=16,'dp'=32] {'dp'}, dimensions={0} | all-to-all | bytes 524288 | tf_op jit(solution)/shard_map/all_to_all | solution.py:63
  195.5 0.7 broadcast_in_dim.29
  196.2 3.5 %all-to-all-start.7 = ((f32[16,16,128]{2,1,0:T(8,128)}), f32[16,16,128]{2,1,0:T(8,128)S(1)}, u32[]{:S(2)}, u32[]{:S(2)}) async-start(f32[16,16,128]{2,1,0:T(8,128)} %broadcast_in_dim.29), calls=%async_computation.7 | async-start | bytes 262144 | tf_op jit(solution)/shard_map/all_to_all | solution.py:63
  199.7 1.0 fusion.53
  200.7 6.5 %all-to-all-done.7 = f32[16,16,128]{2,1,0:T(8,128)S(1)} async-done(((f32[16,16,128]{2,1,0:T(8,128)}), f32[16,16,128]{2,1,0:T(8,128)S(1)}, u32[]{:S(2)}, u32[]{:S(2)}) %all-to-all-start.7) | async-done | bytes 131104 | tf_op jit(solution)/shard_map/all_to_all | solution.py:63
  207.2 0.7 reshape.151.s_ref
  207.9 4.0 %shard_map.103 = f32[32,32]{1,0:T(8,128)} custom-call(f32[2,32,32]{2,1,0:T(8,128)} %reshape.151.s_ref), custom_call_target="tpu_custom_call" | custom-call | tf_op jit(solution)/shard_map/pallas_call | solution.py:40
  211.9 0.9 fusion.40
  212.8 0.4 convolution_add_fusion.1
  213.2 0.4 convolution_add_fusion.2
  213.6 0.7 convolution_add_fusion.4
  214.3 0.6 copy.123
  214.9 0.6 copy.124
  215.5 0.7 convolution_add_fusion.3
  (61 shorter events, 1.4 us)
Async XLA Ops:
  7.2 18.3 %copy-start.5 = (f32[2,128]{1,0:T(2,128)S(1)}, f32[2,128]{1,0:T(2,128)}, u32[]{:S(2)}) copy-start(f32[2,128]{1,0:T(2,128)} %param.11) | copy-start | bytes 3076
  7.2 18.1 %copy-start = (f32[2,64,128]{2,1,0:T(8,128)S(1)}, f32[2,64,128]{2,1,0:T(8,128)}, u32[]{:S(2)}) copy-start(f32[2,64,128]{2,1,0:T(8,128)} %param.10) | copy-start | bytes 196612
  7.2 18.2 %copy-start.1 = (f32[2,64,128]{2,1,0:T(8,128)S(1)}, f32[2,64,128]{2,1,0:T(8,128)}, u32[]{:S(2)}) copy-start(f32[2,64,128]{2,1,0:T(8,128)} %param.12) | copy-start | bytes 196612
  7.2 18.2 %copy-start.6 = (f32[2,64]{1,0:T(2,128)S(1)}, f32[2,64]{1,0:T(2,128)}, u32[]{:S(2)}) copy-start(f32[2,64]{1,0:T(2,128)} %param.13) | copy-start | bytes 1540
  9.6 16.6 %copy-start.7 = (bf16[256,64]{0,1:T(8,128)(2,1)S(1)}, bf16[256,64]{0,1:T(8,128)(2,1)}, u32[]{:S(2)}) copy-start(bf16[256,64]{0,1:T(8,128)(2,1)} %param.7) | copy-start | bytes 98308
  10.8 44.0 %all-to-all-start = ((bf16[32,129,128]{2,1,0:T(8,128)(2,1)}), bf16[32,129,128]{2,1,0:T(8,128)(2,1)S(1)}, u32[]{:S(2)}, u32[]{:S(2)}) async-start(bf16[32,129,128]{2,1,0:T(8,128)(2,1)} %bitcast.2), calls=%async_computation | async-start | bytes 2228224 | tf_op jit(solution)/shard_map/all_to_all | solution.py:78
  25.2 83.6 %all-gather.2.cloned.1.call-start = ((), (), s32[]{:S(2)}) async-start(), calls=%async_computation.8 | async-start | bytes 2367488 | tf_op jit(solution)/shard_map/all_gather | solution.py:112
  26.2 28.6 %collective-permute-start = (bf16[256,64]{0,1:T(8,128)(2,1)S(1)}, bf16[256,64]{0,1:T(8,128)(2,1)S(1)}, u32[]{:S(2)}, u32[]{:S(2)}) collective-permute-start(bf16[256,64]{0,1:T(8,128)(2,1)S(1)} %copy-done.7), channel_id=1, source_target_pairs={{0,1},{1,0},{2,3},{3,2},{4,5},{5,4},{6,7},{7,6},{8,9},{9,8},{10,11... | collective-permute-start | bytes 98312 | tf_op jit(solution)/shard_map/ppermute | solution.py:69
  54.8 21.9 %copy-start.3 = (bf16[2,32,4,256]{3,2,1,0:T(4,128)(2,1)S(1)}, bf16[2,32,4,256]{3,2,1,0:T(4,128)(2,1)}, u32[]{:S(2)}) copy-start(bf16[2,32,4,256]{3,2,1,0:T(4,128)(2,1)} %param.9) | copy-start | bytes 393220
  54.8 22.8 %copy-start.4 = (f32[4,256]{1,0:T(4,128)S(1)}, f32[4,256]{1,0:T(4,128)}, u32[]{:S(2)}) copy-start(f32[4,256]{1,0:T(4,128)} %param.8) | copy-start | bytes 12292
  71.6 5.9 %collective-permute-start.1 = (f32[16,4,256]{2,0,1:T(8,128)S(1)}, f32[16,4,256]{2,0,1:T(8,128)S(1)}, u32[]{:S(2)}, u32[]{:S(2)}) collective-permute-start(f32[16,4,256]{2,0,1:T(8,128)S(1)} %copy.128), channel_id=1, source_target_pairs={{0,1},{1,0},{2,3},{3,2},{4,5},{5,4},{6,7},{7,6},{8,9},{9,8},{10,11... | collective-permute-start | bytes 196616 | tf_op jit(solution)/shard_map/ppermute | solution.py:69
  97.7 11.2 %all-to-all-start.3 = ((f32[16,16,128]{2,1,0:T(8,128)}), f32[16,16,128]{2,1,0:T(8,128)S(1)}, u32[]{:S(2)}, u32[]{:S(2)}) async-start(f32[16,16,128]{2,1,0:T(8,128)} %broadcast_in_dim.25), calls=%async_computation.3 | async-start | bytes 262144 | tf_op jit(solution)/shard_map/all_to_all | solution.py:63
  115.4 2.1 copy-start.2
  119.5 36.5 %all-to-all-start.4 = ((bf16[32,129,128]{2,1,0:T(8,128)(2,1)}), bf16[32,129,128]{2,1,0:T(8,128)(2,1)S(1)}, u32[]{:S(2)}, u32[]{:S(2)}) async-start(bf16[32,129,128]{2,1,0:T(8,128)(2,1)} %bitcast.18), calls=%async_computation.4 | async-start | bytes 2228224 | tf_op jit(solution)/shard_map/all_to_all | solution.py:78
  170.6 5.4 %collective-permute-start.2 = (f32[16,4,256]{2,0,1:T(8,128)S(1)}, f32[16,4,256]{2,0,1:T(8,128)S(1)}, u32[]{:S(2)}, u32[]{:S(2)}) collective-permute-start(f32[16,4,256]{2,0,1:T(8,128)S(1)} %copy.130), channel_id=1, source_target_pairs={{0,1},{1,0},{2,3},{3,2},{4,5},{5,4},{6,7},{7,6},{8,9},{9,8},{10,11... | collective-permute-start | bytes 196616 | tf_op jit(solution)/shard_map/ppermute | solution.py:69
  196.2 11.0 %all-to-all-start.7 = ((f32[16,16,128]{2,1,0:T(8,128)}), f32[16,16,128]{2,1,0:T(8,128)S(1)}, u32[]{:S(2)}, u32[]{:S(2)}) async-start(f32[16,16,128]{2,1,0:T(8,128)} %broadcast_in_dim.29), calls=%async_computation.7 | async-start | bytes 262144 | tf_op jit(solution)/shard_map/all_to_all | solution.py:63
Sparse Core Ops, SparseCore 0:
  28.2 66.8 all-gather.1

commit v12 on v11

--- a/solution.py
+++ b/solution.py
@@ -4,6 +4,7 @@
 import jax.numpy as jnp
 from jax import lax
 from jax.experimental import pallas as pl
+from jax.experimental.pallas import tpu as pltpu
 from jax.sharding import PartitionSpec as P
 
 UPDATES = 2
@@ -19,7 +20,8 @@
     return lax.linalg.triangular_solve(factor, middle, left_side=True, lower=True, transpose_a=True)
 
 
-def _eliminate(s_ref, o_ref, *, scale, ridge):
+def _eliminate(s_ref, *rest, scale, ridge):
+    o_ref = rest[-1]
     a = s_ref[0] * scale
     b = s_ref[1] * scale
     n = a.shape[0]
@@ -35,9 +37,17 @@
         b = jnp.where(rows == k, rb, b - col * rb)
     o_ref[...] = b
 
-def solve_spd(sums, scale, ridge):
+
+def solve_spd(sums, scale, ridge, after=()):
     kernel = functools.partial(_eliminate, scale=scale, ridge=ridge)
-    return pl.pallas_call(kernel, out_shape=jax.ShapeDtypeStruct(sums.shape[1:], sums.dtype))(sums)
+    specs = [pl.BlockSpec(memory_space=pltpu.VMEM)] + [pl.BlockSpec(memory_space=pl.ANY) for _ in after]
+    return pl.pallas_call(
+        kernel,
+        out_shape=jax.ShapeDtypeStruct(sums.shape[1:], sums.dtype),
+        in_specs=specs,
+        out_specs=pl.BlockSpec(memory_space=pltpu.VMEM),
+    )(sums, *after)
+
 
 def pack(w_in, b_in, w_out, b_out):
     n, hid = w_in.shape[0], w_in.shape[2]
@@ -126,9 +136,7 @@
             anomaly, misfit, (((1,), (1,)), ((), ())), precision=lax.Precision.HIGHEST
         )
         sums = gather_sum(gather_sum(jnp.stack([gram_part, cross_part]), "dp"), "member")
-        if update == 0:
-            sums = sums + whole[0, 0, 0] * 0
-        gain = solve_spd(sums, 1.0 / count, ridge_level)
+        gain = solve_spd(sums, 1.0 / count, ridge_level, (whole,) if update == 0 else ())
         if update == 0:
             first_gain = gain
             columns = lax.dynamic_slice_in_dim(gain, first, per_device, 1)

time: 224 us -> 223 us (level)
  no operation moved by 1% of the time
where the time goes in v12:
time: 223 us; the launch traced here: 222 us
  waiting for transfers between devices  71.4 us (32%)
  blocking collectives  62 us (28%)
  starting transfers between devices  39.9 us (18%)
  between operations  14.5 us (7%)
  local copies, waits for them, and re-layouts  11.8 us (5%)
  matrix products  11.1 us (5%)
  Pallas kernels  8.01 us (4%)
  other arithmetic  2.9 us (1%)
    all_to_all x2, waiting for transfers between devices, predict(): got = lax.all_to_all(tiles, 'dp', split_axis=0, concat_axis=0, tiled=True)  55.9 us
    all_to_all x2, blocking collectives, gather_sum(): got = lax.all_to_all(tiles, axis, split_axis=0, concat_axis=0, tiled=True)  36.9 us
    all_to_all x2, blocking collectives, collect(): lax.all_to_all(blocks, 'member', split_axis=0, concat_axis=0, tiled=True)  25.1 us
    all_to_all x2, starting transfers between devices, predict(): got = lax.all_to_all(tiles, 'dp', split_axis=0, concat_axis=0, tiled=True)  20.8 us
    all_to_all x2, waiting for transfers between devices, gather_sum(): got = lax.all_to_all(tiles, axis, split_axis=0, concat_axis=0, tiled=True)  13.9 us
    ppermute x3, starting transfers between devices, swap_pair(): return lax.ppermute(x, 'dp', [(i, i ^ 1) for i in range(n)])  11.8 us
    pallas_call x2, Pallas kernels, solve_spd(): pl.pallas_call(kernel, out_shape=jax.ShapeDtypeStruct(sums.shape[1:], sum...  8.01 us
    all_to_all x2, starting transfers between devices, gather_sum(): got = lax.all_to_all(tiles, axis, split_axis=0, concat_axis=0, tiled=True)  7.25 us
  transfers between devices with their start and end apart: 8, of which 6 were waited for; matrix products, arithmetic and copies ran while one was open for 3% of the time, Pallas kernels for 0%

profile of v12, /device:TPU:1, one launch (start us, length us, event | category | flops | bytes accessed | tf_op | source)
XLA Modules:
  0.0 221.7 jit_solution(16272052359168814086)
XLA Ops:
  7.2 0.7 bitcast_convert_fusion
  7.9 0.8 convert.16
  8.8 0.8 convert.17
  9.7 1.1 broadcast_in_dim.22
  10.8 14.4 %all-to-all-start = ((bf16[32,129,128]{2,1,0:T(8,128)(2,1)}), bf16[32,129,128]{2,1,0:T(8,128)(2,1)S(1)}, u32[]{:S(2)}, u32[]{:S(2)}) async-start(bf16[32,129,128]{2,1,0:T(8,128)(2,1)} %bitcast.2), calls=%async_computation | async-start | bytes 2228224 | tf_op jit(solution)/shard_map/all_to_all | solution.py:88
  25.5 0.7 copy.108
  26.2 2.1 collective-permute-start
  28.4 26.4 %all-to-all-done = bf16[32,129,128]{2,1,0:T(8,128)(2,1)S(1)} async-done(((bf16[32,129,128]{2,1,0:T(8,128)(2,1)}), bf16[32,129,128]{2,1,0:T(8,128)(2,1)S(1)}, u32[]{:S(2)}, u32[]{:S(2)}) %all-to-all-start) | async-done | bytes 1056800 | tf_op jit(solution)/shard_map/all_to_all | solution.py:88
  54.8 2.5 %fusion.10 = f32[64,512]{1,0:T(8,128)S(1)} fusion(f32[32,128]{1,0:T(8,128)S(1)} %bitcast.83, bf16[32,129,128]{2,1,0:T(8,128)(2,1)S(1)} %all-to-all-done, f32[64]{0:T(128)S(1)} %fusion.46, bf16[256,64]{0,1:T(8,128)(2,1)S(1)} %collective-permute-done, bf16[256,64]{0,1:T(8,128)(2,1)S(1)} %copy-done.7), kind=kOutput, calls=%fused_computation.11 | convolution fusion | flops 541229056 | bytes 1262080 | tf_op jit(solution)/shard_map/doh,sdh->os/dot_general | solution.py:96
  57.3 14.2 %all_to_all.40 = f32[16,4,512]{2,1,0:T(4,128)S(1)} all-to-all(f32[16,4,512]{2,1,0:T(4,128)S(1)} %reshape.146), channel_id=1, replica_groups=mesh['member'=16,'dp'=32] {'member'}, dimensions={0} | all-to-all | bytes 262144 | tf_op jit(solution)/shard_map/all_to_all | solution.py:104
  71.6 5.1 %collective-permute-start.1 = (f32[16,4,256]{2,0,1:T(8,128)S(1)}, f32[16,4,256]{2,0,1:T(8,128)S(1)}, u32[]{:S(2)}, u32[]{:S(2)}) collective-permute-start(f32[16,4,256]{2,0,1:T(8,128)S(1)} %copy.128), channel_id=1, source_target_pairs={{0,1},{1,0},{2,3},{3,2},{4,5},{5,4},{6,7},{7,6},{8,9},{9,8},{10,11... | collective-permute-start | bytes 196616 | tf_op jit(solution)/shard_map/ppermute | solution.py:79
  76.8 0.8 collective-permute-done.1
  77.7 0.1 copy.101
  77.8 0.1 copy.105
  77.9 0.2 convolution_bitcast_fusion.3
  78.1 0.3 convolution_bitcast_fusion.2
  78.5 18.5 %all_to_all.41 = f32[32,16,128]{2,1,0:T(8,128)S(1)} all-to-all(f32[32,16,128]{2,1,0:T(8,128)S(1)} %broadcast_in_dim.24), channel_id=1, replica_groups=mesh['member'=16,'dp'=32] {'dp'}, dimensions={0} | all-to-all | bytes 524288 | tf_op jit(solution)/shard_map/all_to_all | solution.py:73
  97.0 0.7 broadcast_in_dim.25
  97.7 3.7 %all-to-all-start.3 = ((f32[16,16,128]{2,1,0:T(8,128)}), f32[16,16,128]{2,1,0:T(8,128)S(1)}, u32[]{:S(2)}, u32[]{:S(2)}) async-start(f32[16,16,128]{2,1,0:T(8,128)} %broadcast_in_dim.25), calls=%async_computation.3 | async-start | bytes 262144 | tf_op jit(solution)/shard_map/all_to_all | solution.py:73
  101.4 7.4 %all-to-all-done.3 = f32[16,16,128]{2,1,0:T(8,128)S(1)} async-done(((f32[16,16,128]{2,1,0:T(8,128)}), f32[16,16,128]{2,1,0:T(8,128)S(1)}, u32[]{:S(2)}, u32[]{:S(2)}) %all-to-all-start.3) | async-done | bytes 131104 | tf_op jit(solution)/shard_map/all_to_all | solution.py:73
  108.9 0.7 reshape.147.s_ref
  109.6 2.0 copy.110
  111.6 4.0 %shard_map.102 = f32[32,32]{1,0:T(8,128)} custom-call(f32[2,32,32]{2,1,0:T(8,128)} %reshape.147.s_ref, f32[32,130,128]{2,1,0:T(8,128)} %all-gather.2.cloned.1.call-done.rest_0_), custom_call_target="tpu_custom_call" | custom-call | tf_op jit(solution)/shard_map/pallas_call | solution.py:44
  115.6 1.5 convolution_add_fusion
  117.2 1.1 broadcast_in_dim.26
  118.3 6.4 %all-to-all-start.4 = ((bf16[32,129,128]{2,1,0:T(8,128)(2,1)}), bf16[32,129,128]{2,1,0:T(8,128)(2,1)S(1)}, u32[]{:S(2)}, u32[]{:S(2)}) async-start(bf16[32,129,128]{2,1,0:T(8,128)(2,1)} %bitcast.17), calls=%async_computation.4 | async-start | bytes 2228224 | tf_op jit(solution)/shard_map/all_to_all | solution.py:88
  124.7 29.5 %all-to-all-done.4 = bf16[32,129,128]{2,1,0:T(8,128)(2,1)S(1)} async-done(((bf16[32,129,128]{2,1,0:T(8,128)(2,1)}), bf16[32,129,128]{2,1,0:T(8,128)(2,1)S(1)}, u32[]{:S(2)}, u32[]{:S(2)}) %all-to-all-start.4) | async-done | bytes 1056800 | tf_op jit(solution)/shard_map/all_to_all | solution.py:88
  154.2 3.1 %fusion.11 = f32[64,512]{1,0:T(8,128)} fusion(f32[32,128]{1,0:T(8,128)S(1)} %bitcast.84, bf16[32,129,128]{2,1,0:T(8,128)(2,1)S(1)} %all-to-all-done.4, f32[64]{0:T(128)S(1)} %fusion.47, bf16[256,64]{0,1:T(8,128)(2,1)S(1)} %collective-permute-done, bf16[256,64]{0,1:T(8,128)(2,1)S(1)} %copy-done.7), kind=kOutput, calls=%fused_computation.12 | convolution fusion | flops 541229056 | bytes 1262080 | tf_op jit(solution)/shard_map/doh,sdh->os/dot_general | solution.py:96
  157.3 0.9 reshape.149
  158.3 10.9 %all_to_all.42 = f32[16,4,512]{2,1,0:T(4,128)S(1)} all-to-all(f32[16,4,512]{2,1,0:T(4,128)S(1)} %reshape.149), channel_id=1, replica_groups=mesh['member'=16,'dp'=32] {'member'}, dimensions={0} | all-to-all | bytes 262144 | tf_op jit(solution)/shard_map/all_to_all | solution.py:104
  169.2 4.6 %collective-permute-start.2 = (f32[16,4,256]{2,0,1:T(8,128)S(1)}, f32[16,4,256]{2,0,1:T(8,128)S(1)}, u32[]{:S(2)}, u32[]{:S(2)}) collective-permute-start(f32[16,4,256]{2,0,1:T(8,128)S(1)} %copy.130), channel_id=1, source_target_pairs={{0,1},{1,0},{2,3},{3,2},{4,5},{5,4},{6,7},{7,6},{8,9},{9,8},{10,11... | collective-permute-start | bytes 196616 | tf_op jit(solution)/shard_map/ppermute | solution.py:79
  173.8 0.9 collective-permute-done.2
  174.9 0.2 convolution_bitcast_fusion.1
  175.2 0.3 convolution_bitcast_fusion
  175.6 18.5 %all_to_all.43 = f32[32,16,128]{2,1,0:T(8,128)S(1)} all-to-all(f32[32,16,128]{2,1,0:T(8,128)S(1)} %broadcast_in_dim.28), channel_id=1, replica_groups=mesh['member'=16,'dp'=32] {'dp'}, dimensions={0} | all-to-all | bytes 524288 | tf_op jit(solution)/shard_map/all_to_all | solution.py:73
  194.1 0.7 broadcast_in_dim.29
  194.8 3.5 %all-to-all-start.7 = ((f32[16,16,128]{2,1,0:T(8,128)}), f32[16,16,128]{2,1,0:T(8,128)S(1)}, u32[]{:S(2)}, u32[]{:S(2)}) async-start(f32[16,16,128]{2,1,0:T(8,128)} %broadcast_in_dim.29), calls=%async_computation.7 | async-start | bytes 262144 | tf_op jit(solution)/shard_map/all_to_all | solution.py:73
  198.3 1.0 fusion.53
  199.3 6.5 %all-to-all-done.7 = f32[16,16,128]{2,1,0:T(8,128)S(1)} async-done(((f32[16,16,128]{2,1,0:T(8,128)}), f32[16,16,128]{2,1,0:T(8,128)S(1)}, u32[]{:S(2)}, u32[]{:S(2)}) %all-to-all-start.7) | async-done | bytes 131104 | tf_op jit(solution)/shard_map/all_to_all | solution.py:73
  205.8 0.7 reshape.150.s_ref
  206.5 4.0 %shard_map.103 = f32[32,32]{1,0:T(8,128)} custom-call(f32[2,32,32]{2,1,0:T(8,128)} %reshape.150.s_ref), custom_call_target="tpu_custom_call" | custom-call | tf_op jit(solution)/shard_map/pallas_call | solution.py:44
  210.5 0.9 fusion.40
  211.4 0.4 convolution_add_fusion.1
  211.8 0.4 convolution_add_fusion.2
  212.2 0.7 convolution_add_fusion.4
  212.9 0.6 copy.123
  213.5 0.6 copy.124
  214.1 0.7 convolution_add_fusion.3
  (59 shorter events, 1.3 us)
Async XLA Ops:
  7.2 18.3 %copy-start.5 = (f32[2,128]{1,0:T(2,128)S(1)}, f32[2,128]{1,0:T(2,128)}, u32[]{:S(2)}) copy-start(f32[2,128]{1,0:T(2,128)} %param.11) | copy-start | bytes 3076
  7.2 18.1 %copy-start = (f32[2,64,128]{2,1,0:T(8,128)S(1)}, f32[2,64,128]{2,1,0:T(8,128)}, u32[]{:S(2)}) copy-start(f32[2,64,128]{2,1,0:T(8,128)} %param.10) | copy-start | bytes 196612
  7.2 18.2 %copy-start.1 = (f32[2,64,128]{2,1,0:T(8,128)S(1)}, f32[2,64,128]{2,1,0:T(8,128)}, u32[]{:S(2)}) copy-start(f32[2,64,128]{2,1,0:T(8,128)} %param.12) | copy-start | bytes 196612
  7.2 18.2 %copy-start.6 = (f32[2,64]{1,0:T(2,128)S(1)}, f32[2,64]{1,0:T(2,128)}, u32[]{:S(2)}) copy-start(f32[2,64]{1,0:T(2,128)} %param.13) | copy-start | bytes 1540
  9.6 16.6 %copy-start.7 = (bf16[256,64]{0,1:T(8,128)(2,1)S(1)}, bf16[256,64]{0,1:T(8,128)(2,1)}, u32[]{:S(2)}) copy-start(bf16[256,64]{0,1:T(8,128)(2,1)} %param.7) | copy-start | bytes 98308
  10.8 44.0 %all-to-all-start = ((bf16[32,129,128]{2,1,0:T(8,128)(2,1)}), bf16[32,129,128]{2,1,0:T(8,128)(2,1)S(1)}, u32[]{:S(2)}, u32[]{:S(2)}) async-start(bf16[32,129,128]{2,1,0:T(8,128)(2,1)} %bitcast.2), calls=%async_computation | async-start | bytes 2228224 | tf_op jit(solution)/shard_map/all_to_all | solution.py:88
  25.2 84.3 %all-gather.2.cloned.1.call-start = ((), (), s32[]{:S(2)}) async-start(), calls=%async_computation.8 | async-start | bytes 2367488 | tf_op jit(solution)/shard_map/all_gather | solution.py:122
  26.2 28.6 %collective-permute-start = (bf16[256,64]{0,1:T(8,128)(2,1)S(1)}, bf16[256,64]{0,1:T(8,128)(2,1)S(1)}, u32[]{:S(2)}, u32[]{:S(2)}) collective-permute-start(bf16[256,64]{0,1:T(8,128)(2,1)S(1)} %copy-done.7), channel_id=1, source_target_pairs={{0,1},{1,0},{2,3},{3,2},{4,5},{5,4},{6,7},{7,6},{8,9},{9,8},{10,11... | collective-permute-start | bytes 98312 | tf_op jit(solution)/shard_map/ppermute | solution.py:79
  54.8 21.9 %copy-start.3 = (bf16[2,32,4,256]{3,2,1,0:T(4,128)(2,1)S(1)}, bf16[2,32,4,256]{3,2,1,0:T(4,128)(2,1)}, u32[]{:S(2)}) copy-start(bf16[2,32,4,256]{3,2,1,0:T(4,128)(2,1)} %param.9) | copy-start | bytes 393220
  54.8 22.8 %copy-start.4 = (f32[4,256]{1,0:T(4,128)S(1)}, f32[4,256]{1,0:T(4,128)}, u32[]{:S(2)}) copy-start(f32[4,256]{1,0:T(4,128)} %param.8) | copy-start | bytes 12292
  71.6 6.0 %collective-permute-start.1 = (f32[16,4,256]{2,0,1:T(8,128)S(1)}, f32[16,4,256]{2,0,1:T(8,128)S(1)}, u32[]{:S(2)}, u32[]{:S(2)}) collective-permute-start(f32[16,4,256]{2,0,1:T(8,128)S(1)} %copy.128), channel_id=1, source_target_pairs={{0,1},{1,0},{2,3},{3,2},{4,5},{5,4},{6,7},{7,6},{8,9},{9,8},{10,11... | collective-permute-start | bytes 196616 | tf_op jit(solution)/shard_map/ppermute | solution.py:79
  97.7 11.2 %all-to-all-start.3 = ((f32[16,16,128]{2,1,0:T(8,128)}), f32[16,16,128]{2,1,0:T(8,128)S(1)}, u32[]{:S(2)}, u32[]{:S(2)}) async-start(f32[16,16,128]{2,1,0:T(8,128)} %broadcast_in_dim.25), calls=%async_computation.3 | async-start | bytes 262144 | tf_op jit(solution)/shard_map/all_to_all | solution.py:73
  118.3 35.9 %all-to-all-start.4 = ((bf16[32,129,128]{2,1,0:T(8,128)(2,1)}), bf16[32,129,128]{2,1,0:T(8,128)(2,1)S(1)}, u32[]{:S(2)}, u32[]{:S(2)}) async-start(bf16[32,129,128]{2,1,0:T(8,128)(2,1)} %bitcast.17), calls=%async_computation.4 | async-start | bytes 2228224 | tf_op jit(solution)/shard_map/all_to_all | solution.py:88
  169.2 41.3 %copy-start.2 = (f32[32,32]{1,0:T(8,128)S(1)}, f32[32,32]{1,0:T(8,128)}, u32[]{:S(2)}) copy-start(f32[32,32]{1,0:T(8,128)} %shard_map.102) | copy-start | bytes 12292
  169.2 5.4 %collective-permute-start.2 = (f32[16,4,256]{2,0,1:T(8,128)S(1)}, f32[16,4,256]{2,0,1:T(8,128)S(1)}, u32[]{:S(2)}, u32[]{:S(2)}) collective-permute-start(f32[16,4,256]{2,0,1:T(8,128)S(1)} %copy.130), channel_id=1, source_target_pairs={{0,1},{1,0},{2,3},{3,2},{4,5},{5,4},{6,7},{7,6},{8,9},{9,8},{10,11... | collective-permute-start | bytes 196616 | tf_op jit(solution)/shard_map/ppermute | solution.py:79
  194.8 11.0 %all-to-all-start.7 = ((f32[16,16,128]{2,1,0:T(8,128)}), f32[16,16,128]{2,1,0:T(8,128)S(1)}, u32[]{:S(2)}, u32[]{:S(2)}) async-start(f32[16,16,128]{2,1,0:T(8,128)} %broadcast_in_dim.29), calls=%async_computation.7 | async-start | bytes 262144 | tf_op jit(solution)/shard_map/all_to_all | solution.py:73
Sparse Core Ops, SparseCore 0:
  28.2 66.8 all-gather.1

commit v13 on v12

--- a/solution.py
+++ b/solution.py
@@ -29,9 +29,9 @@
     cols = lax.broadcasted_iota(jnp.int32, a.shape, 1)
     a = jnp.where(rows == cols, a + ridge, a)
     for k in range(n):
-        pivot = a[k : k + 1, k : k + 1]
-        ra = a[k : k + 1, :] / pivot
-        rb = b[k : k + 1, :] / pivot
+        inverse = 1.0 / a[k : k + 1, k : k + 1]
+        ra = a[k : k + 1, :] * inverse
+        rb = b[k : k + 1, :] * inverse
         col = a[:, k : k + 1]
         a = jnp.where(rows == k, ra, a - col * ra)
         b = jnp.where(rows == k, rb, b - col * rb)

time: 223 us -> 223 us (level)
  no operation moved by 1% of the time
where the time goes in v13:
time: 223 us; the launch traced here: 222 us
  waiting for transfers between devices  71.4 us (32%)
  blocking collectives  62.1 us (28%)
  starting transfers between devices  39.9 us (18%)
  between operations  14.5 us (7%)
  local copies, waits for them, and re-layouts  11.8 us (5%)
  matrix products  11.1 us (5%)
  Pallas kernels  8.05 us (4%)
  other arithmetic  2.9 us (1%)
    all_to_all x2, waiting for transfers between devices, predict(): got = lax.all_to_all(tiles, 'dp', split_axis=0, concat_axis=0, tiled=True)  55.9 us
    all_to_all x2, blocking collectives, gather_sum(): got = lax.all_to_all(tiles, axis, split_axis=0, concat_axis=0, tiled=True)  36.9 us
    all_to_all x2, blocking collectives, collect(): lax.all_to_all(blocks, 'member', split_axis=0, concat_axis=0, tiled=True)  25.1 us
    all_to_all x2, starting transfers between devices, predict(): got = lax.all_to_all(tiles, 'dp', split_axis=0, concat_axis=0, tiled=True)  20.8 us
    all_to_all x2, waiting for transfers between devices, gather_sum(): got = lax.all_to_all(tiles, axis, split_axis=0, concat_axis=0, tiled=True)  13.9 us
    ppermute x3, starting transfers between devices, swap_pair(): return lax.ppermute(x, 'dp', [(i, i ^ 1) for i in range(n)])  11.8 us
    pallas_call x2, Pallas kernels, solve_spd(): pl.pallas_call(kernel, out_shape=jax.ShapeDtypeStruct(sums.shape[1:], sum...  8.05 us
    all_to_all x2, starting transfers between devices, gather_sum(): got = lax.all_to_all(tiles, axis, split_axis=0, concat_axis=0, tiled=True)  7.25 us
  transfers between devices with their start and end apart: 8, of which 6 were waited for; matrix products, arithmetic and copies ran while one was open for 3% of the time, Pallas kernels for 0%

profile of v13, /device:TPU:1, one launch (start us, length us, event | category | flops | bytes accessed | tf_op | source)
XLA Modules:
  0.0 221.7 jit_solution(16706175123764212450)
XLA Ops:
  7.2 0.7 bitcast_convert_fusion
  7.9 0.8 convert.16
  8.8 0.8 convert.17
  9.7 1.1 broadcast_in_dim.22
  10.8 14.4 %all-to-all-start = ((bf16[32,129,128]{2,1,0:T(8,128)(2,1)}), bf16[32,129,128]{2,1,0:T(8,128)(2,1)S(1)}, u32[]{:S(2)}, u32[]{:S(2)}) async-start(bf16[32,129,128]{2,1,0:T(8,128)(2,1)} %bitcast.2), calls=%async_computation | async-start | bytes 2228224 | tf_op jit(solution)/shard_map/all_to_all | solution.py:88
  25.5 0.7 copy.108
  26.2 2.1 collective-permute-start
  28.4 26.4 %all-to-all-done = bf16[32,129,128]{2,1,0:T(8,128)(2,1)S(1)} async-done(((bf16[32,129,128]{2,1,0:T(8,128)(2,1)}), bf16[32,129,128]{2,1,0:T(8,128)(2,1)S(1)}, u32[]{:S(2)}, u32[]{:S(2)}) %all-to-all-start) | async-done | bytes 1056800 | tf_op jit(solution)/shard_map/all_to_all | solution.py:88
  54.8 2.5 %fusion.10 = f32[64,512]{1,0:T(8,128)S(1)} fusion(f32[32,128]{1,0:T(8,128)S(1)} %bitcast.83, bf16[32,129,128]{2,1,0:T(8,128)(2,1)S(1)} %all-to-all-done, f32[64]{0:T(128)S(1)} %fusion.46, bf16[256,64]{0,1:T(8,128)(2,1)S(1)} %collective-permute-done, bf16[256,64]{0,1:T(8,128)(2,1)S(1)} %copy-done.7), kind=kOutput, calls=%fused_computation.11 | convolution fusion | flops 541229056 | bytes 1262080 | tf_op jit(solution)/shard_map/doh,sdh->os/dot_general | solution.py:96
  57.3 14.2 %all_to_all.40 = f32[16,4,512]{2,1,0:T(4,128)S(1)} all-to-all(f32[16,4,512]{2,1,0:T(4,128)S(1)} %reshape.146), channel_id=1, replica_groups=mesh['member'=16,'dp'=32] {'member'}, dimensions={0} | all-to-all | bytes 262144 | tf_op jit(solution)/shard_map/all_to_all | solution.py:104
  71.6 5.1 %collective-permute-start.1 = (f32[16,4,256]{2,0,1:T(8,128)S(1)}, f32[16,4,256]{2,0,1:T(8,128)S(1)}, u32[]{:S(2)}, u32[]{:S(2)}) collective-permute-start(f32[16,4,256]{2,0,1:T(8,128)S(1)} %copy.128), channel_id=1, source_target_pairs={{0,1},{1,0},{2,3},{3,2},{4,5},{5,4},{6,7},{7,6},{8,9},{9,8},{10,11... | collective-permute-start | bytes 196616 | tf_op jit(solution)/shard_map/ppermute | solution.py:79
  76.8 0.8 collective-permute-done.1
  77.7 0.1 copy.101
  77.8 0.1 copy.105
  77.9 0.2 convolution_bitcast_fusion.3
  78.1 0.3 convolution_bitcast_fusion.2
  78.5 18.5 %all_to_all.41 = f32[32,16,128]{2,1,0:T(8,128)S(1)} all-to-all(f32[32,16,128]{2,1,0:T(8,128)S(1)} %broadcast_in_dim.24), channel_id=1, replica_groups=mesh['member'=16,'dp'=32] {'dp'}, dimensions={0} | all-to-all | bytes 524288 | tf_op jit(solution)/shard_map/all_to_all | solution.py:73
  97.0 0.7 broadcast_in_dim.25
  97.7 3.7 %all-to-all-start.3 = ((f32[16,16,128]{2,1,0:T(8,128)}), f32[16,16,128]{2,1,0:T(8,128)S(1)}, u32[]{:S(2)}, u32[]{:S(2)}) async-start(f32[16,16,128]{2,1,0:T(8,128)} %broadcast_in_dim.25), calls=%async_computation.3 | async-start | bytes 262144 | tf_op jit(solution)/shard_map/all_to_all | solution.py:73
  101.4 7.4 %all-to-all-done.3 = f32[16,16,128]{2,1,0:T(8,128)S(1)} async-done(((f32[16,16,128]{2,1,0:T(8,128)}), f32[16,16,128]{2,1,0:T(8,128)S(1)}, u32[]{:S(2)}, u32[]{:S(2)}) %all-to-all-start.3) | async-done | bytes 131104 | tf_op jit(solution)/shard_map/all_to_all | solution.py:73
  108.9 0.7 reshape.147.s_ref
  109.6 2.0 copy.110
  111.6 4.0 %shard_map.102 = f32[32,32]{1,0:T(8,128)} custom-call(f32[2,32,32]{2,1,0:T(8,128)} %reshape.147.s_ref, f32[32,130,128]{2,1,0:T(8,128)} %all-gather.2.cloned.1.call-done.rest_0_), custom_call_target="tpu_custom_call" | custom-call | tf_op jit(solution)/shard_map/pallas_call | solution.py:44
  115.6 1.5 convolution_add_fusion
  117.2 1.1 broadcast_in_dim.26
  118.3 6.4 %all-to-all-start.4 = ((bf16[32,129,128]{2,1,0:T(8,128)(2,1)}), bf16[32,129,128]{2,1,0:T(8,128)(2,1)S(1)}, u32[]{:S(2)}, u32[]{:S(2)}) async-start(bf16[32,129,128]{2,1,0:T(8,128)(2,1)} %bitcast.17), calls=%async_computation.4 | async-start | bytes 2228224 | tf_op jit(solution)/shard_map/all_to_all | solution.py:88
  124.7 29.5 %all-to-all-done.4 = bf16[32,129,128]{2,1,0:T(8,128)(2,1)S(1)} async-done(((bf16[32,129,128]{2,1,0:T(8,128)(2,1)}), bf16[32,129,128]{2,1,0:T(8,128)(2,1)S(1)}, u32[]{:S(2)}, u32[]{:S(2)}) %all-to-all-start.4) | async-done | bytes 1056800 | tf_op jit(solution)/shard_map/all_to_all | solution.py:88
  154.2 3.1 %fusion.11 = f32[64,512]{1,0:T(8,128)} fusion(f32[32,128]{1,0:T(8,128)S(1)} %bitcast.84, bf16[32,129,128]{2,1,0:T(8,128)(2,1)S(1)} %all-to-all-done.4, f32[64]{0:T(128)S(1)} %fusion.47, bf16[256,64]{0,1:T(8,128)(2,1)S(1)} %collective-permute-done, bf16[256,64]{0,1:T(8,128)(2,1)S(1)} %copy-done.7), kind=kOutput, calls=%fused_computation.12 | convolution fusion | flops 541229056 | bytes 1262080 | tf_op jit(solution)/shard_map/doh,sdh->os/dot_general | solution.py:96
  157.3 0.9 reshape.149
  158.3 10.9 %all_to_all.42 = f32[16,4,512]{2,1,0:T(4,128)S(1)} all-to-all(f32[16,4,512]{2,1,0:T(4,128)S(1)} %reshape.149), channel_id=1, replica_groups=mesh['member'=16,'dp'=32] {'member'}, dimensions={0} | all-to-all | bytes 262144 | tf_op jit(solution)/shard_map/all_to_all | solution.py:104
  169.3 4.5 %collective-permute-start.2 = (f32[16,4,256]{2,0,1:T(8,128)S(1)}, f32[16,4,256]{2,0,1:T(8,128)S(1)}, u32[]{:S(2)}, u32[]{:S(2)}) collective-permute-start(f32[16,4,256]{2,0,1:T(8,128)S(1)} %copy.130), channel_id=1, source_target_pairs={{0,1},{1,0},{2,3},{3,2},{4,5},{5,4},{6,7},{7,6},{8,9},{9,8},{10,11... | collective-permute-start | bytes 196616 | tf_op jit(solution)/shard_map/ppermute | solution.py:79
  173.8 0.9 collective-permute-done.2
  174.9 0.2 convolution_bitcast_fusion.1
  175.2 0.3 convolution_bitcast_fusion
  175.6 18.5 %all_to_all.43 = f32[32,16,128]{2,1,0:T(8,128)S(1)} all-to-all(f32[32,16,128]{2,1,0:T(8,128)S(1)} %broadcast_in_dim.28), channel_id=1, replica_groups=mesh['member'=16,'dp'=32] {'dp'}, dimensions={0} | all-to-all | bytes 524288 | tf_op jit(solution)/shard_map/all_to_all | solution.py:73
  194.1 0.7 broadcast_in_dim.29
  194.8 3.5 %all-to-all-start.7 = ((f32[16,16,128]{2,1,0:T(8,128)}), f32[16,16,128]{2,1,0:T(8,128)S(1)}, u32[]{:S(2)}, u32[]{:S(2)}) async-start(f32[16,16,128]{2,1,0:T(8,128)} %broadcast_in_dim.29), calls=%async_computation.7 | async-start | bytes 262144 | tf_op jit(solution)/shard_map/all_to_all | solution.py:73
  198.3 1.0 fusion.53
  199.3 6.5 %all-to-all-done.7 = f32[16,16,128]{2,1,0:T(8,128)S(1)} async-done(((f32[16,16,128]{2,1,0:T(8,128)}), f32[16,16,128]{2,1,0:T(8,128)S(1)}, u32[]{:S(2)}, u32[]{:S(2)}) %all-to-all-start.7) | async-done | bytes 131104 | tf_op jit(solution)/shard_map/all_to_all | solution.py:73
  205.8 0.7 reshape.150.s_ref
  206.5 4.0 %shard_map.103 = f32[32,32]{1,0:T(8,128)} custom-call(f32[2,32,32]{2,1,0:T(8,128)} %reshape.150.s_ref), custom_call_target="tpu_custom_call" | custom-call | tf_op jit(solution)/shard_map/pallas_call | solution.py:44
  210.5 0.9 fusion.40
  211.4 0.4 convolution_add_fusion.1
  211.8 0.4 convolution_add_fusion.2
  212.2 0.7 convolution_add_fusion.4
  212.9 0.6 copy.123
  213.5 0.6 copy.124
  214.2 0.7 convolution_add_fusion.3
  (59 shorter events, 1.3 us)
Async XLA Ops:
  7.2 18.3 %copy-start.5 = (f32[2,128]{1,0:T(2,128)S(1)}, f32[2,128]{1,0:T(2,128)}, u32[]{:S(2)}) copy-start(f32[2,128]{1,0:T(2,128)} %param.11) | copy-start | bytes 3076
  7.2 18.1 %copy-start = (f32[2,64,128]{2,1,0:T(8,128)S(1)}, f32[2,64,128]{2,1,0:T(8,128)}, u32[]{:S(2)}) copy-start(f32[2,64,128]{2,1,0:T(8,128)} %param.10) | copy-start | bytes 196612
  7.2 18.2 %copy-start.1 = (f32[2,64,128]{2,1,0:T(8,128)S(1)}, f32[2,64,128]{2,1,0:T(8,128)}, u32[]{:S(2)}) copy-start(f32[2,64,128]{2,1,0:T(8,128)} %param.12) | copy-start | bytes 196612
  7.2 18.2 %copy-start.6 = (f32[2,64]{1,0:T(2,128)S(1)}, f32[2,64]{1,0:T(2,128)}, u32[]{:S(2)}) copy-start(f32[2,64]{1,0:T(2,128)} %param.13) | copy-start | bytes 1540
  9.6 16.6 %copy-start.7 = (bf16[256,64]{0,1:T(8,128)(2,1)S(1)}, bf16[256,64]{0,1:T(8,128)(2,1)}, u32[]{:S(2)}) copy-start(bf16[256,64]{0,1:T(8,128)(2,1)} %param.7) | copy-start | bytes 98308
  10.8 44.0 %all-to-all-start = ((bf16[32,129,128]{2,1,0:T(8,128)(2,1)}), bf16[32,129,128]{2,1,0:T(8,128)(2,1)S(1)}, u32[]{:S(2)}, u32[]{:S(2)}) async-start(bf16[32,129,128]{2,1,0:T(8,128)(2,1)} %bitcast.2), calls=%async_computation | async-start | bytes 2228224 | tf_op jit(solution)/shard_map/all_to_all | solution.py:88
  25.2 84.3 %all-gather.2.cloned.1.call-start = ((), (), s32[]{:S(2)}) async-start(), calls=%async_computation.8 | async-start | bytes 2367488 | tf_op jit(solution)/shard_map/all_gather | solution.py:122
  26.2 28.6 %collective-permute-start = (bf16[256,64]{0,1:T(8,128)(2,1)S(1)}, bf16[256,64]{0,1:T(8,128)(2,1)S(1)}, u32[]{:S(2)}, u32[]{:S(2)}) collective-permute-start(bf16[256,64]{0,1:T(8,128)(2,1)S(1)} %copy-done.7), channel_id=1, source_target_pairs={{0,1},{1,0},{2,3},{3,2},{4,5},{5,4},{6,7},{7,6},{8,9},{9,8},{10,11... | collective-permute-start | bytes 98312 | tf_op jit(solution)/shard_map/ppermute | solution.py:79
  54.8 21.9 %copy-start.3 = (bf16[2,32,4,256]{3,2,1,0:T(4,128)(2,1)S(1)}, bf16[2,32,4,256]{3,2,1,0:T(4,128)(2,1)}, u32[]{:S(2)}) copy-start(bf16[2,32,4,256]{3,2,1,0:T(4,128)(2,1)} %param.9) | copy-start | bytes 393220
  54.8 22.8 %copy-start.4 = (f32[4,256]{1,0:T(4,128)S(1)}, f32[4,256]{1,0:T(4,128)}, u32[]{:S(2)}) copy-start(f32[4,256]{1,0:T(4,128)} %param.8) | copy-start | bytes 12292
  71.6 6.0 %collective-permute-start.1 = (f32[16,4,256]{2,0,1:T(8,128)S(1)}, f32[16,4,256]{2,0,1:T(8,128)S(1)}, u32[]{:S(2)}, u32[]{:S(2)}) collective-permute-start(f32[16,4,256]{2,0,1:T(8,128)S(1)} %copy.128), channel_id=1, source_target_pairs={{0,1},{1,0},{2,3},{3,2},{4,5},{5,4},{6,7},{7,6},{8,9},{9,8},{10,11... | collective-permute-start | bytes 196616 | tf_op jit(solution)/shard_map/ppermute | solution.py:79
  97.7 11.2 %all-to-all-start.3 = ((f32[16,16,128]{2,1,0:T(8,128)}), f32[16,16,128]{2,1,0:T(8,128)S(1)}, u32[]{:S(2)}, u32[]{:S(2)}) async-start(f32[16,16,128]{2,1,0:T(8,128)} %broadcast_in_dim.25), calls=%async_computation.3 | async-start | bytes 262144 | tf_op jit(solution)/shard_map/all_to_all | solution.py:73
  118.3 35.9 %all-to-all-start.4 = ((bf16[32,129,128]{2,1,0:T(8,128)(2,1)}), bf16[32,129,128]{2,1,0:T(8,128)(2,1)S(1)}, u32[]{:S(2)}, u32[]{:S(2)}) async-start(bf16[32,129,128]{2,1,0:T(8,128)(2,1)} %bitcast.17), calls=%async_computation.4 | async-start | bytes 2228224 | tf_op jit(solution)/shard_map/all_to_all | solution.py:88
  169.2 41.3 %copy-start.2 = (f32[32,32]{1,0:T(8,128)S(1)}, f32[32,32]{1,0:T(8,128)}, u32[]{:S(2)}) copy-start(f32[32,32]{1,0:T(8,128)} %shard_map.102) | copy-start | bytes 12292
  169.3 5.4 %collective-permute-start.2 = (f32[16,4,256]{2,0,1:T(8,128)S(1)}, f32[16,4,256]{2,0,1:T(8,128)S(1)}, u32[]{:S(2)}, u32[]{:S(2)}) collective-permute-start(f32[16,4,256]{2,0,1:T(8,128)S(1)} %copy.130), channel_id=1, source_target_pairs={{0,1},{1,0},{2,3},{3,2},{4,5},{5,4},{6,7},{7,6},{8,9},{9,8},{10,11... | collective-permute-start | bytes 196616 | tf_op jit(solution)/shard_map/ppermute | solution.py:79
  194.8 11.0 %all-to-all-start.7 = ((f32[16,16,128]{2,1,0:T(8,128)}), f32[16,16,128]{2,1,0:T(8,128)S(1)}, u32[]{:S(2)}, u32[]{:S(2)}) async-start(f32[16,16,128]{2,1,0:T(8,128)} %broadcast_in_dim.29), calls=%async_computation.7 | async-start | bytes 262144 | tf_op jit(solution)/shard_map/all_to_all | solution.py:73
Sparse Core Ops, SparseCore 0:
  28.2 66.8 all-gather.1

commit v14 on v12

--- a/solution.py
+++ b/solution.py
@@ -22,9 +22,10 @@
 
 def _eliminate(s_ref, *rest, scale, ridge):
     o_ref = rest[-1]
-    a = s_ref[0] * scale
-    b = s_ref[1] * scale
-    n = a.shape[0]
+    n = o_ref.shape[0]
+    total = jnp.sum(s_ref[...], axis=0)
+    a = total[:, :n] * scale
+    b = total[:, n : 2 * n] * scale
     rows = lax.broadcasted_iota(jnp.int32, a.shape, 0)
     cols = lax.broadcasted_iota(jnp.int32, a.shape, 1)
     a = jnp.where(rows == cols, a + ridge, a)
@@ -43,7 +44,7 @@
     specs = [pl.BlockSpec(memory_space=pltpu.VMEM)] + [pl.BlockSpec(memory_space=pl.ANY) for _ in after]
     return pl.pallas_call(
         kernel,
-        out_shape=jax.ShapeDtypeStruct(sums.shape[1:], sums.dtype),
+        out_shape=jax.ShapeDtypeStruct((sums.shape[1], sums.shape[1]), sums.dtype),
         in_specs=specs,
         out_specs=pl.BlockSpec(memory_space=pltpu.VMEM),
     )(sums, *after)
@@ -72,6 +73,12 @@
     tiles = jnp.broadcast_to(flat[None], (n,) + flat.shape)
     got = lax.all_to_all(tiles, axis, split_axis=0, concat_axis=0, tiled=True)
     return jnp.sum(got, axis=0).reshape(x.shape)
+
+
+def gather_stack(x, axis):
+    n = lax.axis_size(axis)
+    tiles = jnp.broadcast_to(x[None], (n,) + x.shape)
+    return lax.all_to_all(tiles, axis, split_axis=0, concat_axis=0, tiled=True)
 
 
 def swap_pair(x):
@@ -135,7 +142,9 @@
         cross_part = lax.dot_general(
             anomaly, misfit, (((1,), (1,)), ((), ())), precision=lax.Precision.HIGHEST
         )
-        sums = gather_sum(gather_sum(jnp.stack([gram_part, cross_part]), "dp"), "member")
+        pad = jnp.zeros((gram_part.shape[0], 128 - 2 * gram_part.shape[1]), gram_part.dtype)
+        payload = jnp.concatenate([gram_part, cross_part, pad], axis=1)
+        sums = gather_stack(gather_sum(payload, "dp"), "member")
         gain = solve_spd(sums, 1.0 / count, ridge_level, (whole,) if update == 0 else ())
         if update == 0:
             first_gain = gain

time: 223 us -> 235 us (1.054)
  blocking collectives: 62 us -> 70.9 us
    all_to_all x2, blocking collectives: 36.9 us -> 45.4 us  [gather_sum(): got = lax.all_to_all(tiles, axis, split_axis=0, concat_axis=0, tiled=True)]
  transfers between devices with their start and end apart: 8 -> 8, of which waited for: 6 -> 6; matrix products, arithmetic and copies ran while one was open for 3% -> 4% of each run, Pallas kernels for 0% -> 0%
where the time goes in v14:
time: 235 us; the launch traced here: 231 us
  blocking collectives  70.9 us (30%)
  waiting for transfers between devices  70 us (30%)
  starting transfers between devices  41.3 us (18%)
  between operations  14.5 us (6%)
  local copies, waits for them, and re-layouts  12 us (5%)
  matrix products  11.1 us (5%)
  Pallas kernels  8.56 us (4%)
  other arithmetic  3 us (1%)
    all_to_all x2, waiting for transfers between devices, predict(): got = lax.all_to_all(tiles, 'dp', split_axis=0, concat_axis=0, tiled=True)  55.9 us
    all_to_all x2, blocking collectives, gather_sum(): got = lax.all_to_all(tiles, axis, split_axis=0, concat_axis=0, tiled=True)  45.4 us
    all_to_all x2, blocking collectives, collect(): lax.all_to_all(blocks, 'member', split_axis=0, concat_axis=0, tiled=True)  25.5 us
    all_to_all x2, starting transfers between devices, predict(): got = lax.all_to_all(tiles, 'dp', split_axis=0, concat_axis=0, tiled=True)  22.9 us
    all_to_all x2, waiting for transfers between devices, gather_stack(): return lax.all_to_all(tiles, axis, split_axis=0, concat_axis=0, tiled=True)  12.5 us
    ppermute x3, starting transfers between devices, swap_pair(): return lax.ppermute(x, 'dp', [(i, i ^ 1) for i in range(n)])  11.4 us
    pallas_call x2, Pallas kernels, solve_spd(): pl.pallas_call(kernel, out_shape=jax.ShapeDtypeStruct((sums.shape[1], sum...  8.56 us
    all_to_all x2, starting transfers between devices, gather_stack(): return lax.all_to_all(tiles, axis, split_axis=0, concat_axis=0, tiled=True)  7.06 us
  transfers between devices with their start and end apart: 8, of which 6 were waited for; matrix products, arithmetic and copies ran while one was open for 4% of the time, Pallas kernels for 0%

profile of v14, /device:TPU:1, one launch (start us, length us, event | category | flops | bytes accessed | tf_op | source)
XLA Modules:
  0.0 231.4 jit_solution(9550162361615233832)
XLA Ops:
  7.2 0.7 bitcast_convert_fusion
  7.9 0.8 convert.16
  8.8 0.8 convert.17
  9.6 1.1 broadcast_in_dim.18
  10.8 14.4 %all-to-all-start = ((bf16[32,129,128]{2,1,0:T(8,128)(2,1)}), bf16[32,129,128]{2,1,0:T(8,128)(2,1)S(1)}, u32[]{:S(2)}, u32[]{:S(2)}) async-start(bf16[32,129,128]{2,1,0:T(8,128)(2,1)} %bitcast.2), calls=%async_computation | async-start | bytes 2228224 | tf_op jit(solution)/shard_map/all_to_all | solution.py:95
  25.3 2.1 collective-permute-start
  27.7 0.7 copy.166
  28.4 26.4 %all-to-all-done = bf16[32,129,128]{2,1,0:T(8,128)(2,1)S(1)} async-done(((bf16[32,129,128]{2,1,0:T(8,128)(2,1)}), bf16[32,129,128]{2,1,0:T(8,128)(2,1)S(1)}, u32[]{:S(2)}, u32[]{:S(2)}) %all-to-all-start) | async-done | bytes 1056800 | tf_op jit(solution)/shard_map/all_to_all | solution.py:95
  54.8 2.5 %fusion.10 = f32[64,512]{1,0:T(8,128)S(1)} fusion(f32[32,128]{1,0:T(8,128)S(1)} %bitcast.79, bf16[32,129,128]{2,1,0:T(8,128)(2,1)S(1)} %all-to-all-done, f32[64]{0:T(128)S(1)} %fusion.46, bf16[256,64]{0,1:T(8,128)(2,1)S(1)} %collective-permute-done, bf16[256,64]{0,1:T(8,128)(2,1)S(1)} %copy-done.9), kind=kOutput, calls=%fused_computation.11 | convolution fusion | flops 541229056 | bytes 1262080 | tf_op jit(solution)/shard_map/doh,sdh->os/dot_general | solution.py:103
  57.3 14.2 %all_to_all.40 = f32[16,4,512]{2,1,0:T(4,128)S(1)} all-to-all(f32[16,4,512]{2,1,0:T(4,128)S(1)} %reshape.140), channel_id=1, replica_groups=mesh['member'=16,'dp'=32] {'member'}, dimensions={0} | all-to-all | bytes 262144 | tf_op jit(solution)/shard_map/all_to_all | solution.py:111
  71.6 4.7 %collective-permute-start.1 = (f32[16,4,256]{2,0,1:T(8,128)S(1)}, f32[16,4,256]{2,0,1:T(8,128)S(1)}, u32[]{:S(2)}, u32[]{:S(2)}) collective-permute-start(f32[16,4,256]{2,0,1:T(8,128)S(1)} %copy.186), channel_id=1, source_target_pairs={{0,1},{1,0},{2,3},{3,2},{4,5},{5,4},{6,7},{7,6},{8,9},{9,8},{10,11... | collective-permute-start | bytes 196616 | tf_op jit(solution)/shard_map/ppermute | solution.py:86
  76.4 0.7 collective-permute-done.1
  77.3 0.1 copy.159
  77.5 0.2 convolution_bitcast_fusion.3
  77.7 0.3 convolution_bitcast_fusion.2
  78.1 22.9 %all_to_all.41 = f32[32,32,128]{2,1,0:T(8,128)S(1)} all-to-all(f32[32,32,128]{2,1,0:T(8,128)S(1)} %broadcast_in_dim.19), channel_id=1, replica_groups=mesh['member'=16,'dp'=32] {'dp'}, dimensions={0} | all-to-all | bytes 1048576 | tf_op jit(solution)/shard_map/all_to_all | solution.py:74
  101.1 0.7 broadcast_in_dim.20
  101.8 3.5 %all-to-all-start.3 = ((f32[16,32,128]{2,1,0:T(8,128)}), f32[16,32,128]{2,1,0:T(8,128)S(1)}, u32[]{:S(2)}, u32[]{:S(2)}) async-start(f32[16,32,128]{2,1,0:T(8,128)} %broadcast_in_dim.20), calls=%async_computation.3 | async-start | bytes 524288 | tf_op jit(solution)/shard_map/all_to_all | solution.py:81
  105.4 2.0 copy.168
  107.5 5.7 %all-to-all-done.3.s_ref = f32[16,32,128]{2,1,0:T(8,128)S(1)} async-done(((f32[16,32,128]{2,1,0:T(8,128)}), f32[16,32,128]{2,1,0:T(8,128)S(1)}, u32[]{:S(2)}, u32[]{:S(2)}) %all-to-all-start.3) | async-done | bytes 262176 | tf_op jit(solution)/shard_map/all_to_all | solution.py:81
  113.2 0.7 copy-done
  113.9 4.3 %shard_map.102 = f32[32,32]{1,0:T(8,128)} custom-call(f32[16,32,128]{2,1,0:T(8,128)} %copy-done, f32[32,130,128]{2,1,0:T(8,128)} %all-gather.2.cloned.1.call-done.rest_0_), custom_call_target="tpu_custom_call" | custom-call | tf_op jit(solution)/shard_map/pallas_call | solution.py:45
  118.2 1.5 convolution_add_fusion
  119.7 1.1 broadcast_in_dim.21
  120.9 8.4 %all-to-all-start.4 = ((bf16[32,129,128]{2,1,0:T(8,128)(2,1)}), bf16[32,129,128]{2,1,0:T(8,128)(2,1)S(1)}, u32[]{:S(2)}, u32[]{:S(2)}) async-start(bf16[32,129,128]{2,1,0:T(8,128)(2,1)} %bitcast.15), calls=%async_computation.4 | async-start | bytes 2228224 | tf_op jit(solution)/shard_map/all_to_all | solution.py:95
  129.3 29.5 %all-to-all-done.4 = bf16[32,129,128]{2,1,0:T(8,128)(2,1)S(1)} async-done(((bf16[32,129,128]{2,1,0:T(8,128)(2,1)}), bf16[32,129,128]{2,1,0:T(8,128)(2,1)S(1)}, u32[]{:S(2)}, u32[]{:S(2)}) %all-to-all-start.4) | async-done | bytes 1056800 | tf_op jit(solution)/shard_map/all_to_all | solution.py:95
  158.9 3.1 %fusion.11 = f32[64,512]{1,0:T(8,128)} fusion(f32[32,128]{1,0:T(8,128)S(1)} %bitcast.80, bf16[32,129,128]{2,1,0:T(8,128)(2,1)S(1)} %all-to-all-done.4, f32[64]{0:T(128)S(1)} %fusion.47, bf16[256,64]{0,1:T(8,128)(2,1)S(1)} %collective-permute-done, bf16[256,64]{0,1:T(8,128)(2,1)S(1)} %copy-done.9), kind=kOutput, calls=%fused_computation.12 | convolution fusion | flops 541229056 | bytes 1262080 | tf_op jit(solution)/shard_map/doh,sdh->os/dot_general | solution.py:103
  162.0 0.9 reshape.142
  162.9 11.3 %all_to_all.42 = f32[16,4,512]{2,1,0:T(4,128)S(1)} all-to-all(f32[16,4,512]{2,1,0:T(4,128)S(1)} %reshape.142), channel_id=1, replica_groups=mesh['member'=16,'dp'=32] {'member'}, dimensions={0} | all-to-all | bytes 262144 | tf_op jit(solution)/shard_map/all_to_all | solution.py:111
  174.2 4.5 %collective-permute-start.2 = (f32[16,4,256]{2,0,1:T(8,128)S(1)}, f32[16,4,256]{2,0,1:T(8,128)S(1)}, u32[]{:S(2)}, u32[]{:S(2)}) collective-permute-start(f32[16,4,256]{2,0,1:T(8,128)S(1)} %copy.188), channel_id=1, source_target_pairs={{0,1},{1,0},{2,3},{3,2},{4,5},{5,4},{6,7},{7,6},{8,9},{9,8},{10,11... | collective-permute-start | bytes 196616 | tf_op jit(solution)/shard_map/ppermute | solution.py:86
  178.8 0.9 collective-permute-done.2
  179.8 0.1 copy.172
  179.9 0.2 convolution_bitcast_fusion.1
  180.2 0.3 convolution_bitcast_fusion
  180.6 22.5 %all_to_all.43 = f32[32,32,128]{2,1,0:T(8,128)S(1)} all-to-all(f32[32,32,128]{2,1,0:T(8,128)S(1)} %broadcast_in_dim.22), channel_id=1, replica_groups=mesh['member'=16,'dp'=32] {'dp'}, dimensions={0} | all-to-all | bytes 1048576 | tf_op jit(solution)/shard_map/all_to_all | solution.py:74
  203.2 0.7 broadcast_in_dim.23
  203.9 3.5 %all-to-all-start.7 = ((f32[16,32,128]{2,1,0:T(8,128)}), f32[16,32,128]{2,1,0:T(8,128)S(1)}, u32[]{:S(2)}, u32[]{:S(2)}) async-start(f32[16,32,128]{2,1,0:T(8,128)} %broadcast_in_dim.23), calls=%async_computation.7 | async-start | bytes 524288 | tf_op jit(solution)/shard_map/all_to_all | solution.py:81
  207.5 1.0 fusion.53
  208.5 6.8 %all-to-all-done.7.s_ref = f32[16,32,128]{2,1,0:T(8,128)S(1)} async-done(((f32[16,32,128]{2,1,0:T(8,128)}), f32[16,32,128]{2,1,0:T(8,128)S(1)}, u32[]{:S(2)}, u32[]{:S(2)}) %all-to-all-start.7) | async-done | bytes 262176 | tf_op jit(solution)/shard_map/all_to_all | solution.py:81
  215.3 0.7 copy-done.1
  216.0 4.3 %shard_map.103 = f32[32,32]{1,0:T(8,128)} custom-call(f32[16,32,128]{2,1,0:T(8,128)} %copy-done.1), custom_call_target="tpu_custom_call" | custom-call | tf_op jit(solution)/shard_map/pallas_call | solution.py:45
  220.2 0.9 fusion.40
  221.2 0.4 convolution_add_fusion.1
  221.6 0.4 convolution_add_fusion.2
  221.9 0.7 convolution_add_fusion.4
  222.6 0.6 copy.181
  223.3 0.6 copy.182
  223.9 0.7 convolution_add_fusion.3
  (59 shorter events, 1.4 us)
Async XLA Ops:
  7.2 20.4 %copy-start.7 = (f32[2,128]{1,0:T(2,128)S(1)}, f32[2,128]{1,0:T(2,128)}, u32[]{:S(2)}) copy-start(f32[2,128]{1,0:T(2,128)} %param.11) | copy-start | bytes 3076
  7.2 20.3 %copy-start.2 = (f32[2,64,128]{2,1,0:T(8,128)S(1)}, f32[2,64,128]{2,1,0:T(8,128)}, u32[]{:S(2)}) copy-start(f32[2,64,128]{2,1,0:T(8,128)} %param.10) | copy-start | bytes 196612
  7.2 20.3 %copy-start.3 = (f32[2,64,128]{2,1,0:T(8,128)S(1)}, f32[2,64,128]{2,1,0:T(8,128)}, u32[]{:S(2)}) copy-start(f32[2,64,128]{2,1,0:T(8,128)} %param.12) | copy-start | bytes 196612
  7.2 18.1 %copy-start.9 = (bf16[256,64]{0,1:T(8,128)(2,1)S(1)}, bf16[256,64]{0,1:T(8,128)(2,1)}, u32[]{:S(2)}) copy-start(bf16[256,64]{0,1:T(8,128)(2,1)} %param.7) | copy-start | bytes 98308
  7.2 20.4 %copy-start.8 = (f32[2,64]{1,0:T(2,128)S(1)}, f32[2,64]{1,0:T(2,128)}, u32[]{:S(2)}) copy-start(f32[2,64]{1,0:T(2,128)} %param.13) | copy-start | bytes 1540
  10.8 44.0 %all-to-all-start = ((bf16[32,129,128]{2,1,0:T(8,128)(2,1)}), bf16[32,129,128]{2,1,0:T(8,128)(2,1)S(1)}, u32[]{:S(2)}, u32[]{:S(2)}) async-start(bf16[32,129,128]{2,1,0:T(8,128)(2,1)} %bitcast.2), calls=%async_computation | async-start | bytes 2228224 | tf_op jit(solution)/shard_map/all_to_all | solution.py:95
  25.2 80.2 %all-gather.2.cloned.1.call-start = ((), (), s32[]{:S(2)}) async-start(), calls=%async_computation.8 | async-start | bytes 2367488 | tf_op jit(solution)/shard_map/all_gather | solution.py:129
  25.3 29.5 %collective-permute-start = (bf16[256,64]{0,1:T(8,128)(2,1)S(1)}, bf16[256,64]{0,1:T(8,128)(2,1)S(1)}, u32[]{:S(2)}, u32[]{:S(2)}) collective-permute-start(bf16[256,64]{0,1:T(8,128)(2,1)S(1)} %copy-done.9), channel_id=1, source_target_pairs={{0,1},{1,0},{2,3},{3,2},{4,5},{5,4},{6,7},{7,6},{8,9},{9,8},{10,11... | collective-permute-start | bytes 98312 | tf_op jit(solution)/shard_map/ppermute | solution.py:86
  54.8 21.5 %copy-start.5 = (bf16[2,32,4,256]{3,2,1,0:T(4,128)(2,1)S(1)}, bf16[2,32,4,256]{3,2,1,0:T(4,128)(2,1)}, u32[]{:S(2)}) copy-start(bf16[2,32,4,256]{3,2,1,0:T(4,128)(2,1)} %param.9) | copy-start | bytes 393220
  54.8 22.4 %copy-start.6 = (f32[4,256]{1,0:T(4,128)S(1)}, f32[4,256]{1,0:T(4,128)}, u32[]{:S(2)}) copy-start(f32[4,256]{1,0:T(4,128)} %param.8) | copy-start | bytes 12292
  71.6 5.6 %collective-permute-start.1 = (f32[16,4,256]{2,0,1:T(8,128)S(1)}, f32[16,4,256]{2,0,1:T(8,128)S(1)}, u32[]{:S(2)}, u32[]{:S(2)}) collective-permute-start(f32[16,4,256]{2,0,1:T(8,128)S(1)} %copy.186), channel_id=1, source_target_pairs={{0,1},{1,0},{2,3},{3,2},{4,5},{5,4},{6,7},{7,6},{8,9},{9,8},{10,11... | collective-permute-start | bytes 196616 | tf_op jit(solution)/shard_map/ppermute | solution.py:86
  101.8 11.3 %all-to-all-start.3 = ((f32[16,32,128]{2,1,0:T(8,128)}), f32[16,32,128]{2,1,0:T(8,128)S(1)}, u32[]{:S(2)}, u32[]{:S(2)}) async-start(f32[16,32,128]{2,1,0:T(8,128)} %broadcast_in_dim.20), calls=%async_computation.3 | async-start | bytes 524288 | tf_op jit(solution)/shard_map/all_to_all | solution.py:81
  113.2 0.7 copy-start
  120.9 38.0 %all-to-all-start.4 = ((bf16[32,129,128]{2,1,0:T(8,128)(2,1)}), bf16[32,129,128]{2,1,0:T(8,128)(2,1)S(1)}, u32[]{:S(2)}, u32[]{:S(2)}) async-start(bf16[32,129,128]{2,1,0:T(8,128)(2,1)} %bitcast.15), calls=%async_computation.4 | async-start | bytes 2228224 | tf_op jit(solution)/shard_map/all_to_all | solution.py:95
  174.2 5.4 %collective-permute-start.2 = (f32[16,4,256]{2,0,1:T(8,128)S(1)}, f32[16,4,256]{2,0,1:T(8,128)S(1)}, u32[]{:S(2)}, u32[]{:S(2)}) collective-permute-start(f32[16,4,256]{2,0,1:T(8,128)S(1)} %copy.188), channel_id=1, source_target_pairs={{0,1},{1,0},{2,3},{3,2},{4,5},{5,4},{6,7},{7,6},{8,9},{9,8},{10,11... | collective-permute-start | bytes 196616 | tf_op jit(solution)/shard_map/ppermute | solution.py:86
  179.8 40.5 %copy-start.4 = (f32[32,32]{1,0:T(8,128)S(1)}, f32[32,32]{1,0:T(8,128)}, u32[]{:S(2)}) copy-start(f32[32,32]{1,0:T(8,128)} %shard_map.102) | copy-start | bytes 12292
  203.9 11.3 %all-to-all-start.7 = ((f32[16,32,128]{2,1,0:T(8,128)}), f32[16,32,128]{2,1,0:T(8,128)S(1)}, u32[]{:S(2)}, u32[]{:S(2)}) async-start(f32[16,32,128]{2,1,0:T(8,128)} %broadcast_in_dim.23), calls=%async_computation.7 | async-start | bytes 524288 | tf_op jit(solution)/shard_map/all_to_all | solution.py:81
  215.3 0.7 copy-start.1
Sparse Core Ops, SparseCore 0:
  28.5 67.9 all-gather.1

commit v15 on v12

--- a/solution.py
+++ b/solution.py
@@ -135,7 +135,15 @@
         cross_part = lax.dot_general(
             anomaly, misfit, (((1,), (1,)), ((), ())), precision=lax.Precision.HIGHEST
         )
-        sums = gather_sum(gather_sum(jnp.stack([gram_part, cross_part]), "dp"), "member")
+        h = gram_part.shape[0] // 2
+        payload = jnp.concatenate(
+            [gram_part[:h].reshape(-1), gram_part[h:, h:].reshape(-1), cross_part.reshape(-1)]
+        )
+        payload = gather_sum(gather_sum(payload, "dp"), "member")
+        top = payload[: 2 * h * h].reshape(h, 2 * h)
+        corner = payload[2 * h * h : 3 * h * h].reshape(h, h)
+        gram = jnp.concatenate([top, jnp.concatenate([top[:, h:].T, corner], axis=1)], axis=0)
+        sums = jnp.stack([gram, payload[3 * h * h :].reshape(cross_part.shape)])
         gain = solve_spd(sums, 1.0 / count, ridge_level, (whole,) if update == 0 else ())
         if update == 0:
             first_gain = gain

time: 223 us -> 224 us (level)
  blocking collectives: 62 us -> 43.2 us
  waiting for transfers between devices: 71.4 us -> 84.4 us
  starting transfers between devices: 39.9 us -> 45.1 us
    all_to_all x2 -> x1, blocking collectives: 36.9 us -> 18.5 us  [gather_sum(): got = lax.all_to_all(tiles, axis, split_axis=0, concat_axis=0, tiled=True)]
    all_to_all x2 -> x3, waiting for transfers between devices: 13.9 us -> 26.8 us  [gather_sum(): got = lax.all_to_all(tiles, axis, split_axis=0, concat_axis=0, tiled=True)]
    all_to_all x2 -> x3, starting transfers between devices: 7.25 us -> 13 us  [gather_sum(): got = lax.all_to_all(tiles, axis, split_axis=0, concat_axis=0, tiled=True)]
  transfers between devices with their start and end apart: 8 -> 9, of which waited for: 6 -> 7; matrix products, arithmetic and copies ran while one was open for 3% -> 3% of each run, Pallas kernels for 0% -> 0%
where the time goes in v15:
time: 224 us; the launch traced here: 223 us
  waiting for transfers between devices  84.4 us (38%)
  starting transfers between devices  45.1 us (20%)
  blocking collectives  43.2 us (19%)
  between operations  14.5 us (6%)
  local copies, waits for them, and re-layouts  12.4 us (6%)
  matrix products  11.1 us (5%)
  Pallas kernels  8 us (4%)
  other arithmetic  4.33 us (2%)
    all_to_all x2, waiting for transfers between devices, predict(): got = lax.all_to_all(tiles, 'dp', split_axis=0, concat_axis=0, tiled=True)  55.9 us
    all_to_all x3, waiting for transfers between devices, gather_sum(): got = lax.all_to_all(tiles, axis, split_axis=0, concat_axis=0, tiled=True)  26.8 us
    all_to_all x2, blocking collectives, collect(): lax.all_to_all(blocks, 'member', split_axis=0, concat_axis=0, tiled=True)  24.7 us
    all_to_all x2, starting transfers between devices, predict(): got = lax.all_to_all(tiles, 'dp', split_axis=0, concat_axis=0, tiled=True)  20.3 us
    all_to_all x1, blocking collectives, gather_sum(): got = lax.all_to_all(tiles, axis, split_axis=0, concat_axis=0, tiled=True)  18.5 us
    all_to_all x3, starting transfers between devices, gather_sum(): got = lax.all_to_all(tiles, axis, split_axis=0, concat_axis=0, tiled=True)  13 us
    ppermute x3, starting transfers between devices, swap_pair(): return lax.ppermute(x, 'dp', [(i, i ^ 1) for i in range(n)])  11.8 us
    pallas_call x2, Pallas kernels, solve_spd(): pl.pallas_call(kernel, out_shape=jax.ShapeDtypeStruct(sums.shape[1:], sum...  8 us
  transfers between devices with their start and end apart: 9, of which 7 were waited for; matrix products, arithmetic and copies ran while one was open for 3% of the time, Pallas kernels for 0%

profile of v15, /device:TPU:1, one launch (start us, length us, event | category | flops | bytes accessed | tf_op | source)
XLA Modules:
  0.0 222.9 jit_solution(16032166813191279827)
XLA Ops:
  7.2 0.7 bitcast_convert_fusion
  7.9 0.8 convert.16
  8.8 0.8 convert.17
  9.7 1.1 broadcast_in_dim.22
  10.8 14.4 %all-to-all-start = ((bf16[32,129,128]{2,1,0:T(8,128)(2,1)}), bf16[32,129,128]{2,1,0:T(8,128)(2,1)S(1)}, u32[]{:S(2)}, u32[]{:S(2)}) async-start(bf16[32,129,128]{2,1,0:T(8,128)(2,1)} %bitcast.2), calls=%async_computation | async-start | bytes 2228224 | tf_op jit(solution)/shard_map/all_to_all | solution.py:88
  25.5 0.7 copy.167
  26.2 2.1 collective-permute-start
  28.4 26.4 %all-to-all-done = bf16[32,129,128]{2,1,0:T(8,128)(2,1)S(1)} async-done(((bf16[32,129,128]{2,1,0:T(8,128)(2,1)}), bf16[32,129,128]{2,1,0:T(8,128)(2,1)S(1)}, u32[]{:S(2)}, u32[]{:S(2)}) %all-to-all-start) | async-done | bytes 1056800 | tf_op jit(solution)/shard_map/all_to_all | solution.py:88
  54.8 2.5 %fusion.10 = f32[64,512]{1,0:T(8,128)S(1)} fusion(f32[32,128]{1,0:T(8,128)S(1)} %bitcast.91, bf16[32,129,128]{2,1,0:T(8,128)(2,1)S(1)} %all-to-all-done, f32[64]{0:T(128)S(1)} %fusion.46, bf16[256,64]{0,1:T(8,128)(2,1)S(1)} %collective-permute-done, bf16[256,64]{0,1:T(8,128)(2,1)S(1)} %copy-done.7), kind=kOutput, calls=%fused_computation.11 | convolution fusion | flops 541229056 | bytes 1262080 | tf_op jit(solution)/shard_map/doh,sdh->os/dot_general | solution.py:96
  57.3 14.2 %all_to_all.40 = f32[16,4,512]{2,1,0:T(4,128)S(1)} all-to-all(f32[16,4,512]{2,1,0:T(4,128)S(1)} %reshape.184), channel_id=1, replica_groups=mesh['member'=16,'dp'=32] {'member'}, dimensions={0} | all-to-all | bytes 262144 | tf_op jit(solution)/shard_map/all_to_all | solution.py:104
  71.6 5.1 %collective-permute-start.1 = (f32[16,4,256]{2,0,1:T(8,128)S(1)}, f32[16,4,256]{2,0,1:T(8,128)S(1)}, u32[]{:S(2)}, u32[]{:S(2)}) collective-permute-start(f32[16,4,256]{2,0,1:T(8,128)S(1)} %copy.194), channel_id=1, source_target_pairs={{0,1},{1,0},{2,3},{3,2},{4,5},{5,4},{6,7},{7,6},{8,9},{9,8},{10,11... | collective-permute-start | bytes 196616 | tf_op jit(solution)/shard_map/ppermute | solution.py:79
  76.8 0.8 collective-permute-done.1
  77.8 0.2 convolution_bitcast_fusion.3
  78.4 0.3 convolution_bitcast_fusion.2
  78.7 18.5 %all_to_all.41 = f32[32,14,128]{2,1,0:T(8,128)S(1)} all-to-all(f32[32,14,128]{2,1,0:T(8,128)S(1)} %broadcast_in_dim.24), channel_id=1, replica_groups=mesh['member'=16,'dp'=32] {'dp'}, dimensions={0} | all-to-all | bytes 458752 | tf_op jit(solution)/shard_map/all_to_all | solution.py:73
  97.3 0.7 broadcast_in_dim.25
  97.9 3.7 %all-to-all-start.3 = ((f32[16,14,128]{2,1,0:T(8,128)}), f32[16,14,128]{2,1,0:T(8,128)S(1)}, u32[]{:S(2)}, u32[]{:S(2)}) async-start(f32[16,14,128]{2,1,0:T(8,128)} %broadcast_in_dim.25), calls=%async_computation.3 | async-start | bytes 262144 | tf_op jit(solution)/shard_map/all_to_all | solution.py:73
  101.7 7.4 %all-to-all-done.3 = f32[16,14,128]{2,1,0:T(8,128)S(1)} async-done(((f32[16,14,128]{2,1,0:T(8,128)}), f32[16,14,128]{2,1,0:T(8,128)S(1)}, u32[]{:S(2)}, u32[]{:S(2)}) %all-to-all-start.3) | async-done | bytes 114720 | tf_op jit(solution)/shard_map/all_to_all | solution.py:73
  109.6 0.6 pad_maximum_fusion.4.s_ref
  110.2 2.0 copy.169
  112.3 4.0 %shard_map.102 = f32[32,32]{1,0:T(8,128)} custom-call(f32[2,32,32]{2,1,0:T(8,128)} %pad_maximum_fusion.4.s_ref, f32[32,130,128]{2,1,0:T(8,128)} %all-gather.2.cloned.1.call-done.rest_0_), custom_call_target="tpu_custom_call" | custom-call | tf_op jit(solution)/shard_map/pallas_call | solution.py:44
  116.3 1.5 convolution_add_fusion
  117.8 1.1 broadcast_in_dim.26
  119.0 5.9 %all-to-all-start.4 = ((bf16[32,129,128]{2,1,0:T(8,128)(2,1)}), bf16[32,129,128]{2,1,0:T(8,128)(2,1)S(1)}, u32[]{:S(2)}, u32[]{:S(2)}) async-start(bf16[32,129,128]{2,1,0:T(8,128)(2,1)} %bitcast.18), calls=%async_computation.4 | async-start | bytes 2228224 | tf_op jit(solution)/shard_map/all_to_all | solution.py:88
  124.8 29.5 %all-to-all-done.4 = bf16[32,129,128]{2,1,0:T(8,128)(2,1)S(1)} async-done(((bf16[32,129,128]{2,1,0:T(8,128)(2,1)}), bf16[32,129,128]{2,1,0:T(8,128)(2,1)S(1)}, u32[]{:S(2)}, u32[]{:S(2)}) %all-to-all-start.4) | async-done | bytes 1056800 | tf_op jit(solution)/shard_map/all_to_all | solution.py:88
  154.4 3.1 %fusion.11 = f32[64,512]{1,0:T(8,128)} fusion(f32[32,128]{1,0:T(8,128)S(1)} %bitcast.92, bf16[32,129,128]{2,1,0:T(8,128)(2,1)S(1)} %all-to-all-done.4, f32[64]{0:T(128)S(1)} %fusion.47, bf16[256,64]{0,1:T(8,128)(2,1)S(1)} %collective-permute-done, bf16[256,64]{0,1:T(8,128)(2,1)S(1)} %copy-done.7), kind=kOutput, calls=%fused_computation.12 | convolution fusion | flops 541229056 | bytes 1262080 | tf_op jit(solution)/shard_map/doh,sdh->os/dot_general | solution.py:96
  157.5 0.9 reshape.191
  158.4 10.5 %all_to_all.42 = f32[16,4,512]{2,1,0:T(4,128)S(1)} all-to-all(f32[16,4,512]{2,1,0:T(4,128)S(1)} %reshape.191), channel_id=1, replica_groups=mesh['member'=16,'dp'=32] {'member'}, dimensions={0} | all-to-all | bytes 262144 | tf_op jit(solution)/shard_map/all_to_all | solution.py:104
  168.9 4.5 %collective-permute-start.2 = (f32[16,4,256]{2,0,1:T(8,128)S(1)}, f32[16,4,256]{2,0,1:T(8,128)S(1)}, u32[]{:S(2)}, u32[]{:S(2)}) collective-permute-start(f32[16,4,256]{2,0,1:T(8,128)S(1)} %copy.200), channel_id=1, source_target_pairs={{0,1},{1,0},{2,3},{3,2},{4,5},{5,4},{6,7},{7,6},{8,9},{9,8},{10,11... | collective-permute-start | bytes 196616 | tf_op jit(solution)/shard_map/ppermute | solution.py:79
  173.5 0.9 collective-permute-done.2
  174.6 0.2 convolution_bitcast_fusion.1
  175.2 0.3 convolution_bitcast_fusion
  175.5 0.7 broadcast_in_dim.28
  176.2 5.7 %all-to-all-start.6 = ((f32[32,14,128]{2,1,0:T(8,128)}), f32[32,14,128]{2,1,0:T(8,128)S(1)}, u32[]{:S(2)}, u32[]{:S(2)}) async-start(f32[32,14,128]{2,1,0:T(8,128)} %broadcast_in_dim.28), calls=%async_computation.6 | async-start | bytes 524288 | tf_op jit(solution)/shard_map/all_to_all | solution.py:73
  182.0 1.0 fusion.53
  183.0 11.9 %all-to-all-done.6 = f32[32,14,128]{2,1,0:T(8,128)S(1)} async-done(((f32[32,14,128]{2,1,0:T(8,128)}), f32[32,14,128]{2,1,0:T(8,128)S(1)}, u32[]{:S(2)}, u32[]{:S(2)}) %all-to-all-start.6) | async-done | bytes 229408 | tf_op jit(solution)/shard_map/all_to_all | solution.py:73
  195.0 0.7 broadcast_in_dim.29
  195.6 3.5 %all-to-all-start.7 = ((f32[16,14,128]{2,1,0:T(8,128)}), f32[16,14,128]{2,1,0:T(8,128)S(1)}, u32[]{:S(2)}, u32[]{:S(2)}) async-start(f32[16,14,128]{2,1,0:T(8,128)} %broadcast_in_dim.29), calls=%async_computation.7 | async-start | bytes 262144 | tf_op jit(solution)/shard_map/all_to_all | solution.py:73
  199.2 7.5 %all-to-all-done.7 = f32[16,14,128]{2,1,0:T(8,128)S(1)} async-done(((f32[16,14,128]{2,1,0:T(8,128)}), f32[16,14,128]{2,1,0:T(8,128)S(1)}, u32[]{:S(2)}, u32[]{:S(2)}) %all-to-all-start.7) | async-done | bytes 114720 | tf_op jit(solution)/shard_map/all_to_all | solution.py:73
  207.1 0.6 pad_maximum_fusion.5.s_ref
  207.8 4.0 %shard_map.103 = f32[32,32]{1,0:T(8,128)} custom-call(f32[2,32,32]{2,1,0:T(8,128)} %pad_maximum_fusion.5.s_ref), custom_call_target="tpu_custom_call" | custom-call | tf_op jit(solution)/shard_map/pallas_call | solution.py:44
  211.8 0.9 fusion.40
  212.7 0.4 convolution_add_fusion.1
  213.1 0.4 convolution_add_fusion.2
  213.4 0.7 convolution_add_fusion.4
  214.1 0.6 copy.185
  214.8 0.6 copy.186
  215.4 0.7 convolution_add_fusion.3
  (86 shorter events, 2.8 us)
Async XLA Ops:
  7.2 18.3 %copy-start.5 = (f32[2,128]{1,0:T(2,128)S(1)}, f32[2,128]{1,0:T(2,128)}, u32[]{:S(2)}) copy-start(f32[2,128]{1,0:T(2,128)} %param.11) | copy-start | bytes 3076
  7.2 18.1 %copy-start = (f32[2,64,128]{2,1,0:T(8,128)S(1)}, f32[2,64,128]{2,1,0:T(8,128)}, u32[]{:S(2)}) copy-start(f32[2,64,128]{2,1,0:T(8,128)} %param.10) | copy-start | bytes 196612
  7.2 18.2 %copy-start.1 = (f32[2,64,128]{2,1,0:T(8,128)S(1)}, f32[2,64,128]{2,1,0:T(8,128)}, u32[]{:S(2)}) copy-start(f32[2,64,128]{2,1,0:T(8,128)} %param.12) | copy-start | bytes 196612
  7.2 18.2 %copy-start.6 = (f32[2,64]{1,0:T(2,128)S(1)}, f32[2,64]{1,0:T(2,128)}, u32[]{:S(2)}) copy-start(f32[2,64]{1,0:T(2,128)} %param.13) | copy-start | bytes 1540
  9.6 16.6 %copy-start.7 = (bf16[256,64]{0,1:T(8,128)(2,1)S(1)}, bf16[256,64]{0,1:T(8,128)(2,1)}, u32[]{:S(2)}) copy-start(bf16[256,64]{0,1:T(8,128)(2,1)} %param.7) | copy-start | bytes 98308
  10.8 44.0 %all-to-all-start = ((bf16[32,129,128]{2,1,0:T(8,128)(2,1)}), bf16[32,129,128]{2,1,0:T(8,128)(2,1)S(1)}, u32[]{:S(2)}, u32[]{:S(2)}) async-start(bf16[32,129,128]{2,1,0:T(8,128)(2,1)} %bitcast.2), calls=%async_computation | async-start | bytes 2228224 | tf_op jit(solution)/shard_map/all_to_all | solution.py:88
  25.2 85.0 %all-gather.2.cloned.1.call-start = ((), (), s32[]{:S(2)}) async-start(), calls=%async_computation.8 | async-start | bytes 2367488 | tf_op jit(solution)/shard_map/all_gather | solution.py:122
  26.2 28.6 %collective-permute-start = (bf16[256,64]{0,1:T(8,128)(2,1)S(1)}, bf16[256,64]{0,1:T(8,128)(2,1)S(1)}, u32[]{:S(2)}, u32[]{:S(2)}) collective-permute-start(bf16[256,64]{0,1:T(8,128)(2,1)S(1)} %copy-done.7), channel_id=1, source_target_pairs={{0,1},{1,0},{2,3},{3,2},{4,5},{5,4},{6,7},{7,6},{8,9},{9,8},{10,11... | collective-permute-start | bytes 98312 | tf_op jit(solution)/shard_map/ppermute | solution.py:79
  54.8 21.9 %copy-start.3 = (bf16[2,32,4,256]{3,2,1,0:T(4,128)(2,1)S(1)}, bf16[2,32,4,256]{3,2,1,0:T(4,128)(2,1)}, u32[]{:S(2)}) copy-start(bf16[2,32,4,256]{3,2,1,0:T(4,128)(2,1)} %param.9) | copy-start | bytes 393220
  54.8 22.8 %copy-start.4 = (f32[4,256]{1,0:T(4,128)S(1)}, f32[4,256]{1,0:T(4,128)}, u32[]{:S(2)}) copy-start(f32[4,256]{1,0:T(4,128)} %param.8) | copy-start | bytes 12292
  71.6 6.0 %collective-permute-start.1 = (f32[16,4,256]{2,0,1:T(8,128)S(1)}, f32[16,4,256]{2,0,1:T(8,128)S(1)}, u32[]{:S(2)}, u32[]{:S(2)}) collective-permute-start(f32[16,4,256]{2,0,1:T(8,128)S(1)} %copy.194), channel_id=1, source_target_pairs={{0,1},{1,0},{2,3},{3,2},{4,5},{5,4},{6,7},{7,6},{8,9},{9,8},{10,11... | collective-permute-start | bytes 196616 | tf_op jit(solution)/shard_map/ppermute | solution.py:79
  97.9 11.1 %all-to-all-start.3 = ((f32[16,14,128]{2,1,0:T(8,128)}), f32[16,14,128]{2,1,0:T(8,128)S(1)}, u32[]{:S(2)}, u32[]{:S(2)}) async-start(f32[16,14,128]{2,1,0:T(8,128)} %broadcast_in_dim.25), calls=%async_computation.3 | async-start | bytes 262144 | tf_op jit(solution)/shard_map/all_to_all | solution.py:73
  119.0 35.4 %all-to-all-start.4 = ((bf16[32,129,128]{2,1,0:T(8,128)(2,1)}), bf16[32,129,128]{2,1,0:T(8,128)(2,1)S(1)}, u32[]{:S(2)}, u32[]{:S(2)}) async-start(bf16[32,129,128]{2,1,0:T(8,128)(2,1)} %bitcast.18), calls=%async_computation.4 | async-start | bytes 2228224 | tf_op jit(solution)/shard_map/all_to_all | solution.py:88
  168.9 42.8 %copy-start.2 = (f32[32,32]{1,0:T(8,128)S(1)}, f32[32,32]{1,0:T(8,128)}, u32[]{:S(2)}) copy-start(f32[32,32]{1,0:T(8,128)} %shard_map.102) | copy-start | bytes 12292
  168.9 5.4 %collective-permute-start.2 = (f32[16,4,256]{2,0,1:T(8,128)S(1)}, f32[16,4,256]{2,0,1:T(8,128)S(1)}, u32[]{:S(2)}, u32[]{:S(2)}) collective-permute-start(f32[16,4,256]{2,0,1:T(8,128)S(1)} %copy.200), channel_id=1, source_target_pairs={{0,1},{1,0},{2,3},{3,2},{4,5},{5,4},{6,7},{7,6},{8,9},{9,8},{10,11... | collective-permute-start | bytes 196616 | tf_op jit(solution)/shard_map/ppermute | solution.py:79
  176.2 18.7 %all-to-all-start.6 = ((f32[32,14,128]{2,1,0:T(8,128)}), f32[32,14,128]{2,1,0:T(8,128)S(1)}, u32[]{:S(2)}, u32[]{:S(2)}) async-start(f32[32,14,128]{2,1,0:T(8,128)} %broadcast_in_dim.28), calls=%async_computation.6 | async-start | bytes 524288 | tf_op jit(solution)/shard_map/all_to_all | solution.py:73
  195.6 11.0 %all-to-all-start.7 = ((f32[16,14,128]{2,1,0:T(8,128)}), f32[16,14,128]{2,1,0:T(8,128)S(1)}, u32[]{:S(2)}, u32[]{:S(2)}) async-start(f32[16,14,128]{2,1,0:T(8,128)} %broadcast_in_dim.29), calls=%async_computation.7 | async-start | bytes 262144 | tf_op jit(solution)/shard_map/all_to_all | solution.py:73
Sparse Core Ops, SparseCore 0:
  28.2 66.5 all-gather.1
